TPU v7x, 512 devices: a whole 4x8x8 slice. The times are simulated.
512 devices in a mesh: dp: 16 (over z, core), expert: 32 (over x, y).
Axes of the slice: x: 4, y: 8, z: 8, core: 2. Of those that a mesh axis runs over, the one named last changes fastest.
Arguments:
- residual_in: bfloat16 [16384, 2048], P(('dp', 'expert')), may hold values from -6 to 6
- attention_out: bfloat16 [16384, 2048], P(('dp', 'expert')), may hold values from -6 to 6
- out_weight: bfloat16 [2048, 2048], P(None, 'dp'), may hold values from -0.125 to 0.125
- post_gain: float32 [2048], replicated, may hold values from 0.1 to 1.9
- router_weight: bfloat16 [2048, 32], replicated, may hold values from -0.125 to 0.125
- expert_ids: int32 [16384, 6], P(('dp', 'expert')), may hold values from 0 to 31, all different within a row; in each aligned block of 32 rows (0 to 31, 32 to 63, ...) at most 12 rows name the same one
- expert_slot: int32 [32], replicated, may hold values from 0 to 31, each once
- expert_gate_up: bfloat16 [32, 2048, 1408], P('expert', 'dp'), may hold values from -0.125 to 0.125
- expert_down: bfloat16 [32, 704, 2048], P('expert', None, 'dp'), may hold values from -0.21875 to 0.21875
- shared_gate_up: bfloat16 [2048, 2, 2816], P(None, None, 'dp'), may hold values from -0.125 to 0.125
- shared_down: bfloat16 [2816, 2048], P(None, 'dp'), may hold values from -0.109375 to 0.109375
- final_gain: float32 [2048], replicated, may hold values from 0.1 to 1.9
Outputs:
- mixed: bfloat16 [16384, 2048], P(('dp', 'expert'))
Inputs may be any that keep to these rules, and one draw needn't show every extreme that they name: `expert_ids`: each row names 6 different experts. In each aligned block of 32 rows (the rows of one device) no expert is named by more than 12 rows, a bound that some block reaches. A permutation: expert e is held in slot expert_slot[e].
All inputs are finite; a program needn't handle non-finite values.
Results may differ from a plain program's by a relative error of at most 0.0069.
Values may be sent and summed in bfloat16 or wider, within the bound.
No kernel may reach another device: no remote copies, remote signals or barrier semaphores. Data moves between devices by JAX's collectives and lax.ppermute only.
A program may use at most 64 MiB of HBM per device.

v0:
```python
import jax
import jax.numpy as jnp
from jax import lax
from jax.sharding import PartitionSpec as P

EPS = 1e-06


def in_order(blocks, dim):
    shape = list(blocks.shape[1:])
    shape[dim] *= blocks.shape[0]
    return jnp.moveaxis(blocks, 0, dim).reshape(shape)


def sent_to_all(array, axis):
    copies = jnp.broadcast_to(array, (lax.axis_size(axis), *array.shape))
    return lax.all_to_all(copies, axis, split_axis=0, concat_axis=0, tiled=True)


def collect(array, axis, dim):
    return in_order(sent_to_all(array, axis), dim)


def turned_gather(arrays, axis, dims):
    turned = [jnp.moveaxis(a, dim, 0) for a, dim in zip(arrays, dims)]
    widths = [t[0].size for t in turned]
    both = jnp.concatenate([t.reshape(-1, w) for t, w in zip(turned, widths)], axis=1)
    out = lax.all_gather(both, axis, axis=0, tiled=True)
    blocks = jnp.split(out, [sum(widths[:k]) for k in range(1, len(widths))], axis=1)
    return tuple(
        (
            jnp.moveaxis(b.reshape(-1, *t.shape[1:]), 0, dim)
            for b, t, dim in zip(blocks, turned, dims)
        )
    )


def rms_scale(values, gain):
    values = values.astype(jnp.float32)
    inverse = lax.rsqrt(jnp.mean(values * values, axis=-1, keepdims=True) + EPS)
    return values * inverse * gain


def per_device(
    residual_in,
    attention_out,
    out_weight,
    post_gain,
    router_weight,
    expert_ids,
    expert_slot,
    expert_gate_up,
    expert_down,
    shared_gate_up,
    shared_down,
    final_gain,
):
    rows = residual_in.shape[0]
    width = residual_in.shape[1]
    experts = router_weight.shape[1]
    choose = expert_ids.shape[1]
    capacity = max(2, min(rows, 2 * rows * choose // experts))
    proj_cols = jnp.dot(
        collect(attention_out, "dp", 0), out_weight, preferred_element_type=jnp.float32
    ).astype(jnp.bfloat16)
    proj = lax.all_to_all(proj_cols, "dp", split_axis=0, concat_axis=1, tiled=True)
    resid = (residual_in.astype(jnp.float32) + proj.astype(jnp.float32)).astype(jnp.bfloat16)
    normed = rms_scale(resid, post_gain).astype(jnp.bfloat16)
    logits = jnp.dot(normed, router_weight, preferred_element_type=jnp.float32)
    expert_range = jnp.arange(experts, dtype=jnp.int32)
    picked = expert_ids[:, :, None] == expert_range[None, None, :]
    chosen = jnp.sum(jnp.where(picked, logits[:, None, :], 0.0), axis=2)
    raised = jnp.exp(chosen)
    gates = raised / jnp.sum(raised, axis=1, keepdims=True)
    slots = jnp.sum(jnp.where(picked, expert_slot[None, None, :], 0), axis=2).reshape(-1)
    marked = (slots[:, None] == expert_range[None, :]).astype(jnp.int32)
    before = jnp.cumsum(marked, axis=0) - marked
    position = jnp.sum(before * marked, axis=1)
    target = slots * capacity + position
    placed = target[:, None] == jnp.arange(experts * capacity, dtype=jnp.int32)[None, :]
    select = jnp.any(placed.reshape(rows, choose, experts * capacity), axis=1).astype(jnp.bfloat16)
    outgoing = jnp.einsum("rs,rd->sd", select, normed, preferred_element_type=jnp.float32)
    outgoing = outgoing.astype(jnp.bfloat16).reshape(experts, capacity, width)
    gate_up_all, down_all = turned_gather((expert_gate_up, expert_down), "dp", (1, 2))
    gate_up_full = gate_up_all[0]
    down_full = down_all[0]
    hidden_units = gate_up_full.shape[1] // 2
    received = lax.all_to_all(outgoing, "expert", split_axis=0, concat_axis=0, tiled=True)
    sources, count, _ = received.shape
    flat = received.reshape(sources * count, width)
    both = jnp.dot(flat, gate_up_full, preferred_element_type=jnp.float32)
    active = (jax.nn.silu(both[:, :hidden_units]) * both[:, hidden_units:]).astype(jnp.bfloat16)
    result = jnp.dot(active, down_full, preferred_element_type=jnp.float32).astype(jnp.bfloat16)
    result = result.reshape(sources, count, width)
    returned = lax.all_to_all(result, "expert", split_axis=0, concat_axis=0, tiled=True)
    shared_units = shared_gate_up.shape[2]
    shared_pair = shared_gate_up.reshape(width, 2 * shared_units)
    both = jnp.dot(
        lax.all_gather(normed, "dp", axis=0, tiled=True),
        shared_pair,
        preferred_element_type=jnp.float32,
    )
    shared_hidden = (jax.nn.silu(both[:, :shared_units]) * both[:, shared_units:]).astype(
        jnp.bfloat16
    )
    out_cols = jnp.dot(
        lax.all_gather(shared_hidden, "dp", axis=1, tiled=True),
        shared_down,
        preferred_element_type=jnp.float32,
    )
    shared_out = lax.all_to_all(out_cols, "dp", split_axis=0, concat_axis=1, tiled=True)
    back_rows = jnp.take(returned.reshape(experts * capacity, width), target, axis=0)
    back_rows = back_rows.reshape(rows, choose, width).astype(jnp.float32)
    routed = jnp.sum(gates[:, :, None] * back_rows, axis=1)
    total = resid.astype(jnp.float32) + routed + shared_out
    return rms_scale(total, final_gain).astype(jnp.bfloat16)


def solution(mesh):
    in_specs = (
        P(("dp", "expert"), None),
        P(("dp", "expert"), None),
        P(None, "dp"),
        P(),
        P(),
        P(("dp", "expert"), None),
        P(),
        P("expert", "dp", None),
        P("expert", None, "dp"),
        P(None, None, "dp"),
        P(None, "dp"),
        P(),
    )
    out_specs = P(("dp", "expert"), None)
    return jax.shard_map(
        per_device, mesh=mesh, in_specs=in_specs, out_specs=out_specs, check_vma=False
    )
```

profile of v0, /device:TPU:1, one launch (start us, length us, event | category | flops | bytes accessed | tf_op | source)
XLA Modules:
  0.0 282.8 jit_solution(13538233987763280168)
XLA Ops:
  6.5 1.3 broadcast_in_dim.50
  7.8 62.8 %all_to_all.47 = bf16[16,32,2048]{2,1,0:T(8,128)(2,1)S(1)} all-to-all(bf16[16,32,2048]{2,1,0:T(8,128)(2,1)S(1)} %broadcast_in_dim.50), channel_id=1, replica_groups=mesh['dp'=16,'expert'=32] {'dp'}, dimensions={0} | all-to-all | bytes 4194304 | tf_op jit(solution)/shard_map/all_to_all | solution.py:17
  71.4 11.9 %all_to_all.48 = bf16[16,32,128]{2,1,0:T(8,128)(2,1)S(1)} all-to-all(bf16[16,32,128]{2,1,0:T(8,128)(2,1)S(1)} %bitcast.66), channel_id=1, replica_groups=mesh['dp'=16,'expert'=32] {'dp'}, dimensions={0} | all-to-all | bytes 262144 | tf_op jit(solution)/shard_map/all_to_all | solution.py:66
  85.0 0.9 pad_maximum_fusion
  88.9 1.6 reshape.147
  90.6 9.7 %all-to-all-start.2 = ((bf16[32,12,2048]{2,1,0:T(8,128)(2,1)}), bf16[32,12,2048]{2,1,0:T(8,128)(2,1)S(1)}, u32[]{:S(2)}, u32[]{:S(2)}) async-start(bf16[32,12,2048]{2,1,0:T(8,128)(2,1)} %reshape.147), calls=%async_computation.2 | async-start | bytes 4194304 | tf_op jit(solution)/shard_map/all_to_all | solution.py:88
  100.3 24.4 %all-gather.6.cloned.1.call-done = bf16[512,2048]{1,0:T(8,128)(2,1)} async-done(((bf16[32,2048]{1,0:T(8,128)(2,1)}), bf16[512,2048]{1,0:T(8,128)(2,1)}) %all-gather.6.cloned.1.call-update) | async-done | bytes 2097168 | tf_op jit(solution)/shard_map/all_gather | solution.py:99
  124.7 2.5 fusion.21
  127.3 0.8 fusion.7
  128.1 22.2 %all-to-all-done.2 = bf16[32,12,2048]{2,1,0:T(8,128)(2,1)S(1)} async-done(((bf16[32,12,2048]{2,1,0:T(8,128)(2,1)}), bf16[32,12,2048]{2,1,0:T(8,128)(2,1)S(1)}, u32[]{:S(2)}, u32[]{:S(2)}) %all-to-all-start.2) | async-done | bytes 1572896 | tf_op jit(solution)/shard_map/all_to_all | solution.py:88
  150.2 1.4 reshape.148
  151.7 35.1 %all-gather.4.cloned.1.call-done = bf16[2048,2112]{1,0:T(8,128)(2,1)} async-done(((bf16[128,2112]{1,0:T(8,128)(2,1)}), bf16[2048,2112]{1,0:T(8,128)(2,1)}) %all-gather.4.cloned.1.call-update) | async-done | bytes 8650768 | tf_op jit(solution)/shard_map/all_gather | solution.py:28
  186.8 5.7 %fusion = f32[384,1408]{1,0:T(8,128)S(1)} fusion(bf16[384,2048]{1,0:T(8,128)(2,1)} %reshape.148, bf16[2048,2112]{1,0:T(8,128)(2,1)} %all-gather.4.cloned.1.call-done), kind=kOutput, calls=%fused_computation.1 | convolution fusion | flops 2214592512 | bytes 9502720 | tf_op jit(solution)/shard_map/dot_general | solution.py:91
  192.5 3.3 %fusion.3 = bf16[384,2048]{1,0:T(8,128)(2,1)S(1)} fusion(bf16[2048,2112]{1,0:T(8,128)(2,1)} %all-gather.4.cloned.1.call-done, f32[384,1408]{1,0:T(8,128)S(1)} %fusion), kind=kOutput, calls=%fused_computation.5 | convolution fusion | flops 1109704704 | bytes 7077888 | tf_op jit(solution)/shard_map/dot_general | solution.py:93
  195.8 1.5 reshape.151
  197.4 9.3 %all-to-all-start.3 = ((bf16[32,12,2048]{2,1,0:T(8,128)(2,1)}), bf16[32,12,2048]{2,1,0:T(8,128)(2,1)S(1)}, u32[]{:S(2)}, u32[]{:S(2)}) async-start(bf16[32,12,2048]{2,1,0:T(8,128)(2,1)} %reshape.151), calls=%async_computation.3 | async-start | bytes 4194304 | tf_op jit(solution)/shard_map/all_to_all | solution.py:95
  207.2 0.8 copy.31
  208.6 1.3 copy.29
  211.3 1.1 fusion.20
  212.4 0.9 select_reduce_fusion.1
  213.3 17.8 %all-gather.8.cloned.1.call-done = bf16[512,2816]{0,1:T(8,128)(2,1)} async-done(((bf16[512,176]{0,1:T(8,128)(2,1)}), bf16[512,2816]{0,1:T(8,128)(2,1)}) %all-gather.8.cloned.1.call-update) | async-done | bytes 2883600 | tf_op jit(solution)/shard_map/all_gather | solution.py:107
  231.1 3.6 %fusion.22 = f32[512,128]{1,0:T(8,128)} fusion(bf16[512,2816]{0,1:T(8,128)(2,1)} %all-gather.8.cloned.1.call-done, bf16[2816,128]{1,0:T(8,128)(2,1)} %param.22), kind=kOutput, calls=%fused_computation.55 | convolution fusion | flops 369098752 | bytes 3866624 | tf_op jit(solution)/shard_map/dot_general | solution.py:106
  234.8 20.8 %all-to-all-done.3 = bf16[32,12,2048]{2,1,0:T(8,128)(2,1)S(1)} async-done(((bf16[32,12,2048]{2,1,0:T(8,128)(2,1)}), bf16[32,12,2048]{2,1,0:T(8,128)(2,1)S(1)}, u32[]{:S(2)}, u32[]{:S(2)}) %all-to-all-start.3) | async-done | bytes 1572896 | tf_op jit(solution)/shard_map/all_to_all | solution.py:95
  255.5 6.1 %all-to-all-start.4 = ((f32[16,32,128]{2,1,0:T(8,128)}), f32[16,32,128]{2,1,0:T(8,128)}, u32[]{:S(2)}, u32[]{:S(2)}) async-start(f32[16,32,128]{2,1,0:T(8,128)} %bitcast.65), calls=%async_computation.4 | async-start | bytes 524288 | tf_op jit(solution)/shard_map/all_to_all | solution.py:111
  262.3 0.8 copy.24
  263.0 2.5 reshape.152
  265.6 2.2 gather_fusion
  267.7 1.4 gather.7
  269.1 1.7 multiply_reduce_fusion
  270.8 2.7 all-to-all-done.4
  273.5 1.1 multiply_reduce_fusion.1
  274.6 1.7 multiply_convert_fusion
  (64 shorter events, 8.7 us)
Async XLA Ops:
  6.5 118.2 %copy-start = (bf16[2048,2,176]{0,2,1:T(8,128)(2,1)S(1)}, bf16[2048,2,176]{0,2,1:T(8,128)(2,1)}, u32[]{:S(2)}) copy-start(bf16[2048,2,176]{0,2,1:T(8,128)(2,1)} %param.21) | copy-start | bytes 4325380
  6.5 118.2 %all-gather.6.cloned.1.call-start = ((), (), s32[]{:S(2)}) async-start(), calls=%async_computation.6 | async-start | bytes 2228224 | tf_op jit(solution)/shard_map/all_gather | solution.py:99
  7.8 62.8 %copy-start.5 = (bf16[2048,128]{1,0:T(8,128)(2,1)S(1)}, bf16[2048,128]{1,0:T(8,128)(2,1)}, u32[]{:S(2)}) copy-start(bf16[2048,128]{1,0:T(8,128)(2,1)} %param.14) | copy-start | bytes 1572868
  70.6 12.6 %copy-start.8 = (bf16[32,2048]{1,0:T(8,128)(2,1)S(1)}, bf16[32,2048]{1,0:T(8,128)(2,1)}, u32[]{:S(2)}) copy-start(bf16[32,2048]{1,0:T(8,128)(2,1)} %param.12) | copy-start | bytes 393220
  70.6 13.4 %copy-start.13 = (f32[2048]{0:T(1024)S(1)}, f32[2048]{0:T(1024)}, u32[]{:S(2)}) copy-start(f32[2048]{0:T(1024)} %param.15) | copy-start | bytes 24580
  70.6 14.3 %copy-start.7 = (bf16[1,704,128]{2,1,0:T(8,128)(2,1)S(1)}, bf16[1,704,128]{2,1,0:T(8,128)(2,1)}, u32[]{:S(2)}) copy-start(bf16[1,704,128]{2,1,0:T(8,128)(2,1)} %param.20) | copy-start | bytes 540676
  70.6 14.4 %copy-start.6 = (bf16[1,128,1408]{2,1,0:T(8,128)(2,1)S(1)}, bf16[1,128,1408]{2,1,0:T(8,128)(2,1)}, u32[]{:S(2)}) copy-start(bf16[1,128,1408]{2,1,0:T(8,128)(2,1)} %param.19) | copy-start | bytes 1081348
  71.3 14.6 %copy-start.10 = (s32[32,6]{0,1:T(8,128)S(1)}, s32[32,6]{0,1:T(8,128)}, u32[]{:S(2)}) copy-start(s32[32,6]{0,1:T(8,128)} %param.17) | copy-start | bytes 2308
  71.3 14.6 %copy-start.14 = (s32[32]{0:T(128)S(1)}, s32[32]{0:T(128)}, u32[]{:S(2)}) copy-start(s32[32]{0:T(128)} %param.18) | copy-start | bytes 388
  83.4 0.6 copy-start.2
  84.8 3.5 %copy-start.4 = (bf16[32,2048]{1,0:T(8,128)(2,1)S(1)}, bf16[32,2048]{1,0:T(8,128)(2,1)}, u32[]{:S(2)}) copy-start(bf16[32,2048]{1,0:T(8,128)(2,1)} %fusion.11) | copy-start | bytes 393220
  84.8 101.9 %all-gather.4.cloned.1.call-start = ((), (), s32[]{:S(2)}) async-start(), calls=%async_computation.5 | async-start | bytes 9469952 | tf_op jit(solution)/shard_map/all_gather | solution.py:28
  87.4 0.8 copy-start.11
  90.6 59.7 %all-to-all-start.2 = ((bf16[32,12,2048]{2,1,0:T(8,128)(2,1)}), bf16[32,12,2048]{2,1,0:T(8,128)(2,1)S(1)}, u32[]{:S(2)}, u32[]{:S(2)}) async-start(bf16[32,12,2048]{2,1,0:T(8,128)(2,1)} %reshape.147), calls=%async_computation.2 | async-start | bytes 4194304 | tf_op jit(solution)/shard_map/all_to_all | solution.py:88
  100.2 130.9 %all-gather.8.cloned.1.call-start = ((), (), s32[]{:S(2)}) async-start(), calls=%async_computation.7 | async-start | bytes 3063808 | tf_op jit(solution)/shard_map/all_gather | solution.py:107
  197.4 58.2 %all-to-all-start.3 = ((bf16[32,12,2048]{2,1,0:T(8,128)(2,1)}), bf16[32,12,2048]{2,1,0:T(8,128)(2,1)S(1)}, u32[]{:S(2)}, u32[]{:S(2)}) async-start(bf16[32,12,2048]{2,1,0:T(8,128)(2,1)} %reshape.151), calls=%async_computation.3 | async-start | bytes 4194304 | tf_op jit(solution)/shard_map/all_to_all | solution.py:95
  255.5 6.7 %copy-start.1 = (bf16[32,12,2048]{2,1,0:T(8,128)(2,1)}, bf16[32,12,2048]{2,1,0:T(8,128)(2,1)S(1)}, u32[]{:S(2)}) copy-start(bf16[32,12,2048]{2,1,0:T(8,128)(2,1)S(1)} %all-to-all-done.3) | copy-start | bytes 4718596
  255.5 18.0 %all-to-all-start.4 = ((f32[16,32,128]{2,1,0:T(8,128)}), f32[16,32,128]{2,1,0:T(8,128)}, u32[]{:S(2)}, u32[]{:S(2)}) async-start(f32[16,32,128]{2,1,0:T(8,128)} %bitcast.65), calls=%async_computation.4 | async-start | bytes 524288 | tf_op jit(solution)/shard_map/all_to_all | solution.py:111
  265.5 3.6 %copy-start.9 = (pred[32,6]{1,0:T(8,128)(4,1)S(1)}, pred[32,6]{1,0:T(8,128)(4,1)}, u32[]{:S(2)}) copy-start(pred[32,6]{1,0:T(8,128)(4,1)} %copy.29) | copy-start | bytes 580
  267.7 5.8 %copy-start.3 = (bf16[32,2048]{1,0:T(8,128)(2,1)S(1)}, bf16[32,2048]{1,0:T(8,128)(2,1)}, u32[]{:S(2)}) copy-start(bf16[32,2048]{1,0:T(8,128)(2,1)} %copy-done.2) | copy-start | bytes 393220
  267.7 6.9 %copy-start.12 = (f32[2048]{0:T(1024)S(1)}, f32[2048]{0:T(1024)}, u32[]{:S(2)}) copy-start(f32[2048]{0:T(1024)} %param.23) | copy-start | bytes 24580
Sparse Core Ops, SparseCore 0:
  84.9 39.7 all-gather.5
  126.8 59.8 all-gather.3
  188.9 42.1 all-gather.7
where the time goes:
time: 284 us; the launch traced here: 283 us
  waiting for transfers between devices  123 us (43%)
  blocking collectives  74.6 us (26%)
  starting transfers between devices  25.1 us (9%)
  matrix products  17.7 us (6%)
  local copies, waits for them, and re-layouts  16.8 us (6%)
  between operations  13.4 us (5%)
  other arithmetic  12.2 us (4%)
    all_to_all x1, blocking collectives, sent_to_all(): return lax.all_to_all(copies, axis, split_axis=0, concat_axis=0, tiled=True)  62.8 us
    all_gather x1, waiting for transfers between devices, turned_gather(): out = lax.all_gather(both, axis, axis=0, tiled=True)  35.1 us
    all_gather x1, waiting for transfers between devices, per_device(): lax.all_gather(normed, 'dp', axis=0, tiled=True)  24.4 us
    all_to_all x1, waiting for transfers between devices, per_device(): lax.all_to_all(outgoing, 'expert', split_axis=0, concat_axis=0, tiled=True)  22.2 us
    all_to_all x1, waiting for transfers between devices, per_device(): lax.all_to_all(result, 'expert', split_axis=0, concat_axis=0, tiled=True)  20.8 us
    all_gather x1, waiting for transfers between devices, per_device(): lax.all_gather(shared_hidden, 'dp', axis=1, tiled=True)  17.8 us
    all_to_all x1, blocking collectives, per_device(): lax.all_to_all(proj_cols, 'dp', split_axis=0, concat_axis=1, tiled=True)  11.9 us
    all_to_all x1, starting transfers between devices, per_device(): lax.all_to_all(outgoing, 'expert', split_axis=0, concat_axis=0, tiled=True)  9.67 us
  transfers between devices with their start and end apart: 6, of which 6 were waited for; matrix products, arithmetic and copies ran while one was open for 14% of the time, Pallas kernels for 0%

commit v1 on v0

--- a/solution.py
+++ b/solution.py
@@ -6,33 +6,20 @@
 EPS = 1e-06
 
 
+def gathered(array, axis):
+    n = lax.axis_size(axis)
+    me = lax.axis_index(axis)
+    outs = [array] + [
+        lax.ppermute(array, axis, [(s, (s + k) % n) for s in range(n)]) for k in range(1, n)
+    ]
+    stack = jnp.stack(outs)
+    return jnp.take(stack, (me - jnp.arange(n)) % n, axis=0)
+
+
 def in_order(blocks, dim):
     shape = list(blocks.shape[1:])
     shape[dim] *= blocks.shape[0]
     return jnp.moveaxis(blocks, 0, dim).reshape(shape)
-
-
-def sent_to_all(array, axis):
-    copies = jnp.broadcast_to(array, (lax.axis_size(axis), *array.shape))
-    return lax.all_to_all(copies, axis, split_axis=0, concat_axis=0, tiled=True)
-
-
-def collect(array, axis, dim):
-    return in_order(sent_to_all(array, axis), dim)
-
-
-def turned_gather(arrays, axis, dims):
-    turned = [jnp.moveaxis(a, dim, 0) for a, dim in zip(arrays, dims)]
-    widths = [t[0].size for t in turned]
-    both = jnp.concatenate([t.reshape(-1, w) for t, w in zip(turned, widths)], axis=1)
-    out = lax.all_gather(both, axis, axis=0, tiled=True)
-    blocks = jnp.split(out, [sum(widths[:k]) for k in range(1, len(widths))], axis=1)
-    return tuple(
-        (
-            jnp.moveaxis(b.reshape(-1, *t.shape[1:]), 0, dim)
-            for b, t, dim in zip(blocks, turned, dims)
-        )
-    )
 
 
 def rms_scale(values, gain):
@@ -59,13 +46,33 @@
     width = residual_in.shape[1]
     experts = router_weight.shape[1]
     choose = expert_ids.shape[1]
+    groups = lax.axis_size("dp")
+    me = lax.axis_index("dp")
     capacity = max(2, min(rows, 2 * rows * choose // experts))
-    proj_cols = jnp.dot(
-        collect(attention_out, "dp", 0), out_weight, preferred_element_type=jnp.float32
-    ).astype(jnp.bfloat16)
-    proj = lax.all_to_all(proj_cols, "dp", split_axis=0, concat_axis=1, tiled=True)
-    resid = (residual_in.astype(jnp.float32) + proj.astype(jnp.float32)).astype(jnp.bfloat16)
-    normed = rms_scale(resid, post_gain).astype(jnp.bfloat16)
+
+    both_in = jnp.concatenate([attention_out, residual_in], axis=1)
+    group_in = gathered(both_in, "dp").reshape(groups * rows, 2 * width)
+    group_attn = group_in[:, :width]
+    group_resid_in = group_in[:, width:]
+    proj_cols = jnp.dot(group_attn, out_weight, preferred_element_type=jnp.float32).astype(
+        jnp.bfloat16
+    )
+    group_proj = in_order(gathered(proj_cols, "dp"), 1)
+    group_resid = (group_resid_in.astype(jnp.float32) + group_proj.astype(jnp.float32)).astype(
+        jnp.bfloat16
+    )
+    group_normed = rms_scale(group_resid, post_gain).astype(jnp.bfloat16)
+    gate_up_part = expert_gate_up[0]
+    down_turned = expert_down[0].T
+    hidden_units = down_turned.shape[1]
+    weights_part = jnp.concatenate([gate_up_part, down_turned], axis=1)
+    weights_part, group_proj = lax.optimization_barrier((weights_part, group_proj))
+    weights_full = in_order(gathered(weights_part, "dp"), 0)
+    gate_up_full = weights_full[:, : 2 * hidden_units]
+    down_turned_full = weights_full[:, 2 * hidden_units :]
+    resid = lax.dynamic_slice_in_dim(group_resid, me * rows, rows, axis=0)
+    normed = lax.dynamic_slice_in_dim(group_normed, me * rows, rows, axis=0)
+
     logits = jnp.dot(normed, router_weight, preferred_element_type=jnp.float32)
     expert_range = jnp.arange(experts, dtype=jnp.int32)
     picked = expert_ids[:, :, None] == expert_range[None, None, :]
@@ -81,30 +88,25 @@
     select = jnp.any(placed.reshape(rows, choose, experts * capacity), axis=1).astype(jnp.bfloat16)
     outgoing = jnp.einsum("rs,rd->sd", select, normed, preferred_element_type=jnp.float32)
     outgoing = outgoing.astype(jnp.bfloat16).reshape(experts, capacity, width)
-    gate_up_all, down_all = turned_gather((expert_gate_up, expert_down), "dp", (1, 2))
-    gate_up_full = gate_up_all[0]
-    down_full = down_all[0]
-    hidden_units = gate_up_full.shape[1] // 2
     received = lax.all_to_all(outgoing, "expert", split_axis=0, concat_axis=0, tiled=True)
     sources, count, _ = received.shape
     flat = received.reshape(sources * count, width)
     both = jnp.dot(flat, gate_up_full, preferred_element_type=jnp.float32)
     active = (jax.nn.silu(both[:, :hidden_units]) * both[:, hidden_units:]).astype(jnp.bfloat16)
-    result = jnp.dot(active, down_full, preferred_element_type=jnp.float32).astype(jnp.bfloat16)
+    result = lax.dot_general(
+        active, down_turned_full, (((1,), (1,)), ((), ())), preferred_element_type=jnp.float32
+    ).astype(jnp.bfloat16)
     result = result.reshape(sources, count, width)
     returned = lax.all_to_all(result, "expert", split_axis=0, concat_axis=0, tiled=True)
+
     shared_units = shared_gate_up.shape[2]
     shared_pair = shared_gate_up.reshape(width, 2 * shared_units)
-    both = jnp.dot(
-        lax.all_gather(normed, "dp", axis=0, tiled=True),
-        shared_pair,
-        preferred_element_type=jnp.float32,
-    )
+    both = jnp.dot(group_normed, shared_pair, preferred_element_type=jnp.float32)
     shared_hidden = (jax.nn.silu(both[:, :shared_units]) * both[:, shared_units:]).astype(
         jnp.bfloat16
     )
     out_cols = jnp.dot(
-        lax.all_gather(shared_hidden, "dp", axis=1, tiled=True),
+        in_order(gathered(shared_hidden, "dp"), 1),
         shared_down,
         preferred_element_type=jnp.float32,
     )

time: 284 us -> 851 us (3.00)
  waiting for transfers between devices: 123 us -> 400 us
  starting transfers between devices: 25.1 us -> 277 us
  local copies, waits for them, and re-layouts: 16.8 us -> 123 us
  blocking collectives: 74.6 us -> 0 us
  other arithmetic: 12.2 us -> 29.8 us
  between operations: 13.4 us -> 0.85 us
    ppermute x0 -> x60, waiting for transfers between devices: none -> 397 us  [gathered(): lax.ppermute(array, axis, [(s, (s + k) % n) for s in range(n)])]
    ppermute x0 -> x60, starting transfers between devices: none -> 232 us  [gathered(): lax.ppermute(array, axis, [(s, (s + k) % n) for s in range(n)])]
    all_gather x3 -> x0, waiting for transfers between devices: 77.4 us -> none  [the longest x1 35.1 us: turned_gather(): out = lax.all_gather(both, axis, axis=0, tiled=True)]
    all_to_all x2 -> x0, blocking collectives: 74.6 us -> none  [the longest x1 62.8 us: sent_to_all(): return lax.all_to_all(copies, axis, split_axis=0, concat_axis=0, tiled=True)]
    unnamed x30 -> x94, local copies, waits for them, and re-layouts: 0.69 us -> 51.4 us
    gather x0 -> x5, local copies, waits for them, and re-layouts: none -> 31.9 us  [gathered(): return jnp.take(stack, (me - jnp.arange(n)) % n, axis=0)]
    all_to_all x1, waiting for transfers between devices: 22.2 us -> 0.01 us  [per_device(): lax.all_to_all(outgoing, 'expert', split_axis=0, concat_axis=0, tiled=True)]
    all_to_all x1, waiting for transfers between devices: 20.8 us -> 0.01 us  [per_device(): lax.all_to_all(result, 'expert', split_axis=0, concat_axis=0, tiled=True)]
  transfers between devices with their start and end apart: 6 -> 63, of which waited for: 6 -> 32; matrix products, arithmetic and copies ran while one was open for 14% -> 16% of each run, Pallas kernels for 0% -> 0%
where the time goes in v1:
time: 851 us; the launch traced here: 847 us
  waiting for transfers between devices  400 us (47%)
  starting transfers between devices  277 us (33%)
  local copies, waits for them, and re-layouts  123 us (14%)
  other arithmetic  29.8 us (4%)
  matrix products  16.5 us (2%)
    ppermute x60, waiting for transfers between devices, gathered(): lax.ppermute(array, axis, [(s, (s + k) % n) for s in range(n)])  397 us
    ppermute x60, starting transfers between devices, gathered(): lax.ppermute(array, axis, [(s, (s + k) % n) for s in range(n)])  232 us
    unnamed x94, local copies, waits for them, and re-layouts  51.4 us
    gather x5, local copies, waits for them, and re-layouts, gathered(): return jnp.take(stack, (me - jnp.arange(n)) % n, axis=0)  31.9 us
    all_to_all x1, starting transfers between devices, per_device(): lax.all_to_all(result, 'expert', split_axis=0, concat_axis=0, tiled=True)  29.3 us
  transfers between devices with their start and end apart: 63, of which 32 were waited for; matrix products, arithmetic and copies ran while one was open for 16% of the time, Pallas kernels for 0%

profile of v1, /device:TPU:1, one launch (start us, length us, event | category | flops | bytes accessed | tf_op | source)
XLA Modules:
  0.0 847.4 jit_solution(10184935598753883537)
XLA Ops:
  13.5 6.1 collective-permute-start.3
  33.6 6.6 collective-permute-start.6
  44.5 6.9 collective-permute-start.8
  59.3 17.0 %collective-permute-done.5 = bf16[32,4096]{1,0:T(8,128)(2,1)S(1)} collective-permute-done((bf16[32,4096]{1,0:T(8,128)(2,1)S(1)}, bf16[32,4096]{1,0:T(8,128)(2,1)S(1)}, u32[]{:S(2)}, u32[]{:S(2)}) %collective-permute-start.5) | collective-permute-done | bytes 262176 | tf_op jit(solution)/shard_map/ppermute | solution.py:13
  80.9 11.9 %collective-permute-done.6 = bf16[32,4096]{1,0:T(8,128)(2,1)S(1)} collective-permute-done((bf16[32,4096]{1,0:T(8,128)(2,1)S(1)}, bf16[32,4096]{1,0:T(8,128)(2,1)S(1)}, u32[]{:S(2)}, u32[]{:S(2)}) %collective-permute-start.6) | collective-permute-done | bytes 262176 | tf_op jit(solution)/shard_map/ppermute | solution.py:13
  92.8 14.6 %collective-permute-start.11 = (bf16[32,4096]{1,0:T(8,128)(2,1)S(1)}, bf16[32,4096]{1,0:T(8,128)(2,1)S(1)}, u32[]{:S(2)}, u32[]{:S(2)}) collective-permute-start(bf16[32,4096]{1,0:T(8,128)(2,1)S(1)} %constant_dynamic-update-slice_fusion), channel_id=1, source_target_pairs={{0,384},{32,416},{64,448},{96,480},{128,0},{160,32},{192,64},{224,... | collective-permute-start | bytes 786440 | tf_op jit(solution)/shard_map/ppermute | solution.py:13
  116.1 7.7 collective-permute-done.12
  252.0 9.8 %all-to-all-start = ((bf16[32,12,2048]{2,1,0:T(8,128)(2,1)}), bf16[32,12,2048]{2,1,0:T(8,128)(2,1)S(1)}, u32[]{:S(2)}, u32[]{:S(2)}) async-start(bf16[32,12,2048]{2,1,0:T(8,128)(2,1)} %reshape.199), calls=%async_computation | async-start | bytes 4194304 | tf_op jit(solution)/shard_map/all_to_all | solution.py:91
  283.5 12.8 %collective-permute-done.30 = bf16[128,2112]{0,1:T(8,128)(2,1)S(1)} collective-permute-done((bf16[128,2112]{0,1:T(8,128)(2,1)S(1)}, bf16[128,2112]{0,1:T(8,128)(2,1)S(1)}, u32[]{:S(2)}, u32[]{:S(2)}) %collective-permute-start.30) | collective-permute-done | bytes 540704 | tf_op jit(solution)/shard_map/ppermute | solution.py:13
  299.0 18.8 %collective-permute-done.31 = bf16[128,2112]{0,1:T(8,128)(2,1)S(1)} collective-permute-done((bf16[128,2112]{0,1:T(8,128)(2,1)S(1)}, bf16[128,2112]{0,1:T(8,128)(2,1)S(1)}, u32[]{:S(2)}, u32[]{:S(2)}) %collective-permute-start.31) | collective-permute-done | bytes 540704 | tf_op jit(solution)/shard_map/ppermute | solution.py:13
  321.7 18.6 %collective-permute-done.32 = bf16[128,2112]{0,1:T(8,128)(2,1)S(1)} collective-permute-done((bf16[128,2112]{0,1:T(8,128)(2,1)S(1)}, bf16[128,2112]{0,1:T(8,128)(2,1)S(1)}, u32[]{:S(2)}, u32[]{:S(2)}) %collective-permute-start.32) | collective-permute-done | bytes 540704 | tf_op jit(solution)/shard_map/ppermute | solution.py:13
  343.1 25.2 %collective-permute-done.33 = bf16[128,2112]{0,1:T(8,128)(2,1)S(1)} collective-permute-done((bf16[128,2112]{0,1:T(8,128)(2,1)S(1)}, bf16[128,2112]{0,1:T(8,128)(2,1)S(1)}, u32[]{:S(2)}, u32[]{:S(2)}) %collective-permute-start.33) | collective-permute-done | bytes 540704 | tf_op jit(solution)/shard_map/ppermute | solution.py:13
  371.3 29.0 %collective-permute-done.34 = bf16[128,2112]{0,1:T(8,128)(2,1)S(1)} collective-permute-done((bf16[128,2112]{0,1:T(8,128)(2,1)S(1)}, bf16[128,2112]{0,1:T(8,128)(2,1)S(1)}, u32[]{:S(2)}, u32[]{:S(2)}) %collective-permute-start.34) | collective-permute-done | bytes 540704 | tf_op jit(solution)/shard_map/ppermute | solution.py:13
  403.4 34.8 %collective-permute-done.35 = bf16[128,2112]{0,1:T(8,128)(2,1)S(1)} collective-permute-done((bf16[128,2112]{0,1:T(8,128)(2,1)S(1)}, bf16[128,2112]{0,1:T(8,128)(2,1)S(1)}, u32[]{:S(2)}, u32[]{:S(2)}) %collective-permute-start.35) | collective-permute-done | bytes 540704 | tf_op jit(solution)/shard_map/ppermute | solution.py:13
  438.3 8.6 %collective-permute-start.36 = (bf16[128,2112]{0,1:T(8,128)(2,1)S(1)}, bf16[128,2112]{0,1:T(8,128)(2,1)S(1)}, u32[]{:S(2)}, u32[]{:S(2)}) collective-permute-start(bf16[128,2112]{0,1:T(8,128)(2,1)S(1)} %copy-done.6), channel_id=1, source_target_pairs={{0,224},{32,256},{64,288},{96,320},{128,352},{160,384},{192,416},{... | collective-permute-start | bytes 1622024 | tf_op jit(solution)/shard_map/ppermute | solution.py:13
  447.7 27.5 %collective-permute-done.36 = bf16[128,2112]{0,1:T(8,128)(2,1)S(1)} collective-permute-done((bf16[128,2112]{0,1:T(8,128)(2,1)S(1)}, bf16[128,2112]{0,1:T(8,128)(2,1)S(1)}, u32[]{:S(2)}, u32[]{:S(2)}) %collective-permute-start.36) | collective-permute-done | bytes 540704 | tf_op jit(solution)/shard_map/ppermute | solution.py:13
  481.6 20.5 %collective-permute-done.37 = bf16[128,2112]{0,1:T(8,128)(2,1)S(1)} collective-permute-done((bf16[128,2112]{0,1:T(8,128)(2,1)S(1)}, bf16[128,2112]{0,1:T(8,128)(2,1)S(1)}, u32[]{:S(2)}, u32[]{:S(2)}) %collective-permute-start.37) | collective-permute-done | bytes 540704 | tf_op jit(solution)/shard_map/ppermute | solution.py:13
  504.9 16.1 %collective-permute-done.38 = bf16[128,2112]{0,1:T(8,128)(2,1)S(1)} collective-permute-done((bf16[128,2112]{0,1:T(8,128)(2,1)S(1)}, bf16[128,2112]{0,1:T(8,128)(2,1)S(1)}, u32[]{:S(2)}, u32[]{:S(2)}) %collective-permute-start.38) | collective-permute-done | bytes 540704 | tf_op jit(solution)/shard_map/ppermute | solution.py:13
  524.9 41.4 %collective-permute-done.39 = bf16[128,2112]{0,1:T(8,128)(2,1)S(1)} collective-permute-done((bf16[128,2112]{0,1:T(8,128)(2,1)S(1)}, bf16[128,2112]{0,1:T(8,128)(2,1)S(1)}, u32[]{:S(2)}, u32[]{:S(2)}) %collective-permute-start.39) | collective-permute-done | bytes 540704 | tf_op jit(solution)/shard_map/ppermute | solution.py:13
  566.3 23.2 %collective-permute-start.40 = (bf16[128,2112]{0,1:T(8,128)(2,1)S(1)}, bf16[128,2112]{0,1:T(8,128)(2,1)S(1)}, u32[]{:S(2)}, u32[]{:S(2)}) collective-permute-start(bf16[128,2112]{0,1:T(8,128)(2,1)S(1)} %copy-done.6), channel_id=1, source_target_pairs={{0,352},{32,384},{64,416},{96,448},{128,480},{160,0},{192,32},{224... | collective-permute-start | bytes 1622024 | tf_op jit(solution)/shard_map/ppermute | solution.py:13
  590.4 17.1 %collective-permute-done.40 = bf16[128,2112]{0,1:T(8,128)(2,1)S(1)} collective-permute-done((bf16[128,2112]{0,1:T(8,128)(2,1)S(1)}, bf16[128,2112]{0,1:T(8,128)(2,1)S(1)}, u32[]{:S(2)}, u32[]{:S(2)}) %collective-permute-start.40) | collective-permute-done | bytes 540704 | tf_op jit(solution)/shard_map/ppermute | solution.py:13
  610.3 20.1 %collective-permute-done.41 = bf16[128,2112]{0,1:T(8,128)(2,1)S(1)} collective-permute-done((bf16[128,2112]{0,1:T(8,128)(2,1)S(1)}, bf16[128,2112]{0,1:T(8,128)(2,1)S(1)}, u32[]{:S(2)}, u32[]{:S(2)}) %collective-permute-start.41) | collective-permute-done | bytes 540704 | tf_op jit(solution)/shard_map/ppermute | solution.py:13
  633.1 19.6 %collective-permute-done.42 = bf16[128,2112]{0,1:T(8,128)(2,1)S(1)} collective-permute-done((bf16[128,2112]{0,1:T(8,128)(2,1)S(1)}, bf16[128,2112]{0,1:T(8,128)(2,1)S(1)}, u32[]{:S(2)}, u32[]{:S(2)}) %collective-permute-start.42) | collective-permute-done | bytes 540704 | tf_op jit(solution)/shard_map/ppermute | solution.py:13
  657.4 11.1 %collective-permute-done.43 = bf16[128,2112]{0,1:T(8,128)(2,1)S(1)} collective-permute-done((bf16[128,2112]{0,1:T(8,128)(2,1)S(1)}, bf16[128,2112]{0,1:T(8,128)(2,1)S(1)}, u32[]{:S(2)}, u32[]{:S(2)}) %collective-permute-start.43) | collective-permute-done | bytes 540704 | tf_op jit(solution)/shard_map/ppermute | solution.py:13
  670.2 7.1 collective-permute-done.44
  682.8 8.5 gather_fusion.2
  691.3 11.7 %copy.60 = bf16[16,128,2112]{2,1,0:T(8,128)(2,1)} copy(bf16[16,128,2112]{1,2,0:T(8,128)(2,1)} %gather_fusion.2) | data formatting | bytes 17301504 | tf_op jit(solution)/shard_map/jit(_take)/gather | solution.py:16
  703.0 8.1 bitcast_select_fusion
  723.1 29.3 %all-to-all-start.1 = ((bf16[32,12,2048]{2,1,0:T(8,128)(2,1)}), bf16[32,12,2048]{2,1,0:T(8,128)(2,1)S(1)}, u32[]{:S(2)}, u32[]{:S(2)}) async-start(bf16[32,12,2048]{2,1,0:T(8,128)(2,1)} %reshape.201), calls=%async_computation.1 | async-start | bytes 4194304 | tf_op jit(solution)/shard_map/all_to_all | solution.py:100
  757.3 7.2 collective-permute-start.55
  807.0 7.6 copy.62
  814.6 8.4 dot_general.29
  (259 shorter events, 333.3 us)
Async XLA Ops:
  1.9 29.0 %collective-permute-start = (bf16[32,4096]{1,0:T(8,128)(2,1)S(1)}, bf16[32,4096]{1,0:T(8,128)(2,1)S(1)}, u32[]{:S(2)}, u32[]{:S(2)}) collective-permute-start(bf16[32,4096]{1,0:T(8,128)(2,1)S(1)} %constant_dynamic-update-slice_fusion), channel_id=1, source_target_pairs={{0,32},{32,64},{64,96},{96,128},{128,160},{160,192},{192,224},{224... | collective-permute-start | bytes 786440 | tf_op jit(solution)/shard_map/ppermute | solution.py:13
  5.4 28.2 %collective-permute-start.1 = (bf16[32,4096]{1,0:T(8,128)(2,1)S(1)}, bf16[32,4096]{1,0:T(8,128)(2,1)S(1)}, u32[]{:S(2)}, u32[]{:S(2)}) collective-permute-start(bf16[32,4096]{1,0:T(8,128)(2,1)S(1)} %constant_dynamic-update-slice_fusion), channel_id=1, source_target_pairs={{0,64},{32,96},{64,128},{96,160},{128,192},{160,224},{192,256},{22... | collective-permute-start | bytes 786440 | tf_op jit(solution)/shard_map/ppermute | solution.py:13
  9.4 31.6 %collective-permute-start.2 = (bf16[32,4096]{1,0:T(8,128)(2,1)S(1)}, bf16[32,4096]{1,0:T(8,128)(2,1)S(1)}, u32[]{:S(2)}, u32[]{:S(2)}) collective-permute-start(bf16[32,4096]{1,0:T(8,128)(2,1)S(1)} %constant_dynamic-update-slice_fusion), channel_id=1, source_target_pairs={{0,96},{32,128},{64,160},{96,192},{128,224},{160,256},{192,288},{2... | collective-permute-start | bytes 786440 | tf_op jit(solution)/shard_map/ppermute | solution.py:13
  13.5 31.1 %collective-permute-start.3 = (bf16[32,4096]{1,0:T(8,128)(2,1)S(1)}, bf16[32,4096]{1,0:T(8,128)(2,1)S(1)}, u32[]{:S(2)}, u32[]{:S(2)}) collective-permute-start(bf16[32,4096]{1,0:T(8,128)(2,1)S(1)} %constant_dynamic-update-slice_fusion), channel_id=1, source_target_pairs={{0,128},{32,160},{64,192},{96,224},{128,256},{160,288},{192,320},{... | collective-permute-start | bytes 786440 | tf_op jit(solution)/shard_map/ppermute | solution.py:13
  19.6 36.5 %collective-permute-start.4 = (bf16[32,4096]{1,0:T(8,128)(2,1)S(1)}, bf16[32,4096]{1,0:T(8,128)(2,1)S(1)}, u32[]{:S(2)}, u32[]{:S(2)}) collective-permute-start(bf16[32,4096]{1,0:T(8,128)(2,1)S(1)} %constant_dynamic-update-slice_fusion), channel_id=1, source_target_pairs={{0,160},{32,192},{64,224},{96,256},{128,288},{160,320},{192,352},{... | collective-permute-start | bytes 786440 | tf_op jit(solution)/shard_map/ppermute | solution.py:13
  31.0 45.3 %collective-permute-start.5 = (bf16[32,4096]{1,0:T(8,128)(2,1)S(1)}, bf16[32,4096]{1,0:T(8,128)(2,1)S(1)}, u32[]{:S(2)}, u32[]{:S(2)}) collective-permute-start(bf16[32,4096]{1,0:T(8,128)(2,1)S(1)} %constant_dynamic-update-slice_fusion), channel_id=1, source_target_pairs={{0,192},{32,224},{64,256},{96,288},{128,320},{160,352},{192,384},{... | collective-permute-start | bytes 786440 | tf_op jit(solution)/shard_map/ppermute | solution.py:13
  33.6 59.2 %collective-permute-start.6 = (bf16[32,4096]{1,0:T(8,128)(2,1)S(1)}, bf16[32,4096]{1,0:T(8,128)(2,1)S(1)}, u32[]{:S(2)}, u32[]{:S(2)}) collective-permute-start(bf16[32,4096]{1,0:T(8,128)(2,1)S(1)} %constant_dynamic-update-slice_fusion), channel_id=1, source_target_pairs={{0,224},{32,256},{64,288},{96,320},{128,352},{160,384},{192,416},{... | collective-permute-start | bytes 786440 | tf_op jit(solution)/shard_map/ppermute | solution.py:13
  41.0 67.2 %collective-permute-start.7 = (bf16[32,4096]{1,0:T(8,128)(2,1)S(1)}, bf16[32,4096]{1,0:T(8,128)(2,1)S(1)}, u32[]{:S(2)}, u32[]{:S(2)}) collective-permute-start(bf16[32,4096]{1,0:T(8,128)(2,1)S(1)} %constant_dynamic-update-slice_fusion), channel_id=1, source_target_pairs={{0,256},{32,288},{64,320},{96,352},{128,384},{160,416},{192,448},{... | collective-permute-start | bytes 786440 | tf_op jit(solution)/shard_map/ppermute | solution.py:13
  44.5 66.3 %collective-permute-start.8 = (bf16[32,4096]{1,0:T(8,128)(2,1)S(1)}, bf16[32,4096]{1,0:T(8,128)(2,1)S(1)}, u32[]{:S(2)}, u32[]{:S(2)}) collective-permute-start(bf16[32,4096]{1,0:T(8,128)(2,1)S(1)} %constant_dynamic-update-slice_fusion), channel_id=1, source_target_pairs={{0,288},{32,320},{64,352},{96,384},{128,416},{160,448},{192,480},{... | collective-permute-start | bytes 786440 | tf_op jit(solution)/shard_map/ppermute | solution.py:13
  56.1 57.4 %collective-permute-start.9 = (bf16[32,4096]{1,0:T(8,128)(2,1)S(1)}, bf16[32,4096]{1,0:T(8,128)(2,1)S(1)}, u32[]{:S(2)}, u32[]{:S(2)}) collective-permute-start(bf16[32,4096]{1,0:T(8,128)(2,1)S(1)} %constant_dynamic-update-slice_fusion), channel_id=1, source_target_pairs={{0,320},{32,352},{64,384},{96,416},{128,448},{160,480},{192,0},{22... | collective-permute-start | bytes 786440 | tf_op jit(solution)/shard_map/ppermute | solution.py:13
  76.3 38.3 %collective-permute-start.10 = (bf16[32,4096]{1,0:T(8,128)(2,1)S(1)}, bf16[32,4096]{1,0:T(8,128)(2,1)S(1)}, u32[]{:S(2)}, u32[]{:S(2)}) collective-permute-start(bf16[32,4096]{1,0:T(8,128)(2,1)S(1)} %constant_dynamic-update-slice_fusion), channel_id=1, source_target_pairs={{0,352},{32,384},{64,416},{96,448},{128,480},{160,0},{192,32},{224... | collective-permute-start | bytes 786440 | tf_op jit(solution)/shard_map/ppermute | solution.py:13
  164.2 26.0 %collective-permute-start.21 = (bf16[512,128]{1,0:T(8,128)(2,1)S(1)}, bf16[512,128]{1,0:T(8,128)(2,1)S(1)}, u32[]{:S(2)}, u32[]{:S(2)}) collective-permute-start(bf16[512,128]{1,0:T(8,128)(2,1)S(1)} %get-tuple-element.14), channel_id=1, source_target_pairs={{0,224},{32,256},{64,288},{96,320},{128,352},{160,384},{192,416},{... | collective-permute-start | bytes 393224 | tf_op jit(solution)/shard_map/ppermute | solution.py:13
  235.6 28.3 %collective-permute-start.45 = (bf16[512,176]{0,1:T(8,128)(2,1)}, bf16[512,176]{0,1:T(8,128)(2,1)S(1)}, u32[]{:S(2)}, u32[]{:S(2)}) collective-permute-start(bf16[512,176]{0,1:T(8,128)(2,1)} %get-tuple-element.10), channel_id=1, source_target_pairs={{0,32},{32,64},{64,96},{96,128},{128,160},{160,192},{192,224},{224... | collective-permute-start | bytes 540680 | tf_op jit(solution)/shard_map/ppermute | solution.py:13
  236.8 32.3 %collective-permute-start.46 = (bf16[512,176]{0,1:T(8,128)(2,1)}, bf16[512,176]{0,1:T(8,128)(2,1)}, u32[]{:S(2)}, u32[]{:S(2)}) collective-permute-start(bf16[512,176]{0,1:T(8,128)(2,1)} %get-tuple-element.10), channel_id=1, source_target_pairs={{0,64},{32,96},{64,128},{96,160},{128,192},{160,224},{192,256},{22... | collective-permute-start | bytes 540680 | tf_op jit(solution)/shard_map/ppermute | solution.py:13
  239.1 32.8 %collective-permute-start.47 = (bf16[512,176]{0,1:T(8,128)(2,1)}, bf16[512,176]{0,1:T(8,128)(2,1)}, u32[]{:S(2)}, u32[]{:S(2)}) collective-permute-start(bf16[512,176]{0,1:T(8,128)(2,1)} %get-tuple-element.10), channel_id=1, source_target_pairs={{0,96},{32,128},{64,160},{96,192},{128,224},{160,256},{192,288},{2... | collective-permute-start | bytes 540680 | tf_op jit(solution)/shard_map/ppermute | solution.py:13
  242.9 34.4 %collective-permute-start.48 = (bf16[512,176]{0,1:T(8,128)(2,1)}, bf16[512,176]{0,1:T(8,128)(2,1)}, u32[]{:S(2)}, u32[]{:S(2)}) collective-permute-start(bf16[512,176]{0,1:T(8,128)(2,1)} %get-tuple-element.10), channel_id=1, source_target_pairs={{0,128},{32,160},{64,192},{96,224},{128,256},{160,288},{192,320},{... | collective-permute-start | bytes 540680 | tf_op jit(solution)/shard_map/ppermute | solution.py:13
  246.3 506.1 %collective-permute-start.49 = (bf16[512,176]{0,1:T(8,128)(2,1)}, bf16[512,176]{0,1:T(8,128)(2,1)S(1)}, u32[]{:S(2)}, u32[]{:S(2)}) collective-permute-start(bf16[512,176]{0,1:T(8,128)(2,1)} %get-tuple-element.10), channel_id=1, source_target_pairs={{0,160},{32,192},{64,224},{96,256},{128,288},{160,320},{192,352},{... | collective-permute-start | bytes 540680 | tf_op jit(solution)/shard_map/ppermute | solution.py:13
  252.0 459.1 %all-to-all-start = ((bf16[32,12,2048]{2,1,0:T(8,128)(2,1)}), bf16[32,12,2048]{2,1,0:T(8,128)(2,1)S(1)}, u32[]{:S(2)}, u32[]{:S(2)}) async-start(bf16[32,12,2048]{2,1,0:T(8,128)(2,1)} %reshape.199), calls=%async_computation | async-start | bytes 4194304 | tf_op jit(solution)/shard_map/all_to_all | solution.py:91
  263.9 493.4 %collective-permute-start.50 = (bf16[512,176]{0,1:T(8,128)(2,1)}, bf16[512,176]{0,1:T(8,128)(2,1)S(1)}, u32[]{:S(2)}, u32[]{:S(2)}) collective-permute-start(bf16[512,176]{0,1:T(8,128)(2,1)} %get-tuple-element.10), channel_id=1, source_target_pairs={{0,192},{32,224},{64,256},{96,288},{128,320},{160,352},{192,384},{... | collective-permute-start | bytes 540680 | tf_op jit(solution)/shard_map/ppermute | solution.py:13
  269.1 27.2 %collective-permute-start.30 = (bf16[128,2112]{0,1:T(8,128)(2,1)S(1)}, bf16[128,2112]{0,1:T(8,128)(2,1)S(1)}, u32[]{:S(2)}, u32[]{:S(2)}) collective-permute-start(bf16[128,2112]{0,1:T(8,128)(2,1)S(1)} %copy-done.6), channel_id=1, source_target_pairs={{0,32},{32,64},{64,96},{96,128},{128,160},{160,192},{192,224},{224... | collective-permute-start | bytes 1622024 | tf_op jit(solution)/shard_map/ppermute | solution.py:13
  271.8 493.4 %collective-permute-start.51 = (bf16[512,176]{0,1:T(8,128)(2,1)}, bf16[512,176]{0,1:T(8,128)(2,1)}, u32[]{:S(2)}, u32[]{:S(2)}) collective-permute-start(bf16[512,176]{0,1:T(8,128)(2,1)} %get-tuple-element.10), channel_id=1, source_target_pairs={{0,224},{32,256},{64,288},{96,320},{128,352},{160,384},{192,416},{... | collective-permute-start | bytes 540680 | tf_op jit(solution)/shard_map/ppermute | solution.py:13
  277.3 491.5 %collective-permute-start.52 = (bf16[512,176]{0,1:T(8,128)(2,1)}, bf16[512,176]{0,1:T(8,128)(2,1)}, u32[]{:S(2)}, u32[]{:S(2)}) collective-permute-start(bf16[512,176]{0,1:T(8,128)(2,1)} %get-tuple-element.10), channel_id=1, source_target_pairs={{0,256},{32,288},{64,320},{96,352},{128,384},{160,416},{192,448},{... | collective-permute-start | bytes 540680 | tf_op jit(solution)/shard_map/ppermute | solution.py:13
  340.4 28.0 %collective-permute-start.33 = (bf16[128,2112]{0,1:T(8,128)(2,1)S(1)}, bf16[128,2112]{0,1:T(8,128)(2,1)S(1)}, u32[]{:S(2)}, u32[]{:S(2)}) collective-permute-start(bf16[128,2112]{0,1:T(8,128)(2,1)S(1)} %copy-done.6), channel_id=1, source_target_pairs={{0,128},{32,160},{64,192},{96,224},{128,256},{160,288},{192,320},{... | collective-permute-start | bytes 1622024 | tf_op jit(solution)/shard_map/ppermute | solution.py:13
  368.3 32.0 %collective-permute-start.34 = (bf16[128,2112]{0,1:T(8,128)(2,1)S(1)}, bf16[128,2112]{0,1:T(8,128)(2,1)S(1)}, u32[]{:S(2)}, u32[]{:S(2)}) collective-permute-start(bf16[128,2112]{0,1:T(8,128)(2,1)S(1)} %copy-done.6), channel_id=1, source_target_pairs={{0,160},{32,192},{64,224},{96,256},{128,288},{160,320},{192,352},{... | collective-permute-start | bytes 1622024 | tf_op jit(solution)/shard_map/ppermute | solution.py:13
  400.3 37.9 %collective-permute-start.35 = (bf16[128,2112]{0,1:T(8,128)(2,1)S(1)}, bf16[128,2112]{0,1:T(8,128)(2,1)S(1)}, u32[]{:S(2)}, u32[]{:S(2)}) collective-permute-start(bf16[128,2112]{0,1:T(8,128)(2,1)S(1)} %copy-done.6), channel_id=1, source_target_pairs={{0,192},{32,224},{64,256},{96,288},{128,320},{160,352},{192,384},{... | collective-permute-start | bytes 1622024 | tf_op jit(solution)/shard_map/ppermute | solution.py:13
  438.3 36.9 %collective-permute-start.36 = (bf16[128,2112]{0,1:T(8,128)(2,1)S(1)}, bf16[128,2112]{0,1:T(8,128)(2,1)S(1)}, u32[]{:S(2)}, u32[]{:S(2)}) collective-permute-start(bf16[128,2112]{0,1:T(8,128)(2,1)S(1)} %copy-done.6), channel_id=1, source_target_pairs={{0,224},{32,256},{64,288},{96,320},{128,352},{160,384},{192,416},{... | collective-permute-start | bytes 1622024 | tf_op jit(solution)/shard_map/ppermute | solution.py:13
  475.1 26.9 %collective-permute-start.37 = (bf16[128,2112]{0,1:T(8,128)(2,1)S(1)}, bf16[128,2112]{0,1:T(8,128)(2,1)S(1)}, u32[]{:S(2)}, u32[]{:S(2)}) collective-permute-start(bf16[128,2112]{0,1:T(8,128)(2,1)S(1)} %copy-done.6), channel_id=1, source_target_pairs={{0,256},{32,288},{64,320},{96,352},{128,384},{160,416},{192,448},{... | collective-permute-start | bytes 1622024 | tf_op jit(solution)/shard_map/ppermute | solution.py:13
  521.0 45.3 %collective-permute-start.39 = (bf16[128,2112]{0,1:T(8,128)(2,1)S(1)}, bf16[128,2112]{0,1:T(8,128)(2,1)S(1)}, u32[]{:S(2)}, u32[]{:S(2)}) collective-permute-start(bf16[128,2112]{0,1:T(8,128)(2,1)S(1)} %copy-done.6), channel_id=1, source_target_pairs={{0,320},{32,352},{64,384},{96,416},{128,448},{160,480},{192,0},{22... | collective-permute-start | bytes 1622024 | tf_op jit(solution)/shard_map/ppermute | solution.py:13
  566.3 41.2 %collective-permute-start.40 = (bf16[128,2112]{0,1:T(8,128)(2,1)S(1)}, bf16[128,2112]{0,1:T(8,128)(2,1)S(1)}, u32[]{:S(2)}, u32[]{:S(2)}) collective-permute-start(bf16[128,2112]{0,1:T(8,128)(2,1)S(1)} %copy-done.6), channel_id=1, source_target_pairs={{0,352},{32,384},{64,416},{96,448},{128,480},{160,0},{192,32},{224... | collective-permute-start | bytes 1622024 | tf_op jit(solution)/shard_map/ppermute | solution.py:13
  677.3 97.5 %collective-permute-start.53 = (bf16[512,176]{0,1:T(8,128)(2,1)}, bf16[512,176]{0,1:T(8,128)(2,1)S(1)}, u32[]{:S(2)}, u32[]{:S(2)}) collective-permute-start(bf16[512,176]{0,1:T(8,128)(2,1)} %get-tuple-element.10), channel_id=1, source_target_pairs={{0,288},{32,320},{64,352},{96,384},{128,416},{160,448},{192,480},{... | collective-permute-start | bytes 540680 | tf_op jit(solution)/shard_map/ppermute | solution.py:13
  723.1 103.4 %all-to-all-start.1 = ((bf16[32,12,2048]{2,1,0:T(8,128)(2,1)}), bf16[32,12,2048]{2,1,0:T(8,128)(2,1)S(1)}, u32[]{:S(2)}, u32[]{:S(2)}) async-start(bf16[32,12,2048]{2,1,0:T(8,128)(2,1)} %reshape.201), calls=%async_computation.1 | async-start | bytes 4194304 | tf_op jit(solution)/shard_map/all_to_all | solution.py:100
  757.3 25.5 %collective-permute-start.55 = (bf16[512,176]{0,1:T(8,128)(2,1)}, bf16[512,176]{0,1:T(8,128)(2,1)S(1)}, u32[]{:S(2)}, u32[]{:S(2)}) collective-permute-start(bf16[512,176]{0,1:T(8,128)(2,1)} %get-tuple-element.10), channel_id=1, source_target_pairs={{0,352},{32,384},{64,416},{96,448},{128,480},{160,0},{192,32},{224... | collective-permute-start | bytes 540680 | tf_op jit(solution)/shard_map/ppermute | solution.py:13
  (48 other events, 1064.7 us)

commit v2 on v0

--- a/solution.py
+++ b/solution.py
@@ -95,8 +95,9 @@
     returned = lax.all_to_all(result, "expert", split_axis=0, concat_axis=0, tiled=True)
     shared_units = shared_gate_up.shape[2]
     shared_pair = shared_gate_up.reshape(width, 2 * shared_units)
+    normed_shared = normed + (gate_up_full[0, 0] * 0).astype(normed.dtype)
     both = jnp.dot(
-        lax.all_gather(normed, "dp", axis=0, tiled=True),
+        lax.all_gather(normed_shared, "dp", axis=0, tiled=True),
         shared_pair,
         preferred_element_type=jnp.float32,
     )

time: 284 us -> 281 us (0.989)
  waiting for transfers between devices: 123 us -> 97.7 us
  blocking collectives: 74.6 us -> 95.4 us
    all_gather x1, waiting for transfers between devices: 35.1 us -> 10.9 us  [turned_gather(): out = lax.all_gather(both, axis, axis=0, tiled=True)]
    all_to_all x1, blocking collectives: 62.8 us -> 81.3 us  [sent_to_all(): return lax.all_to_all(copies, axis, split_axis=0, concat_axis=0, tiled=True)]
    all_gather x1, waiting for transfers between devices: 17.8 us -> 0.02 us  [per_device(): lax.all_gather(shared_hidden, 'dp', axis=1, tiled=True)]
    all_to_all x1, waiting for transfers between devices: 20.8 us -> 38.5 us  [per_device(): lax.all_to_all(result, 'expert', split_axis=0, concat_axis=0, tiled=True)]
    all_to_all x1, waiting for transfers between devices: 22.2 us -> 18.1 us  [per_device(): lax.all_to_all(outgoing, 'expert', split_axis=0, concat_axis=0, tiled=True)]
    all_gather x1, waiting for transfers between devices: 24.4 us -> 27.4 us  [per_device(): lax.all_gather(normed_shared, 'dp', axis=0, tiled=True)]
  transfers between devices with their start and end apart: 6 -> 6, of which waited for: 6 -> 5; matrix products, arithmetic and copies ran while one was open for 14% -> 14% of each run, Pallas kernels for 0% -> 0%
where the time goes in v2:
time: 281 us; the launch traced here: 280 us
  waiting for transfers between devices  97.7 us (35%)
  blocking collectives  95.4 us (34%)
  starting transfers between devices  23.9 us (9%)
  local copies, waits for them, and re-layouts  18 us (6%)
  matrix products  17.9 us (6%)
  between operations  14 us (5%)
  other arithmetic  13.2 us (5%)
    all_to_all x1, blocking collectives, sent_to_all(): return lax.all_to_all(copies, axis, split_axis=0, concat_axis=0, tiled=True)  81.3 us
    all_to_all x1, waiting for transfers between devices, per_device(): lax.all_to_all(result, 'expert', split_axis=0, concat_axis=0, tiled=True)  38.5 us
    all_gather x1, waiting for transfers between devices, per_device(): lax.all_gather(normed_shared, 'dp', axis=0, tiled=True)  27.4 us
    all_to_all x1, waiting for transfers between devices, per_device(): lax.all_to_all(outgoing, 'expert', split_axis=0, concat_axis=0, tiled=True)  18.1 us
    all_to_all x1, blocking collectives, per_device(): lax.all_to_all(proj_cols, 'dp', split_axis=0, concat_axis=1, tiled=True)  14.1 us
    all_gather x1, waiting for transfers between devices, turned_gather(): out = lax.all_gather(both, axis, axis=0, tiled=True)  10.9 us
    all_to_all x1, starting transfers between devices, per_device(): lax.all_to_all(outgoing, 'expert', split_axis=0, concat_axis=0, tiled=True)  9.67 us
    all_to_all x1, starting transfers between devices, per_device(): lax.all_to_all(result, 'expert', split_axis=0, concat_axis=0, tiled=True)  7.51 us
  transfers between devices with their start and end apart: 6, of which 5 were waited for; matrix products, arithmetic and copies ran while one was open for 14% of the time, Pallas kernels for 0%

profile of v2, /device:TPU:1, one launch (start us, length us, event | category | flops | bytes accessed | tf_op | source)
XLA Modules:
  0.0 280.0 jit_solution(11841598669396796711)
XLA Ops:
  6.5 1.2 copy.30
  7.7 1.9 pad_maximum_fusion
  10.0 81.3 %all_to_all.47 = bf16[16,32,2048]{2,1,0:T(8,128)(2,1)S(1)} all-to-all(bf16[16,32,2048]{2,1,0:T(8,128)(2,1)S(1)} %broadcast_in_dim.50), channel_id=1, replica_groups=mesh['dp'=16,'expert'=32] {'dp'}, dimensions={0} | all-to-all | bytes 4194304 | tf_op jit(solution)/shard_map/all_to_all | solution.py:17
  92.0 14.1 %all_to_all.48 = bf16[16,32,128]{2,1,0:T(8,128)(2,1)S(1)} all-to-all(bf16[16,32,128]{2,1,0:T(8,128)(2,1)S(1)} %bitcast.65), channel_id=1, replica_groups=mesh['dp'=16,'expert'=32] {'dp'}, dimensions={0} | all-to-all | bytes 262144 | tf_op jit(solution)/shard_map/all_to_all | solution.py:66
  106.2 10.9 %all-gather.4.cloned.1.call-done = bf16[2048,2112]{1,0:T(8,128)(2,1)} async-done(((bf16[128,2112]{1,0:T(8,128)(2,1)}), bf16[2048,2112]{1,0:T(8,128)(2,1)}) %all-gather.4.cloned.1.call-update) | async-done | bytes 8650768 | tf_op jit(solution)/shard_map/all_gather | solution.py:28
  117.2 1.2 slice.39
  119.0 0.8 broadcast_add_fusion
  123.3 1.6 reshape.149
  125.0 9.7 %all-to-all-start.2 = ((bf16[32,12,2048]{2,1,0:T(8,128)(2,1)}), bf16[32,12,2048]{2,1,0:T(8,128)(2,1)S(1)}, u32[]{:S(2)}, u32[]{:S(2)}) async-start(bf16[32,12,2048]{2,1,0:T(8,128)(2,1)} %reshape.149), calls=%async_computation.2 | async-start | bytes 4194304 | tf_op jit(solution)/shard_map/all_to_all | solution.py:88
  134.7 27.4 %all-gather.6.cloned.1.call-done = bf16[512,2048]{1,0:T(8,128)(2,1)} async-done(((bf16[32,2048]{1,0:T(8,128)(2,1)}), bf16[512,2048]{1,0:T(8,128)(2,1)}) %all-gather.6.cloned.1.call-update) | async-done | bytes 2097168 | tf_op jit(solution)/shard_map/all_gather | solution.py:100
  162.2 2.5 fusion.23
  164.7 0.8 fusion.7
  165.5 18.1 %all-to-all-done.2 = bf16[32,12,2048]{2,1,0:T(8,128)(2,1)S(1)} async-done(((bf16[32,12,2048]{2,1,0:T(8,128)(2,1)}), bf16[32,12,2048]{2,1,0:T(8,128)(2,1)S(1)}, u32[]{:S(2)}, u32[]{:S(2)}) %all-to-all-start.2) | async-done | bytes 1572896 | tf_op jit(solution)/shard_map/all_to_all | solution.py:88
  183.6 1.4 reshape.150
  185.0 5.8 %fusion = f32[384,1408]{1,0:T(8,128)S(1)} fusion(bf16[384,2048]{1,0:T(8,128)(2,1)} %reshape.150, bf16[2048,2112]{1,0:T(8,128)(2,1)} %all-gather.4.cloned.1.call-done), kind=kOutput, calls=%fused_computation.1 | convolution fusion | flops 2214592512 | bytes 9502720 | tf_op jit(solution)/shard_map/dot_general | solution.py:91
  190.8 3.4 %fusion.3 = bf16[384,2048]{1,0:T(8,128)(2,1)S(1)} fusion(bf16[2048,2112]{1,0:T(8,128)(2,1)} %all-gather.4.cloned.1.call-done, f32[384,1408]{1,0:T(8,128)S(1)} %fusion), kind=kOutput, calls=%fused_computation.5 | convolution fusion | flops 1109704704 | bytes 7077888 | tf_op jit(solution)/shard_map/dot_general | solution.py:93
  194.2 1.6 reshape.153
  195.8 7.5 %all-to-all-start.3 = ((bf16[32,12,2048]{2,1,0:T(8,128)(2,1)}), bf16[32,12,2048]{2,1,0:T(8,128)(2,1)S(1)}, u32[]{:S(2)}, u32[]{:S(2)}) async-start(bf16[32,12,2048]{2,1,0:T(8,128)(2,1)} %reshape.153), calls=%async_computation.3 | async-start | bytes 4194304 | tf_op jit(solution)/shard_map/all_to_all | solution.py:95
  205.4 1.3 copy.29
  208.0 1.2 fusion.19
  209.2 0.9 select_reduce_fusion.1
  210.1 3.7 %fusion.24 = f32[512,128]{1,0:T(8,128)} fusion(bf16[512,2816]{0,1:T(8,128)(2,1)} %all-gather.8.cloned.1.call-done, bf16[2816,128]{1,0:T(8,128)(2,1)} %param.22), kind=kOutput, calls=%fused_computation.56 | convolution fusion | flops 369098752 | bytes 3866624 | tf_op jit(solution)/shard_map/dot_general | solution.py:107
  213.7 38.5 %all-to-all-done.3 = bf16[32,12,2048]{2,1,0:T(8,128)(2,1)S(1)} async-done(((bf16[32,12,2048]{2,1,0:T(8,128)(2,1)}), bf16[32,12,2048]{2,1,0:T(8,128)(2,1)S(1)}, u32[]{:S(2)}, u32[]{:S(2)}) %all-to-all-start.3) | async-done | bytes 1572896 | tf_op jit(solution)/shard_map/all_to_all | solution.py:95
  252.2 6.7 %all-to-all-start.4 = ((f32[16,32,128]{2,1,0:T(8,128)}), f32[16,32,128]{2,1,0:T(8,128)}, u32[]{:S(2)}, u32[]{:S(2)}) async-start(f32[16,32,128]{2,1,0:T(8,128)} %bitcast.64), calls=%async_computation.4 | async-start | bytes 524288 | tf_op jit(solution)/shard_map/all_to_all | solution.py:112
  259.5 0.8 copy.24
  260.3 2.5 reshape.154
  262.8 2.2 gather_fusion
  264.9 1.4 gather.7
  266.3 1.7 multiply_reduce_fusion
  268.0 2.6 all-to-all-done.4
  270.7 1.1 multiply_reduce_fusion.1
  271.8 1.7 multiply_convert_fusion
  (63 shorter events, 8.7 us)
Async XLA Ops:
  6.5 155.6 %copy-start = (bf16[2048,2,176]{0,2,1:T(8,128)(2,1)S(1)}, bf16[2048,2,176]{0,2,1:T(8,128)(2,1)}, u32[]{:S(2)}) copy-start(bf16[2048,2,176]{0,2,1:T(8,128)(2,1)} %param.21) | copy-start | bytes 4325380
  6.5 3.2 %copy-start.5 = (bf16[32,2048]{1,0:T(8,128)(2,1)S(1)}, bf16[32,2048]{1,0:T(8,128)(2,1)}, u32[]{:S(2)}) copy-start(bf16[32,2048]{1,0:T(8,128)(2,1)} %param.13) | copy-start | bytes 393220
  6.5 110.6 %all-gather.4.cloned.1.call-start = ((), (), s32[]{:S(2)}) async-start(), calls=%async_computation.5 | async-start | bytes 9469952 | tf_op jit(solution)/shard_map/all_gather | solution.py:28
  9.6 152.5 %all-gather.6.cloned.1.call-start = ((), (), s32[]{:S(2)}) async-start(), calls=%async_computation.6 | async-start | bytes 2228224 | tf_op jit(solution)/shard_map/all_gather | solution.py:100
  10.0 81.3 %copy-start.4 = (bf16[2048,128]{1,0:T(8,128)(2,1)S(1)}, bf16[2048,128]{1,0:T(8,128)(2,1)}, u32[]{:S(2)}) copy-start(bf16[2048,128]{1,0:T(8,128)(2,1)} %param.14) | copy-start | bytes 1572868
  91.2 14.8 %copy-start.6 = (bf16[32,2048]{1,0:T(8,128)(2,1)S(1)}, bf16[32,2048]{1,0:T(8,128)(2,1)}, u32[]{:S(2)}) copy-start(bf16[32,2048]{1,0:T(8,128)(2,1)} %param.12) | copy-start | bytes 393220
  91.2 27.8 %copy-start.7 = (f32[2048]{0:T(1024)S(1)}, f32[2048]{0:T(1024)}, u32[]{:S(2)}) copy-start(f32[2048]{0:T(1024)} %param.15) | copy-start | bytes 24580
  91.2 28.6 %copy-start.9 = (s32[32,6]{0,1:T(8,128)S(1)}, s32[32,6]{0,1:T(8,128)}, u32[]{:S(2)}) copy-start(s32[32,6]{0,1:T(8,128)} %param.17) | copy-start | bytes 2308
  91.2 28.6 %copy-start.13 = (s32[32]{0:T(128)S(1)}, s32[32]{0:T(128)}, u32[]{:S(2)}) copy-start(s32[32]{0:T(128)} %param.18) | copy-start | bytes 388
  106.2 18.8 %copy-start.2 = (bf16[32,2048]{1,0:T(8,128)(2,1)}, bf16[32,2048]{1,0:T(8,128)(2,1)S(1)}, u32[]{:S(2)}) copy-start(bf16[32,2048]{1,0:T(8,128)(2,1)S(1)} %get-tuple-element.8) | copy-start | bytes 393220
  106.2 18.8 %copy-start.12 = (f32[32]{0:T(128)}, f32[32]{0:T(128)S(1)}, u32[]{:S(2)}) copy-start(f32[32]{0:T(128)S(1)} %add_rsqrt_fusion.1) | copy-start | bytes 388
  121.3 0.5 copy-start.10
  125.0 58.6 %all-to-all-start.2 = ((bf16[32,12,2048]{2,1,0:T(8,128)(2,1)}), bf16[32,12,2048]{2,1,0:T(8,128)(2,1)S(1)}, u32[]{:S(2)}, u32[]{:S(2)}) async-start(bf16[32,12,2048]{2,1,0:T(8,128)(2,1)} %reshape.149), calls=%async_computation.2 | async-start | bytes 4194304 | tf_op jit(solution)/shard_map/all_to_all | solution.py:88
  134.7 75.4 %all-gather.8.cloned.1.call-start = ((), (), s32[]{:S(2)}) async-start(), calls=%async_computation.7 | async-start | bytes 3063808 | tf_op jit(solution)/shard_map/all_gather | solution.py:108
  195.8 56.4 %all-to-all-start.3 = ((bf16[32,12,2048]{2,1,0:T(8,128)(2,1)}), bf16[32,12,2048]{2,1,0:T(8,128)(2,1)S(1)}, u32[]{:S(2)}, u32[]{:S(2)}) async-start(bf16[32,12,2048]{2,1,0:T(8,128)(2,1)} %reshape.153), calls=%async_computation.3 | async-start | bytes 4194304 | tf_op jit(solution)/shard_map/all_to_all | solution.py:95
  252.2 7.3 %copy-start.1 = (bf16[32,12,2048]{2,1,0:T(8,128)(2,1)}, bf16[32,12,2048]{2,1,0:T(8,128)(2,1)S(1)}, u32[]{:S(2)}) copy-start(bf16[32,12,2048]{2,1,0:T(8,128)(2,1)S(1)} %all-to-all-done.3) | copy-start | bytes 4718596
  252.2 18.5 %all-to-all-start.4 = ((f32[16,32,128]{2,1,0:T(8,128)}), f32[16,32,128]{2,1,0:T(8,128)}, u32[]{:S(2)}, u32[]{:S(2)}) async-start(f32[16,32,128]{2,1,0:T(8,128)} %bitcast.64), calls=%async_computation.4 | async-start | bytes 524288 | tf_op jit(solution)/shard_map/all_to_all | solution.py:112
  262.8 3.6 %copy-start.8 = (pred[32,6]{1,0:T(8,128)(4,1)S(1)}, pred[32,6]{1,0:T(8,128)(4,1)}, u32[]{:S(2)}) copy-start(pred[32,6]{1,0:T(8,128)(4,1)} %copy.29) | copy-start | bytes 580
  264.9 5.8 %copy-start.3 = (bf16[32,2048]{1,0:T(8,128)(2,1)S(1)}, bf16[32,2048]{1,0:T(8,128)(2,1)}, u32[]{:S(2)}) copy-start(bf16[32,2048]{1,0:T(8,128)(2,1)} %copy-done.2) | copy-start | bytes 393220
  264.9 6.9 %copy-start.11 = (f32[2048]{0:T(1024)S(1)}, f32[2048]{0:T(1024)}, u32[]{:S(2)}) copy-start(f32[2048]{0:T(1024)} %param.23) | copy-start | bytes 24580
Sparse Core Ops, SparseCore 0:
  9.8 107.3 all-gather.3
  120.0 42.1 all-gather.5
  165.6 42.0 all-gather.7

commit v3 on v0

--- a/solution.py
+++ b/solution.py
@@ -4,6 +4,31 @@
 from jax.sharding import PartitionSpec as P
 
 EPS = 1e-06
+
+
+def core_groups(axis):
+    n = lax.axis_size(axis)
+    return [list(range(0, n, 2)), list(range(1, n, 2))]
+
+
+def with_sibling(blocks, axis):
+    other = lax.ppermute(blocks, axis, [(i, i ^ 1) for i in range(lax.axis_size(axis))])
+    pair = jnp.stack([blocks, other], axis=1)
+    pair = jnp.where(lax.axis_index(axis) % 2 == 0, pair, jnp.flip(pair, axis=1))
+    return pair.reshape(-1, *blocks.shape[1:])
+
+
+def pair_gather(array, axis):
+    blocks = lax.all_gather(array, axis, axis=0, axis_index_groups=core_groups(axis))
+    return with_sibling(blocks, axis)
+
+
+def pair_collect(array, axis):
+    copies = jnp.broadcast_to(array, (lax.axis_size(axis) // 2, *array.shape))
+    blocks = lax.all_to_all(
+        copies, axis, 0, 0, tiled=True, axis_index_groups=core_groups(axis)
+    )
+    return with_sibling(blocks, axis)
 
 
 def in_order(blocks, dim):
@@ -60,9 +85,10 @@
     experts = router_weight.shape[1]
     choose = expert_ids.shape[1]
     capacity = max(2, min(rows, 2 * rows * choose // experts))
-    proj_cols = jnp.dot(
-        collect(attention_out, "dp", 0), out_weight, preferred_element_type=jnp.float32
-    ).astype(jnp.bfloat16)
+    group_attn = in_order(pair_collect(attention_out, "dp"), 0)
+    proj_cols = jnp.dot(group_attn, out_weight, preferred_element_type=jnp.float32).astype(
+        jnp.bfloat16
+    )
     proj = lax.all_to_all(proj_cols, "dp", split_axis=0, concat_axis=1, tiled=True)
     resid = (residual_in.astype(jnp.float32) + proj.astype(jnp.float32)).astype(jnp.bfloat16)
     normed = rms_scale(resid, post_gain).astype(jnp.bfloat16)
@@ -81,22 +107,30 @@
     select = jnp.any(placed.reshape(rows, choose, experts * capacity), axis=1).astype(jnp.bfloat16)
     outgoing = jnp.einsum("rs,rd->sd", select, normed, preferred_element_type=jnp.float32)
     outgoing = outgoing.astype(jnp.bfloat16).reshape(experts, capacity, width)
-    gate_up_all, down_all = turned_gather((expert_gate_up, expert_down), "dp", (1, 2))
-    gate_up_full = gate_up_all[0]
-    down_full = down_all[0]
-    hidden_units = gate_up_full.shape[1] // 2
+    hidden_units = expert_down.shape[1]
+    weights_part = jnp.concatenate([expert_gate_up[0], expert_down[0].T], axis=1)
+    weights_blocks = lax.all_gather(
+        weights_part, "dp", axis=0, axis_index_groups=core_groups("dp")
+    )
     received = lax.all_to_all(outgoing, "expert", split_axis=0, concat_axis=0, tiled=True)
+    weights_blocks = weights_blocks + (received[0, 0, 0] * 0).astype(weights_blocks.dtype)
+    weights_full = in_order(with_sibling(weights_blocks, "dp"), 0)
+    gate_up_full = weights_full[:, : 2 * hidden_units]
+    down_turned_full = weights_full[:, 2 * hidden_units :]
     sources, count, _ = received.shape
     flat = received.reshape(sources * count, width)
     both = jnp.dot(flat, gate_up_full, preferred_element_type=jnp.float32)
     active = (jax.nn.silu(both[:, :hidden_units]) * both[:, hidden_units:]).astype(jnp.bfloat16)
-    result = jnp.dot(active, down_full, preferred_element_type=jnp.float32).astype(jnp.bfloat16)
+    result = lax.dot_general(
+        active, down_turned_full, (((1,), (1,)), ((), ())), preferred_element_type=jnp.float32
+    ).astype(jnp.bfloat16)
     result = result.reshape(sources, count, width)
     returned = lax.all_to_all(result, "expert", split_axis=0, concat_axis=0, tiled=True)
     shared_units = shared_gate_up.shape[2]
     shared_pair = shared_gate_up.reshape(width, 2 * shared_units)
+    normed_shared = normed
     both = jnp.dot(
-        lax.all_gather(normed, "dp", axis=0, tiled=True),
+        in_order(pair_gather(normed_shared, "dp"), 0),
         shared_pair,
         preferred_element_type=jnp.float32,
     )
@@ -104,7 +138,7 @@
         jnp.bfloat16
     )
     out_cols = jnp.dot(
-        lax.all_gather(shared_hidden, "dp", axis=1, tiled=True),
+        in_order(pair_gather(shared_hidden, "dp"), 1),
         shared_down,
         preferred_element_type=jnp.float32,
     )

time: 284 us -> 337 us (1.19)
  local copies, waits for them, and re-layouts: 16.8 us -> 62.1 us
  waiting for transfers between devices: 123 us -> 85.7 us
  other arithmetic: 12.2 us -> 48 us
  starting transfers between devices: 25.1 us -> 50.2 us
  blocking collectives: 74.6 us -> 58.5 us
    all_gather x3, waiting for transfers between devices: 77.4 us -> 29.3 us  [the longest x2 29.3 us: pair_gather(): lax.all_gather(array, axis, axis=0, axis_index_groups=core_groups(axis))]
    ppermute x0 -> x4, starting transfers between devices: none -> 18.2 us  [with_sibling(): lax.ppermute(blocks, axis, [(i, i ^ 1) for i in range(lax.axis_size(axis))])]
    all_to_all x2 -> x1, blocking collectives: 74.6 us -> 58.5 us  [per_device(): lax.all_to_all(outgoing, 'expert', split_axis=0, concat_axis=0, tiled=True)]
    all_to_all x1 -> x2, waiting for transfers between devices: 22.2 us -> 38.2 us  [the longest x1 28.3 us: pair_collect(): lax.all_to_all(copies, axis, 0, 0, tiled=True, axis_index_groups=core_gro...]
    select_n x0 -> x4, other arithmetic: none -> 15.8 us  [with_sibling(): jnp.where(lax.axis_index(axis) % 2 == 0, pair, jnp.flip(pair, axis=1))]
    another operation x4 -> x8, other arithmetic: 0.71 us -> 14.6 us  [the longest x4 11.3 us: with_sibling(): pair = jnp.stack([blocks, other], axis=1)]
    all_to_all x1, waiting for transfers between devices: 20.8 us -> 12.1 us  [per_device(): lax.all_to_all(result, 'expert', split_axis=0, concat_axis=0, tiled=True)]
    dot_general x0 -> x1, local copies, waits for them, and re-layouts: none -> 8.44 us  [per_device(): jnp.dot(in_order(pair_gather(shared_hidden, 'dp'), 1), shared_down, prefe...]
  transfers between devices with their start and end apart: 6 -> 11, of which waited for: 6 -> 6; matrix products, arithmetic and copies ran while one was open for 14% -> 33% of each run, Pallas kernels for 0% -> 0%
where the time goes in v3:
time: 337 us; the launch traced here: 335 us
  waiting for transfers between devices  85.7 us (25%)
  local copies, waits for them, and re-layouts  62.1 us (18%)
  blocking collectives  58.5 us (17%)
  starting transfers between devices  50.2 us (15%)
  other arithmetic  48 us (14%)
  matrix products  16 us (5%)
  between operations  14.2 us (4%)
    all_to_all x1, blocking collectives, per_device(): lax.all_to_all(outgoing, 'expert', split_axis=0, concat_axis=0, tiled=True)  58.5 us
    all_gather x2, waiting for transfers between devices, pair_gather(): lax.all_gather(array, axis, axis=0, axis_index_groups=core_groups(axis))  29.3 us
    all_to_all x1, waiting for transfers between devices, pair_collect(): lax.all_to_all(copies, axis, 0, 0, tiled=True, axis_index_groups=core_gro...  28.3 us
    ppermute x4, starting transfers between devices, with_sibling(): lax.ppermute(blocks, axis, [(i, i ^ 1) for i in range(lax.axis_size(axis))])  18.2 us
    select_n x4, other arithmetic, with_sibling(): jnp.where(lax.axis_index(axis) % 2 == 0, pair, jnp.flip(pair, axis=1))  15.8 us
    all_to_all x1, waiting for transfers between devices, per_device(): lax.all_to_all(result, 'expert', split_axis=0, concat_axis=0, tiled=True)  12.1 us
    another operation x4, other arithmetic, with_sibling(): pair = jnp.stack([blocks, other], axis=1)  11.3 us
    all_to_all x1, starting transfers between devices, pair_collect(): lax.all_to_all(copies, axis, 0, 0, tiled=True, axis_index_groups=core_gro...  11 us
  transfers between devices with their start and end apart: 11, of which 6 were waited for; matrix products, arithmetic and copies ran while one was open for 33% of the time, Pallas kernels for 0%

profile of v3, /device:TPU:1, one launch (start us, length us, event | category | flops | bytes accessed | tf_op | source)
XLA Modules:
  0.0 334.7 jit_solution(3112017796512637248)
XLA Ops:
  6.5 2.2 broadcast_in_dim.50
  8.7 11.0 %all-to-all-start = ((bf16[8,32,2048]{2,1,0:T(8,128)(2,1)}), bf16[8,32,2048]{2,1,0:T(8,128)(2,1)S(1)}, u32[]{:S(2)}, u32[]{:S(2)}) async-start(bf16[8,32,2048]{2,1,0:T(8,128)(2,1)} %broadcast_in_dim.50), calls=%async_computation | async-start | bytes 2097152 | tf_op jit(solution)/shard_map/all_to_all | solution.py:28
  20.8 28.3 %all-to-all-done = bf16[8,32,2048]{2,1,0:T(8,128)(2,1)S(1)} async-done(((bf16[8,32,2048]{2,1,0:T(8,128)(2,1)}), bf16[8,32,2048]{2,1,0:T(8,128)(2,1)S(1)}, u32[]{:S(2)}, u32[]{:S(2)}) %all-to-all-start) | async-done | bytes 1048608 | tf_op jit(solution)/shard_map/all_to_all | solution.py:28
  49.1 2.7 collective-permute-start
  55.5 1.9 reduce-window.6
  64.5 5.1 %all-to-all-start.1 = ((bf16[16,32,128]{2,1,0:T(8,128)(2,1)}), bf16[16,32,128]{2,1,0:T(8,128)(2,1)S(1)}, u32[]{:S(2)}, u32[]{:S(2)}) async-start(bf16[16,32,128]{2,1,0:T(8,128)(2,1)} %bitcast.4), calls=%async_computation.1 | async-start | bytes 262144 | tf_op jit(solution)/shard_map/all_to_all | solution.py:92
  70.4 9.9 %all-to-all-done.1 = bf16[16,32,128]{2,1,0:T(8,128)(2,1)S(1)} async-done(((bf16[16,32,128]{2,1,0:T(8,128)(2,1)}), bf16[16,32,128]{2,1,0:T(8,128)(2,1)S(1)}, u32[]{:S(2)}, u32[]{:S(2)}) %all-to-all-start.1) | async-done | bytes 131104 | tf_op jit(solution)/shard_map/all_to_all | solution.py:92
  83.3 58.5 %all_to_all.44 = bf16[32,12,2048]{2,1,0:T(8,128)(2,1)S(1)} all-to-all(bf16[32,12,2048]{2,1,0:T(8,128)(2,1)} %reshape.145), channel_id=1, replica_groups=mesh['dp'=16,'expert'=32] {'expert'}, dimensions={0} | all-to-all | bytes 3145728 | tf_op jit(solution)/shard_map/all_to_all | solution.py:115
  143.1 4.8 %broadcast_add_fusion = bf16[1024,2112]{1,0:T(8,128)(2,1)} fusion(bf16[1024,2112]{1,0:T(8,128)(2,1)} %all-gather.7.cloned.1.call-done, bf16[]{:T(256)} %bitcast.10), kind=kLoop, calls=%fused_computation.13 | loop fusion | flops 2162688 | bytes 8650754 | tf_op jit(solution)/shard_map/add | solution.py:116
  147.9 6.4 %copy.60 = bf16[8,128,2112]{1,2,0:T(8,128)(2,1)} copy(bf16[8,128,2112]{2,1,0:T(8,128)(2,1)} %bitcast.82) | data formatting | bytes 8650752 | tf_op jit(solution)/shard_map/add | solution.py:116
  154.3 5.4 %collective-permute-start.1 = (bf16[8,128,2112]{1,2,0:T(8,128)(2,1)}, bf16[8,128,2112]{1,2,0:T(8,128)(2,1)}, u32[]{:S(2)}, u32[]{:S(2)}) collective-permute-start(bf16[8,128,2112]{1,2,0:T(8,128)(2,1)} %copy.60), channel_id=1, source_target_pairs={{0,32},{32,0},{64,96},{96,64},{128,160},{160,128},{192,224},{224,1... | collective-permute-start | bytes 12976136 | tf_op jit(solution)/shard_map/ppermute | solution.py:15
  159.8 29.3 %all-gather.9.cloned.1.call-done = bf16[256,2048]{1,0:T(8,128)(2,1)} async-done(((bf16[32,2048]{1,0:T(8,128)(2,1)}), bf16[256,2048]{1,0:T(8,128)(2,1)}) %all-gather.9.cloned.1.call-update) | async-done | bytes 1048592 | tf_op jit(solution)/shard_map/all_gather | solution.py:22
  189.0 7.3 %collective-permute-start.2 = (bf16[8,32,2048]{2,1,0:T(8,128)(2,1)}, bf16[8,32,2048]{2,1,0:T(8,128)(2,1)S(1)}, u32[]{:S(2)}, u32[]{:S(2)}) collective-permute-start(bf16[8,32,2048]{2,1,0:T(8,128)(2,1)} %bitcast.95), channel_id=1, source_target_pairs={{0,32},{32,0},{64,96},{96,64},{128,160},{160,128},{192,224},{224,1... | collective-permute-start | bytes 3145736 | tf_op jit(solution)/shard_map/ppermute | solution.py:15
  196.3 2.3 collective-permute-done.2
  203.8 6.4 %copy.61 = bf16[8,128,2112]{2,1,0:T(8,128)(2,1)} copy(bf16[8,128,2112]{1,2,0:T(8,128)(2,1)} %collective-permute-done.1) | data formatting | bytes 8650752 | tf_op jit(solution)/shard_map/ppermute | solution.py:15
  210.2 8.0 %pad_maximum_fusion = bf16[8,2,128,2112]{3,2,0,1:T(8,128)(2,1)} fusion(bf16[8,1,128,2112]{3,2,0,1:T(8,128)(2,1)} %bitcast.84, bf16[8,1,128,2112]{3,2,0,1:T(8,128)(2,1)} %bitcast.83), kind=kLoop, calls=%fused_computation.2 | loop fusion | flops 4325376 | bytes 17301504 | tf_op jit(solution)/shard_map/stack | solution.py:16
  218.2 12.5 %reverse_select_fusion = bf16[8,2,128,2112]{3,2,0,1:T(8,128)(2,1)} fusion(bf16[8,2,128,2112]{3,2,0,1:T(8,128)(2,1)} %pad_maximum_fusion, pred[]{:T(512)S(6)} %eq.58), kind=kLoop, calls=%fused_computation.1 | loop fusion | flops 4325376 | bytes 17301504 | tf_op jit(solution)/shard_map/jit(_where)/select_n | solution.py:17
  230.7 8.2 %copy.62 = bf16[8,2,128,2112]{3,2,1,0:T(8,128)(2,1)} copy(bf16[8,2,128,2112]{3,2,0,1:T(8,128)(2,1)} %reverse_select_fusion) | data formatting | bytes 17301504 | tf_op jit(solution)/shard_map/jit(_where)/select_n | solution.py:17
  238.9 5.2 %fusion = f32[384,1408]{1,0:T(8,128)S(1)} fusion(bf16[384,2048]{1,0:T(8,128)(2,1)S(1)} %copy-done.7, bf16[2048,2112]{1,0:T(8,128)(2,1)} %bitcast.86), kind=kOutput, calls=%fused_computation.3 | convolution fusion | flops 2214592512 | bytes 9502720 | tf_op jit(solution)/shard_map/dot_general | solution.py:122
  244.1 3.3 fusion.4
  249.0 9.3 %all-to-all-start.3 = ((bf16[32,12,2048]{2,1,0:T(8,128)(2,1)}), bf16[32,12,2048]{2,1,0:T(8,128)(2,1)S(1)}, u32[]{:S(2)}, u32[]{:S(2)}) async-start(bf16[32,12,2048]{2,1,0:T(8,128)(2,1)} %reshape.147), calls=%async_computation.3 | async-start | bytes 4194304 | tf_op jit(solution)/shard_map/all_to_all | solution.py:128
  258.3 2.7 copy.84
  261.1 2.8 collective-permute-start.3
  273.2 2.2 reverse_select_fusion.1
  275.4 7.6 %copy.66 = bf16[512,16,176]{2,1,0:T(8,128)(2,1)} copy(bf16[512,16,176]{0,2,1:T(8,128)(2,1)} %bitcast.85) | data formatting | bytes 5767168 | tf_op jit(solution)/shard_map/transpose | solution.py:37
  283.0 8.4 %dot_general.29 = bf16[16,32,2816]{2,1,0:T(8,128)(2,1)} reshape(bf16[512,16,176]{2,1,0:T(8,128)(2,1)} %copy.66) | data formatting | bytes 5767168 | tf_op jit(solution)/shard_map/dot_general | solution.py:140
  291.4 3.4 %fusion.8 = f32[16,32,128]{2,1,0:T(8,128)} fusion(bf16[16,32,2816]{2,1,0:T(8,128)(2,1)} %dot_general.29, bf16[2816,128]{1,0:T(8,128)(2,1)S(1)} %copy-done.8), kind=kOutput, calls=%fused_computation.21 | convolution fusion | flops 369098752 | bytes 3866624 | tf_op jit(solution)/shard_map/dot_general | solution.py:140
  294.9 12.1 %all-to-all-done.3 = bf16[32,12,2048]{2,1,0:T(8,128)(2,1)S(1)} async-done(((bf16[32,12,2048]{2,1,0:T(8,128)(2,1)}), bf16[32,12,2048]{2,1,0:T(8,128)(2,1)S(1)}, u32[]{:S(2)}, u32[]{:S(2)}) %all-to-all-start.3) | async-done | bytes 1572896 | tf_op jit(solution)/shard_map/all_to_all | solution.py:128
  307.0 6.5 %all-to-all-start.4 = ((f32[16,32,128]{2,1,0:T(8,128)}), f32[16,32,128]{2,1,0:T(8,128)}, u32[]{:S(2)}, u32[]{:S(2)}) async-start(f32[16,32,128]{2,1,0:T(8,128)} %fusion.8), calls=%async_computation.4 | async-start | bytes 524288 | tf_op jit(solution)/shard_map/all_to_all | solution.py:145
  313.6 2.5 reshape.148
  316.1 2.3 gather_fusion
  321.5 3.8 %all-to-all-done.4 = f32[16,32,128]{2,1,0:T(8,128)} async-done(((f32[16,32,128]{2,1,0:T(8,128)}), f32[16,32,128]{2,1,0:T(8,128)}, u32[]{:S(2)}, u32[]{:S(2)}) %all-to-all-start.4) | async-done | bytes 262176 | tf_op jit(solution)/shard_map/all_to_all | solution.py:145
  (101 shorter events, 38.3 us)
Async XLA Ops:
  6.5 194.1 %copy-start = (bf16[2048,2,176]{0,2,1:T(8,128)(2,1)S(1)}, bf16[2048,2,176]{0,2,1:T(8,128)(2,1)}, u32[]{:S(2)}) copy-start(bf16[2048,2,176]{0,2,1:T(8,128)(2,1)} %param.21) | copy-start | bytes 4325380
  6.5 13.2 %copy-start.11 = (bf16[1,704,128]{2,1,0:T(8,128)(2,1)S(1)}, bf16[1,704,128]{2,1,0:T(8,128)(2,1)}, u32[]{:S(2)}) copy-start(bf16[1,704,128]{2,1,0:T(8,128)(2,1)} %param.20) | copy-start | bytes 540676
  6.5 13.4 %copy-start.10 = (bf16[1,128,1408]{2,1,0:T(8,128)(2,1)S(1)}, bf16[1,128,1408]{2,1,0:T(8,128)(2,1)}, u32[]{:S(2)}) copy-start(bf16[1,128,1408]{2,1,0:T(8,128)(2,1)} %param.19) | copy-start | bytes 1081348
  8.7 43.2 %copy-start.16 = (s32[32,6]{0,1:T(8,128)S(1)}, s32[32,6]{0,1:T(8,128)}, u32[]{:S(2)}) copy-start(s32[32,6]{0,1:T(8,128)} %param.17) | copy-start | bytes 2308
  8.7 43.2 %copy-start.19 = (s32[32]{0:T(128)S(1)}, s32[32]{0:T(128)}, u32[]{:S(2)}) copy-start(s32[32]{0:T(128)} %param.18) | copy-start | bytes 388
  8.7 40.4 %all-to-all-start = ((bf16[8,32,2048]{2,1,0:T(8,128)(2,1)}), bf16[8,32,2048]{2,1,0:T(8,128)(2,1)S(1)}, u32[]{:S(2)}, u32[]{:S(2)}) async-start(bf16[8,32,2048]{2,1,0:T(8,128)(2,1)} %broadcast_in_dim.50), calls=%async_computation | async-start | bytes 2097152 | tf_op jit(solution)/shard_map/all_to_all | solution.py:28
  19.7 123.4 %all-gather.7.cloned.1.call-start = ((), (), s32[]{:S(2)}) async-start(), calls=%async_computation.5 | async-start | bytes 5013504 | tf_op jit(solution)/shard_map/all_gather | solution.py:112
  49.1 12.8 %collective-permute-start = (bf16[8,32,2048]{2,1,0:T(8,128)(2,1)S(1)}, bf16[8,32,2048]{2,1,0:T(8,128)(2,1)S(1)}, u32[]{:S(2)}, u32[]{:S(2)}) collective-permute-start(bf16[8,32,2048]{2,1,0:T(8,128)(2,1)S(1)} %all-to-all-done), channel_id=1, source_target_pairs={{0,32},{32,0},{64,96},{96,64},{128,160},{160,128},{192,224},{224,1... | collective-permute-start | bytes 3145736 | tf_op jit(solution)/shard_map/ppermute | solution.py:15
  62.1 1.0 copy-start.9
  62.7 7.0 %copy-start.13 = (s32[32,6]{0,1:T(8,128)S(1)}, s32[32,6]{0,1:T(8,128)}, u32[]{:S(2)}) copy-start(s32[32,6]{0,1:T(8,128)} %select_reduce_fusion) | copy-start | bytes 2308
  62.7 7.0 %copy-start.15 = (s32[32,6]{0,1:T(8,128)S(1)}, s32[32,6]{0,1:T(8,128)}, u32[]{:S(2)}) copy-start(s32[32,6]{0,1:T(8,128)} %copy.57) | copy-start | bytes 2308
  62.7 17.5 %copy-start.12 = (bf16[32,2048]{1,0:T(8,128)(2,1)S(1)}, bf16[32,2048]{1,0:T(8,128)(2,1)}, u32[]{:S(2)}) copy-start(bf16[32,2048]{1,0:T(8,128)(2,1)} %param.12) | copy-start | bytes 393220
  62.7 18.3 %copy-start.18 = (f32[2048]{0:T(1024)S(1)}, f32[2048]{0:T(1024)}, u32[]{:S(2)}) copy-start(f32[2048]{0:T(1024)} %param.15) | copy-start | bytes 24580
  64.5 15.7 %all-to-all-start.1 = ((bf16[16,32,128]{2,1,0:T(8,128)(2,1)}), bf16[16,32,128]{2,1,0:T(8,128)(2,1)S(1)}, u32[]{:S(2)}, u32[]{:S(2)}) async-start(bf16[16,32,128]{2,1,0:T(8,128)(2,1)} %bitcast.4), calls=%async_computation.1 | async-start | bytes 262144 | tf_op jit(solution)/shard_map/all_to_all | solution.py:92
  69.6 119.4 %all-gather.9.cloned.1.call-start = ((), (), s32[]{:S(2)}) async-start(), calls=%async_computation.6 | async-start | bytes 1179648 | tf_op jit(solution)/shard_map/all_gather | solution.py:22
  80.4 0.6 copy-start.4
  81.2 0.7 copy-start.6
  154.3 49.5 %collective-permute-start.1 = (bf16[8,128,2112]{1,2,0:T(8,128)(2,1)}, bf16[8,128,2112]{1,2,0:T(8,128)(2,1)}, u32[]{:S(2)}, u32[]{:S(2)}) collective-permute-start(bf16[8,128,2112]{1,2,0:T(8,128)(2,1)} %copy.60), channel_id=1, source_target_pairs={{0,32},{32,0},{64,96},{96,64},{128,160},{160,128},{192,224},{224,1... | collective-permute-start | bytes 12976136 | tf_op jit(solution)/shard_map/ppermute | solution.py:15
  159.7 98.6 %all-gather.11.cloned.1.call-start = ((), (), s32[]{:S(2)}) async-start(), calls=%async_computation.7 | async-start | bytes 1622016 | tf_op jit(solution)/shard_map/all_gather | solution.py:22
  189.0 9.6 %collective-permute-start.2 = (bf16[8,32,2048]{2,1,0:T(8,128)(2,1)}, bf16[8,32,2048]{2,1,0:T(8,128)(2,1)S(1)}, u32[]{:S(2)}, u32[]{:S(2)}) collective-permute-start(bf16[8,32,2048]{2,1,0:T(8,128)(2,1)} %bitcast.95), channel_id=1, source_target_pairs={{0,32},{32,0},{64,96},{96,64},{128,160},{160,128},{192,224},{224,1... | collective-permute-start | bytes 3145736 | tf_op jit(solution)/shard_map/ppermute | solution.py:15
  230.7 8.2 %copy-start.7 = (bf16[384,2048]{1,0:T(8,128)(2,1)S(1)}, bf16[384,2048]{1,0:T(8,128)(2,1)}, u32[]{:S(2)}) copy-start(bf16[384,2048]{1,0:T(8,128)(2,1)} %reshape.146) | copy-start | bytes 4718596
  249.0 57.9 %all-to-all-start.3 = ((bf16[32,12,2048]{2,1,0:T(8,128)(2,1)}), bf16[32,12,2048]{2,1,0:T(8,128)(2,1)S(1)}, u32[]{:S(2)}, u32[]{:S(2)}) async-start(bf16[32,12,2048]{2,1,0:T(8,128)(2,1)} %reshape.147), calls=%async_computation.3 | async-start | bytes 4194304 | tf_op jit(solution)/shard_map/all_to_all | solution.py:128
  258.3 12.2 %copy-start.3 = (bf16[4096,176]{0,1:T(8,128)(2,1)S(1)}, bf16[4096,176]{0,1:T(8,128)(2,1)}, u32[]{:S(2)}) copy-start(bf16[4096,176]{0,1:T(8,128)(2,1)} %all-gather.11.cloned.1.call-done) | copy-start | bytes 4325380
  261.1 10.5 %collective-permute-start.3 = (bf16[8,512,176]{1,2,0:T(8,128)(2,1)}, bf16[8,512,176]{1,2,0:T(8,128)(2,1)}, u32[]{:S(2)}, u32[]{:S(2)}) collective-permute-start(bf16[8,512,176]{1,2,0:T(8,128)(2,1)} %bitcast.80), channel_id=1, source_target_pairs={{0,32},{32,0},{64,96},{96,64},{128,160},{160,128},{192,224},{224,1... | collective-permute-start | bytes 4325384 | tf_op jit(solution)/shard_map/ppermute | solution.py:15
  283.0 8.4 %copy-start.8 = (bf16[2816,128]{1,0:T(8,128)(2,1)S(1)}, bf16[2816,128]{1,0:T(8,128)(2,1)}, u32[]{:S(2)}) copy-start(bf16[2816,128]{1,0:T(8,128)(2,1)} %param.22) | copy-start | bytes 2162692
  307.0 6.5 %copy-start.2 = (bf16[32,12,2048]{2,1,0:T(8,128)(2,1)}, bf16[32,12,2048]{2,1,0:T(8,128)(2,1)S(1)}, u32[]{:S(2)}) copy-start(bf16[32,12,2048]{2,1,0:T(8,128)(2,1)S(1)} %all-to-all-done.3) | copy-start | bytes 4718596
  307.0 18.3 %all-to-all-start.4 = ((f32[16,32,128]{2,1,0:T(8,128)}), f32[16,32,128]{2,1,0:T(8,128)}, u32[]{:S(2)}, u32[]{:S(2)}) async-start(f32[16,32,128]{2,1,0:T(8,128)} %fusion.8), calls=%async_computation.4 | async-start | bytes 524288 | tf_op jit(solution)/shard_map/all_to_all | solution.py:145
  316.1 3.7 %copy-start.14 = (pred[32,6]{1,0:T(8,128)(4,1)S(1)}, pred[32,6]{1,0:T(8,128)(4,1)}, u32[]{:S(2)}) copy-start(pred[32,6]{1,0:T(8,128)(4,1)} %copy.58) | copy-start | bytes 580
  316.1 12.0 %copy-start.1 = (bf16[2048,2,176]{0,2,1:T(8,128)(2,1)S(1)}, bf16[2048,2,176]{0,2,1:T(8,128)(2,1)}, u32[]{:S(2)}) copy-start(bf16[2048,2,176]{0,2,1:T(8,128)(2,1)} %param.21) | copy-start | bytes 4325380
  318.4 6.9 %copy-start.5 = (bf16[32,2048]{1,0:T(8,128)(2,1)S(1)}, bf16[32,2048]{1,0:T(8,128)(2,1)}, u32[]{:S(2)}) copy-start(bf16[32,2048]{1,0:T(8,128)(2,1)} %copy-done.4) | copy-start | bytes 393220
  318.4 8.0 %copy-start.17 = (f32[2048]{0:T(1024)S(1)}, f32[2048]{0:T(1024)}, u32[]{:S(2)}) copy-start(f32[2048]{0:T(1024)} %param.23) | copy-start | bytes 24580
Sparse Core Ops, SparseCore 0:
  22.6 69.7 all-gather.6
  159.8 29.1 all-gather.8
  202.5 36.4 all-gather.10

commit v4 on v0

--- a/solution.py
+++ b/solution.py
@@ -4,6 +4,26 @@
 from jax.sharding import PartitionSpec as P
 
 EPS = 1e-06
+
+
+def core_groups(axis):
+    n = lax.axis_size(axis)
+    return [list(range(0, n, 2)), list(range(1, n, 2))]
+
+
+def with_sibling(blocks, axis):
+    other = lax.ppermute(blocks, axis, [(i, i ^ 1) for i in range(lax.axis_size(axis))])
+    pair = jnp.stack([blocks, other], axis=1)
+    pair = jnp.where(lax.axis_index(axis) % 2 == 0, pair, jnp.flip(pair, axis=1))
+    return pair.reshape(-1, *blocks.shape[1:])
+
+
+def pair_collect(array, axis):
+    copies = jnp.broadcast_to(array, (lax.axis_size(axis) // 2, *array.shape))
+    blocks = lax.all_to_all(
+        copies, axis, 0, 0, tiled=True, axis_index_groups=core_groups(axis)
+    )
+    return with_sibling(blocks, axis)
 
 
 def in_order(blocks, dim):
@@ -61,7 +81,7 @@
     choose = expert_ids.shape[1]
     capacity = max(2, min(rows, 2 * rows * choose // experts))
     proj_cols = jnp.dot(
-        collect(attention_out, "dp", 0), out_weight, preferred_element_type=jnp.float32
+        in_order(pair_collect(attention_out, "dp"), 0), out_weight, preferred_element_type=jnp.float32
     ).astype(jnp.bfloat16)
     proj = lax.all_to_all(proj_cols, "dp", split_axis=0, concat_axis=1, tiled=True)
     resid = (residual_in.astype(jnp.float32) + proj.astype(jnp.float32)).astype(jnp.bfloat16)

time: 284 us -> 267 us (0.940)
  blocking collectives: 74.6 us -> 49.9 us
  starting transfers between devices: 25.1 us -> 29.5 us
    all_to_all x1, blocking collectives: 62.8 us -> 37.9 us  [pair_collect(): lax.all_to_all(copies, axis, 0, 0, tiled=True, axis_index_groups=core_gro...]
    ppermute x0 -> x1, starting transfers between devices: none -> 4.35 us  [with_sibling(): lax.ppermute(blocks, axis, [(i, i ^ 1) for i in range(lax.axis_size(axis))])]
  transfers between devices with their start and end apart: 6 -> 7, of which waited for: 6 -> 7; matrix products, arithmetic and copies ran while one was open for 14% -> 15% of each run, Pallas kernels for 0% -> 0%
where the time goes in v4:
time: 267 us; the launch traced here: 266 us
  waiting for transfers between devices  125 us (47%)
  blocking collectives  49.9 us (19%)
  starting transfers between devices  29.5 us (11%)
  matrix products  17.7 us (7%)
  local copies, waits for them, and re-layouts  17.1 us (6%)
  between operations  13.4 us (5%)
  other arithmetic  13 us (5%)
    all_to_all x1, blocking collectives, pair_collect(): lax.all_to_all(copies, axis, 0, 0, tiled=True, axis_index_groups=core_gro...  37.9 us
    all_gather x1, waiting for transfers between devices, turned_gather(): out = lax.all_gather(both, axis, axis=0, tiled=True)  35.3 us
    all_gather x1, waiting for transfers between devices, per_device(): lax.all_gather(normed, 'dp', axis=0, tiled=True)  24.4 us
    all_to_all x1, waiting for transfers between devices, per_device(): lax.all_to_all(outgoing, 'expert', split_axis=0, concat_axis=0, tiled=True)  21.9 us
    all_to_all x1, waiting for transfers between devices, per_device(): lax.all_to_all(result, 'expert', split_axis=0, concat_axis=0, tiled=True)  20.7 us
    all_gather x1, waiting for transfers between devices, per_device(): lax.all_gather(shared_hidden, 'dp', axis=1, tiled=True)  17.9 us
    all_to_all x1, blocking collectives, per_device(): lax.all_to_all(proj_cols, 'dp', split_axis=0, concat_axis=1, tiled=True)  12 us
    all_to_all x1, starting transfers between devices, per_device(): lax.all_to_all(outgoing, 'expert', split_axis=0, concat_axis=0, tiled=True)  9.68 us
  transfers between devices with their start and end apart: 7, of which 7 were waited for; matrix products, arithmetic and copies ran while one was open for 15% of the time, Pallas kernels for 0%

profile of v4, /device:TPU:1, one launch (start us, length us, event | category | flops | bytes accessed | tf_op | source)
XLA Modules:
  0.0 265.8 jit_solution(15594154486618220334)
XLA Ops:
  6.5 1.1 broadcast_in_dim.50
  7.7 37.9 %all_to_all.47 = bf16[8,32,2048]{2,1,0:T(8,128)(2,1)S(1)} all-to-all(bf16[8,32,2048]{2,1,0:T(8,128)(2,1)S(1)} %broadcast_in_dim.50), channel_id=1, replica_groups={{0,64,128,192,256,320,384,448},{32,96,160,224,288,352,416,480},{1,65,12..., dimensions={0} | all-to-all | bytes 2097152 | tf_op jit(solution)/shard_map/all_to_all | solution.py:23
  45.6 4.4 %collective-permute-start = (bf16[8,32,2048]{2,1,0:T(8,128)(2,1)S(1)}, bf16[8,32,2048]{2,1,0:T(8,128)(2,1)S(1)}, u32[]{:S(2)}, u32[]{:S(2)}) collective-permute-start(bf16[8,32,2048]{2,1,0:T(8,128)(2,1)S(1)} %all_to_all.47), channel_id=1, source_target_pairs={{0,32},{32,0},{64,96},{96,64},{128,160},{160,128},{192,224},{224,1... | collective-permute-start | bytes 3145736 | tf_op jit(solution)/shard_map/ppermute | solution.py:15
  49.9 2.3 collective-permute-done
  54.2 12.0 %all_to_all.48 = bf16[16,32,128]{2,1,0:T(8,128)(2,1)S(1)} all-to-all(bf16[16,32,128]{2,1,0:T(8,128)(2,1)S(1)} %bitcast.72), channel_id=1, replica_groups=mesh['dp'=16,'expert'=32] {'dp'}, dimensions={0} | all-to-all | bytes 262144 | tf_op jit(solution)/shard_map/all_to_all | solution.py:86
  68.0 0.9 pad_maximum_fusion.1
  71.9 1.6 reshape.143
  73.5 9.7 %all-to-all-start.2 = ((bf16[32,12,2048]{2,1,0:T(8,128)(2,1)}), bf16[32,12,2048]{2,1,0:T(8,128)(2,1)S(1)}, u32[]{:S(2)}, u32[]{:S(2)}) async-start(bf16[32,12,2048]{2,1,0:T(8,128)(2,1)} %reshape.143), calls=%async_computation.2 | async-start | bytes 4194304 | tf_op jit(solution)/shard_map/all_to_all | solution.py:108
  83.2 24.4 %all-gather.6.cloned.1.call-done = bf16[512,2048]{1,0:T(8,128)(2,1)} async-done(((bf16[32,2048]{1,0:T(8,128)(2,1)}), bf16[512,2048]{1,0:T(8,128)(2,1)}) %all-gather.6.cloned.1.call-update) | async-done | bytes 2097168 | tf_op jit(solution)/shard_map/all_gather | solution.py:119
  107.7 2.5 fusion.21
  110.2 0.8 fusion.7
  111.0 21.9 %all-to-all-done.2 = bf16[32,12,2048]{2,1,0:T(8,128)(2,1)S(1)} async-done(((bf16[32,12,2048]{2,1,0:T(8,128)(2,1)}), bf16[32,12,2048]{2,1,0:T(8,128)(2,1)S(1)}, u32[]{:S(2)}, u32[]{:S(2)}) %all-to-all-start.2) | async-done | bytes 1572896 | tf_op jit(solution)/shard_map/all_to_all | solution.py:108
  133.0 1.4 reshape.144
  134.4 35.3 %all-gather.4.cloned.1.call-done = bf16[2048,2112]{1,0:T(8,128)(2,1)} async-done(((bf16[128,2112]{1,0:T(8,128)(2,1)}), bf16[2048,2112]{1,0:T(8,128)(2,1)}) %all-gather.4.cloned.1.call-update) | async-done | bytes 8650768 | tf_op jit(solution)/shard_map/all_gather | solution.py:48
  169.7 5.7 %fusion = f32[384,1408]{1,0:T(8,128)S(1)} fusion(bf16[384,2048]{1,0:T(8,128)(2,1)} %reshape.144, bf16[2048,2112]{1,0:T(8,128)(2,1)} %all-gather.4.cloned.1.call-done), kind=kOutput, calls=%fused_computation.1 | convolution fusion | flops 2214592512 | bytes 9502720 | tf_op jit(solution)/shard_map/dot_general | solution.py:111
  175.4 3.3 %fusion.3 = bf16[384,2048]{1,0:T(8,128)(2,1)S(1)} fusion(bf16[2048,2112]{1,0:T(8,128)(2,1)} %all-gather.4.cloned.1.call-done, f32[384,1408]{1,0:T(8,128)S(1)} %fusion), kind=kOutput, calls=%fused_computation.6 | convolution fusion | flops 1109704704 | bytes 7077888 | tf_op jit(solution)/shard_map/dot_general | solution.py:113
  178.8 1.5 reshape.147
  180.3 9.3 %all-to-all-start.3 = ((bf16[32,12,2048]{2,1,0:T(8,128)(2,1)}), bf16[32,12,2048]{2,1,0:T(8,128)(2,1)S(1)}, u32[]{:S(2)}, u32[]{:S(2)}) async-start(bf16[32,12,2048]{2,1,0:T(8,128)(2,1)} %reshape.147), calls=%async_computation.3 | async-start | bytes 4194304 | tf_op jit(solution)/shard_map/all_to_all | solution.py:115
  191.6 1.3 copy.32
  194.2 1.1 fusion.20
  195.3 0.9 select_reduce_fusion.1
  196.2 17.9 %all-gather.8.cloned.1.call-done = bf16[512,2816]{0,1:T(8,128)(2,1)} async-done(((bf16[512,176]{0,1:T(8,128)(2,1)}), bf16[512,2816]{0,1:T(8,128)(2,1)}) %all-gather.8.cloned.1.call-update) | async-done | bytes 2883600 | tf_op jit(solution)/shard_map/all_gather | solution.py:127
  214.1 3.7 %fusion.22 = f32[512,128]{1,0:T(8,128)} fusion(bf16[512,2816]{0,1:T(8,128)(2,1)} %all-gather.8.cloned.1.call-done, bf16[2816,128]{1,0:T(8,128)(2,1)} %param.22), kind=kOutput, calls=%fused_computation.57 | convolution fusion | flops 369098752 | bytes 3866624 | tf_op jit(solution)/shard_map/dot_general | solution.py:126
  217.7 20.7 %all-to-all-done.3 = bf16[32,12,2048]{2,1,0:T(8,128)(2,1)S(1)} async-done(((bf16[32,12,2048]{2,1,0:T(8,128)(2,1)}), bf16[32,12,2048]{2,1,0:T(8,128)(2,1)S(1)}, u32[]{:S(2)}, u32[]{:S(2)}) %all-to-all-start.3) | async-done | bytes 1572896 | tf_op jit(solution)/shard_map/all_to_all | solution.py:115
  238.5 6.1 %all-to-all-start.4 = ((f32[16,32,128]{2,1,0:T(8,128)}), f32[16,32,128]{2,1,0:T(8,128)}, u32[]{:S(2)}, u32[]{:S(2)}) async-start(f32[16,32,128]{2,1,0:T(8,128)} %bitcast.71), calls=%async_computation.4 | async-start | bytes 524288 | tf_op jit(solution)/shard_map/all_to_all | solution.py:131
  246.0 2.5 reshape.148
  248.5 2.2 gather_fusion
  250.7 1.4 gather.7
  252.1 1.7 multiply_reduce_fusion
  253.8 2.7 all-to-all-done.4
  256.4 1.1 multiply_reduce_fusion.1
  257.6 1.7 multiply_convert_fusion
  (68 shorter events, 11.4 us)
Async XLA Ops:
  6.5 101.2 %copy-start = (bf16[2048,2,176]{0,2,1:T(8,128)(2,1)S(1)}, bf16[2048,2,176]{0,2,1:T(8,128)(2,1)}, u32[]{:S(2)}) copy-start(bf16[2048,2,176]{0,2,1:T(8,128)(2,1)} %param.21) | copy-start | bytes 4325380
  6.5 101.1 %all-gather.6.cloned.1.call-start = ((), (), s32[]{:S(2)}) async-start(), calls=%async_computation.6 | async-start | bytes 2228224 | tf_op jit(solution)/shard_map/all_gather | solution.py:119
  45.6 6.6 %collective-permute-start = (bf16[8,32,2048]{2,1,0:T(8,128)(2,1)S(1)}, bf16[8,32,2048]{2,1,0:T(8,128)(2,1)S(1)}, u32[]{:S(2)}, u32[]{:S(2)}) collective-permute-start(bf16[8,32,2048]{2,1,0:T(8,128)(2,1)S(1)} %all_to_all.47), channel_id=1, source_target_pairs={{0,32},{32,0},{64,96},{96,64},{128,160},{160,128},{192,224},{224,1... | collective-permute-start | bytes 3145736 | tf_op jit(solution)/shard_map/ppermute | solution.py:15
  52.4 1.0 copy-start.5
  53.0 13.2 %copy-start.8 = (bf16[32,2048]{1,0:T(8,128)(2,1)S(1)}, bf16[32,2048]{1,0:T(8,128)(2,1)}, u32[]{:S(2)}) copy-start(bf16[32,2048]{1,0:T(8,128)(2,1)} %param.12) | copy-start | bytes 393220
  53.0 14.0 %copy-start.13 = (f32[2048]{0:T(1024)S(1)}, f32[2048]{0:T(1024)}, u32[]{:S(2)}) copy-start(f32[2048]{0:T(1024)} %param.15) | copy-start | bytes 24580
  53.0 14.8 %copy-start.7 = (bf16[1,704,128]{2,1,0:T(8,128)(2,1)S(1)}, bf16[1,704,128]{2,1,0:T(8,128)(2,1)}, u32[]{:S(2)}) copy-start(bf16[1,704,128]{2,1,0:T(8,128)(2,1)} %param.20) | copy-start | bytes 540676
  53.4 14.5 %copy-start.6 = (bf16[1,128,1408]{2,1,0:T(8,128)(2,1)S(1)}, bf16[1,128,1408]{2,1,0:T(8,128)(2,1)}, u32[]{:S(2)}) copy-start(bf16[1,128,1408]{2,1,0:T(8,128)(2,1)} %param.19) | copy-start | bytes 1081348
  54.1 14.7 %copy-start.10 = (s32[32,6]{0,1:T(8,128)S(1)}, s32[32,6]{0,1:T(8,128)}, u32[]{:S(2)}) copy-start(s32[32,6]{0,1:T(8,128)} %param.17) | copy-start | bytes 2308
  54.2 14.7 %copy-start.14 = (s32[32]{0:T(128)S(1)}, s32[32]{0:T(128)}, u32[]{:S(2)}) copy-start(s32[32]{0:T(128)} %param.18) | copy-start | bytes 388
  66.3 0.7 copy-start.2
  67.7 3.5 %copy-start.4 = (bf16[32,2048]{1,0:T(8,128)(2,1)S(1)}, bf16[32,2048]{1,0:T(8,128)(2,1)}, u32[]{:S(2)}) copy-start(bf16[32,2048]{1,0:T(8,128)(2,1)} %fusion.11) | copy-start | bytes 393220
  67.8 101.9 %all-gather.4.cloned.1.call-start = ((), (), s32[]{:S(2)}) async-start(), calls=%async_computation.5 | async-start | bytes 9469952 | tf_op jit(solution)/shard_map/all_gather | solution.py:48
  70.3 0.8 copy-start.11
  73.5 59.4 %all-to-all-start.2 = ((bf16[32,12,2048]{2,1,0:T(8,128)(2,1)}), bf16[32,12,2048]{2,1,0:T(8,128)(2,1)S(1)}, u32[]{:S(2)}, u32[]{:S(2)}) async-start(bf16[32,12,2048]{2,1,0:T(8,128)(2,1)} %reshape.143), calls=%async_computation.2 | async-start | bytes 4194304 | tf_op jit(solution)/shard_map/all_to_all | solution.py:108
  83.2 130.9 %all-gather.8.cloned.1.call-start = ((), (), s32[]{:S(2)}) async-start(), calls=%async_computation.7 | async-start | bytes 3063808 | tf_op jit(solution)/shard_map/all_gather | solution.py:127
  180.3 58.2 %all-to-all-start.3 = ((bf16[32,12,2048]{2,1,0:T(8,128)(2,1)}), bf16[32,12,2048]{2,1,0:T(8,128)(2,1)S(1)}, u32[]{:S(2)}, u32[]{:S(2)}) async-start(bf16[32,12,2048]{2,1,0:T(8,128)(2,1)} %reshape.147), calls=%async_computation.3 | async-start | bytes 4194304 | tf_op jit(solution)/shard_map/all_to_all | solution.py:115
  238.5 6.8 %copy-start.1 = (bf16[32,12,2048]{2,1,0:T(8,128)(2,1)}, bf16[32,12,2048]{2,1,0:T(8,128)(2,1)S(1)}, u32[]{:S(2)}) copy-start(bf16[32,12,2048]{2,1,0:T(8,128)(2,1)S(1)} %all-to-all-done.3) | copy-start | bytes 4718596
  238.5 18.0 %all-to-all-start.4 = ((f32[16,32,128]{2,1,0:T(8,128)}), f32[16,32,128]{2,1,0:T(8,128)}, u32[]{:S(2)}, u32[]{:S(2)}) async-start(f32[16,32,128]{2,1,0:T(8,128)} %bitcast.71), calls=%async_computation.4 | async-start | bytes 524288 | tf_op jit(solution)/shard_map/all_to_all | solution.py:131
  248.5 3.6 %copy-start.9 = (pred[32,6]{1,0:T(8,128)(4,1)S(1)}, pred[32,6]{1,0:T(8,128)(4,1)}, u32[]{:S(2)}) copy-start(pred[32,6]{1,0:T(8,128)(4,1)} %copy.32) | copy-start | bytes 580
  250.7 5.8 %copy-start.3 = (bf16[32,2048]{1,0:T(8,128)(2,1)S(1)}, bf16[32,2048]{1,0:T(8,128)(2,1)}, u32[]{:S(2)}) copy-start(bf16[32,2048]{1,0:T(8,128)(2,1)} %copy-done.2) | copy-start | bytes 393220
  250.7 6.9 %copy-start.12 = (f32[2048]{0:T(1024)S(1)}, f32[2048]{0:T(1024)}, u32[]{:S(2)}) copy-start(f32[2048]{0:T(1024)} %param.23) | copy-start | bytes 24580
Sparse Core Ops, SparseCore 0:
  67.9 39.7 all-gather.5
  109.8 59.8 all-gather.3
  171.8 42.1 all-gather.7

commit v5 on v4

--- a/solution.py
+++ b/solution.py
@@ -115,8 +115,9 @@
     returned = lax.all_to_all(result, "expert", split_axis=0, concat_axis=0, tiled=True)
     shared_units = shared_gate_up.shape[2]
     shared_pair = shared_gate_up.reshape(width, 2 * shared_units)
+    normed_shared = normed + (gate_up_full[0, 0] * 0 + outgoing[0, 0, 0] * 0).astype(normed.dtype)
     both = jnp.dot(
-        lax.all_gather(normed, "dp", axis=0, tiled=True),
+        lax.all_gather(normed_shared, "dp", axis=0, tiled=True),
         shared_pair,
         preferred_element_type=jnp.float32,
     )

time: 267 us -> 253 us (0.948)
  waiting for transfers between devices: 125 us -> 99.6 us
  other arithmetic: 13 us -> 19 us
  blocking collectives: 49.9 us -> 44.2 us
  local copies, waits for them, and re-layouts: 17.1 us -> 22.1 us
  starting transfers between devices: 29.5 us -> 33 us
    all_gather x1, waiting for transfers between devices: 35.3 us -> 2.96 us  [turned_gather(): out = lax.all_gather(both, axis, axis=0, tiled=True)]
    all_to_all x1, waiting for transfers between devices: 20.7 us -> 35.8 us  [per_device(): lax.all_to_all(result, 'expert', split_axis=0, concat_axis=0, tiled=True)]
    all_gather x1, waiting for transfers between devices: 17.9 us -> 2.78 us  [per_device(): lax.all_gather(shared_hidden, 'dp', axis=1, tiled=True)]
    all_to_all x1 -> x0, blocking collectives: 12 us -> none  [per_device(): lax.all_to_all(proj_cols, 'dp', split_axis=0, concat_axis=1, tiled=True)]
    all_to_all x0 -> x1, waiting for transfers between devices: none -> 9.8 us  [per_device(): lax.all_to_all(proj_cols, 'dp', split_axis=0, concat_axis=1, tiled=True)]
    all_to_all x1, waiting for transfers between devices: 21.9 us -> 13.3 us  [per_device(): lax.all_to_all(outgoing, 'expert', split_axis=0, concat_axis=0, tiled=True)]
    all_gather x1, waiting for transfers between devices: 24.4 us -> 32.2 us  [per_device(): lax.all_gather(normed_shared, 'dp', axis=0, tiled=True)]
    all_to_all x1, blocking collectives: 37.9 us -> 44.2 us  [pair_collect(): lax.all_to_all(copies, axis, 0, 0, tiled=True, axis_index_groups=core_gro...]
  transfers between devices with their start and end apart: 7 -> 8, of which waited for: 7 -> 7; matrix products, arithmetic and copies ran while one was open for 15% -> 20% of each run, Pallas kernels for 0% -> 0%
where the time goes in v5:
time: 253 us; the launch traced here: 251 us
  waiting for transfers between devices  99.6 us (39%)
  blocking collectives  44.2 us (17%)
  starting transfers between devices  33 us (13%)
  local copies, waits for them, and re-layouts  22.1 us (9%)
  other arithmetic  19 us (8%)
  matrix products  18.5 us (7%)
  between operations  14.8 us (6%)
    all_to_all x1, blocking collectives, pair_collect(): lax.all_to_all(copies, axis, 0, 0, tiled=True, axis_index_groups=core_gro...  44.2 us
    all_to_all x1, waiting for transfers between devices, per_device(): lax.all_to_all(result, 'expert', split_axis=0, concat_axis=0, tiled=True)  35.8 us
    all_gather x1, waiting for transfers between devices, per_device(): lax.all_gather(normed_shared, 'dp', axis=0, tiled=True)  32.2 us
    all_to_all x1, waiting for transfers between devices, per_device(): lax.all_to_all(outgoing, 'expert', split_axis=0, concat_axis=0, tiled=True)  13.3 us
    all_to_all x1, waiting for transfers between devices, per_device(): lax.all_to_all(proj_cols, 'dp', split_axis=0, concat_axis=1, tiled=True)  9.8 us
    all_to_all x1, starting transfers between devices, per_device(): lax.all_to_all(outgoing, 'expert', split_axis=0, concat_axis=0, tiled=True)  9.68 us
    all_to_all x1, starting transfers between devices, per_device(): lax.all_to_all(result, 'expert', split_axis=0, concat_axis=0, tiled=True)  7.55 us
    all_to_all x1, starting transfers between devices, per_device(): lax.all_to_all(out_cols, 'dp', split_axis=0, concat_axis=1, tiled=True)  6.69 us
  transfers between devices with their start and end apart: 8, of which 7 were waited for; matrix products, arithmetic and copies ran while one was open for 20% of the time, Pallas kernels for 0%

profile of v5, /device:TPU:1, one launch (start us, length us, event | category | flops | bytes accessed | tf_op | source)
XLA Modules:
  0.0 251.3 jit_solution(14357433639363780460)
XLA Ops:
  7.7 1.9 pad_maximum_fusion.1
  9.8 44.2 %all_to_all.47 = bf16[8,32,2048]{2,1,0:T(8,128)(2,1)S(1)} all-to-all(bf16[8,32,2048]{2,1,0:T(8,128)(2,1)S(1)} %broadcast_in_dim.50), channel_id=1, replica_groups={{0,64,128,192,256,320,384,448},{32,96,160,224,288,352,416,480},{1,65,12..., dimensions={0} | all-to-all | bytes 2097152 | tf_op jit(solution)/shard_map/all_to_all | solution.py:23
  54.0 5.5 %collective-permute-start = (bf16[8,32,2048]{2,1,0:T(8,128)(2,1)S(1)}, bf16[8,32,2048]{2,1,0:T(8,128)(2,1)S(1)}, u32[]{:S(2)}, u32[]{:S(2)}) collective-permute-start(bf16[8,32,2048]{2,1,0:T(8,128)(2,1)S(1)} %all_to_all.47), channel_id=1, source_target_pairs={{0,32},{32,0},{64,96},{96,64},{128,160},{160,128},{192,224},{224,1... | collective-permute-start | bytes 3145736 | tf_op jit(solution)/shard_map/ppermute | solution.py:15
  63.2 1.9 reduce-window.6
  66.9 1.3 fusion.15
  70.9 1.4 convolution_convert_fusion.1
  72.3 3.4 %all-to-all-start.1 = ((bf16[16,32,128]{2,1,0:T(8,128)(2,1)}), bf16[16,32,128]{2,1,0:T(8,128)(2,1)S(1)}, u32[]{:S(2)}, u32[]{:S(2)}) async-start(bf16[16,32,128]{2,1,0:T(8,128)(2,1)} %bitcast.4), calls=%async_computation.1 | async-start | bytes 262144 | tf_op jit(solution)/shard_map/all_to_all | solution.py:86
  76.4 9.8 %all-to-all-done.1 = bf16[16,32,128]{2,1,0:T(8,128)(2,1)S(1)} async-done(((bf16[16,32,128]{2,1,0:T(8,128)(2,1)}), bf16[16,32,128]{2,1,0:T(8,128)(2,1)S(1)}, u32[]{:S(2)}, u32[]{:S(2)}) %all-to-all-start.1) | async-done | bytes 131104 | tf_op jit(solution)/shard_map/all_to_all | solution.py:86
  87.1 1.6 reshape.147
  90.5 3.0 %all-gather.4.cloned.1.call-done = bf16[2048,2112]{1,0:T(8,128)(2,1)} async-done(((bf16[128,2112]{1,0:T(8,128)(2,1)}), bf16[2048,2112]{1,0:T(8,128)(2,1)}) %all-gather.4.cloned.1.call-update) | async-done | bytes 8650768 | tf_op jit(solution)/shard_map/all_gather | solution.py:48
  93.5 1.3 slice.43
  96.3 9.7 %all-to-all-start.2 = ((bf16[32,12,2048]{2,1,0:T(8,128)(2,1)}), bf16[32,12,2048]{2,1,0:T(8,128)(2,1)S(1)}, u32[]{:S(2)}, u32[]{:S(2)}) async-start(bf16[32,12,2048]{2,1,0:T(8,128)(2,1)} %reshape.147), calls=%async_computation.2 | async-start | bytes 4194304 | tf_op jit(solution)/shard_map/all_to_all | solution.py:108
  106.0 32.2 %all-gather.6.cloned.1.call-done = bf16[512,2048]{1,0:T(8,128)(2,1)} async-done(((bf16[32,2048]{1,0:T(8,128)(2,1)}), bf16[512,2048]{1,0:T(8,128)(2,1)}) %all-gather.6.cloned.1.call-update) | async-done | bytes 2097168 | tf_op jit(solution)/shard_map/all_gather | solution.py:120
  138.2 2.5 %fusion.23 = f32[512,352]{0,1:T(8,128)S(1)} fusion(bf16[512,2048]{1,0:T(8,128)(2,1)} %all-gather.6.cloned.1.call-done, bf16[2048,352]{0,1:T(8,128)(2,1)S(1)} %bitcast.67), kind=kOutput, calls=%fused_computation.57 | convolution fusion | flops 738197504 | bytes 4259840 | tf_op jit(solution)/shard_map/dot_general | solution.py:119
  141.5 13.3 %all-to-all-done.2 = bf16[32,12,2048]{2,1,0:T(8,128)(2,1)S(1)} async-done(((bf16[32,12,2048]{2,1,0:T(8,128)(2,1)}), bf16[32,12,2048]{2,1,0:T(8,128)(2,1)S(1)}, u32[]{:S(2)}, u32[]{:S(2)}) %all-to-all-start.2) | async-done | bytes 1572896 | tf_op jit(solution)/shard_map/all_to_all | solution.py:108
  154.8 1.4 reshape.148
  156.3 5.7 %fusion = f32[384,1408]{1,0:T(8,128)S(1)} fusion(bf16[384,2048]{1,0:T(8,128)(2,1)} %reshape.148, bf16[2048,2112]{1,0:T(8,128)(2,1)} %all-gather.4.cloned.1.call-done), kind=kOutput, calls=%fused_computation.1 | convolution fusion | flops 2214592512 | bytes 9502720 | tf_op jit(solution)/shard_map/dot_general | solution.py:111
  162.0 3.4 %fusion.3 = bf16[384,2048]{1,0:T(8,128)(2,1)S(1)} fusion(bf16[2048,2112]{1,0:T(8,128)(2,1)} %all-gather.4.cloned.1.call-done, f32[384,1408]{1,0:T(8,128)S(1)} %fusion), kind=kOutput, calls=%fused_computation.6 | convolution fusion | flops 1109704704 | bytes 7077888 | tf_op jit(solution)/shard_map/dot_general | solution.py:113
  165.4 1.6 reshape.151
  167.0 7.6 %all-to-all-start.3 = ((bf16[32,12,2048]{2,1,0:T(8,128)(2,1)}), bf16[32,12,2048]{2,1,0:T(8,128)(2,1)S(1)}, u32[]{:S(2)}, u32[]{:S(2)}) async-start(bf16[32,12,2048]{2,1,0:T(8,128)(2,1)} %reshape.151), calls=%async_computation.3 | async-start | bytes 4194304 | tf_op jit(solution)/shard_map/all_to_all | solution.py:115
  176.5 1.3 copy.32
  179.1 1.2 fusion.19
  181.1 2.8 %all-gather.8.cloned.1.call-done = bf16[512,2816]{0,1:T(8,128)(2,1)} async-done(((bf16[512,176]{0,1:T(8,128)(2,1)}), bf16[512,2816]{0,1:T(8,128)(2,1)}) %all-gather.8.cloned.1.call-update) | async-done | bytes 2883600 | tf_op jit(solution)/shard_map/all_gather | solution.py:128
  183.9 3.6 %fusion.24 = f32[512,128]{1,0:T(8,128)} fusion(bf16[512,2816]{0,1:T(8,128)(2,1)} %all-gather.8.cloned.1.call-done, bf16[2816,128]{1,0:T(8,128)(2,1)} %param.22), kind=kOutput, calls=%fused_computation.58 | convolution fusion | flops 369098752 | bytes 3866624 | tf_op jit(solution)/shard_map/dot_general | solution.py:127
  187.6 35.8 %all-to-all-done.3 = bf16[32,12,2048]{2,1,0:T(8,128)(2,1)S(1)} async-done(((bf16[32,12,2048]{2,1,0:T(8,128)(2,1)}), bf16[32,12,2048]{2,1,0:T(8,128)(2,1)S(1)}, u32[]{:S(2)}, u32[]{:S(2)}) %all-to-all-start.3) | async-done | bytes 1572896 | tf_op jit(solution)/shard_map/all_to_all | solution.py:115
  223.4 6.7 %all-to-all-start.4 = ((f32[16,32,128]{2,1,0:T(8,128)}), f32[16,32,128]{2,1,0:T(8,128)}, u32[]{:S(2)}, u32[]{:S(2)}) async-start(f32[16,32,128]{2,1,0:T(8,128)} %bitcast.71), calls=%async_computation.4 | async-start | bytes 524288 | tf_op jit(solution)/shard_map/all_to_all | solution.py:132
  231.5 2.5 reshape.152
  234.0 2.2 gather_fusion
  236.2 1.4 gather.7
  237.6 1.7 multiply_reduce_fusion
  239.3 2.6 %all-to-all-done.4 = f32[16,32,128]{2,1,0:T(8,128)} async-done(((f32[16,32,128]{2,1,0:T(8,128)}), f32[16,32,128]{2,1,0:T(8,128)}, u32[]{:S(2)}, u32[]{:S(2)}) %all-to-all-start.4) | async-done | bytes 262176 | tf_op jit(solution)/shard_map/all_to_all | solution.py:132
  243.0 1.7 multiply_convert_fusion
  (71 shorter events, 20.3 us)
Async XLA Ops:
  6.5 131.6 %copy-start = (bf16[2048,2,176]{0,2,1:T(8,128)(2,1)S(1)}, bf16[2048,2,176]{0,2,1:T(8,128)(2,1)}, u32[]{:S(2)}) copy-start(bf16[2048,2,176]{0,2,1:T(8,128)(2,1)} %param.21) | copy-start | bytes 4325380
  6.5 3.1 %copy-start.5 = (bf16[32,2048]{1,0:T(8,128)(2,1)S(1)}, bf16[32,2048]{1,0:T(8,128)(2,1)}, u32[]{:S(2)}) copy-start(bf16[32,2048]{1,0:T(8,128)(2,1)} %param.13) | copy-start | bytes 393220
  6.5 86.9 %all-gather.4.cloned.1.call-start = ((), (), s32[]{:S(2)}) async-start(), calls=%async_computation.5 | async-start | bytes 9469952 | tf_op jit(solution)/shard_map/all_gather | solution.py:48
  9.6 50.0 %copy-start.11 = (s32[32,6]{0,1:T(8,128)S(1)}, s32[32,6]{0,1:T(8,128)}, u32[]{:S(2)}) copy-start(s32[32,6]{0,1:T(8,128)} %param.17) | copy-start | bytes 2308
  9.6 50.0 %copy-start.14 = (s32[32]{0:T(128)S(1)}, s32[32]{0:T(128)}, u32[]{:S(2)}) copy-start(s32[32]{0:T(128)} %param.18) | copy-start | bytes 388
  54.0 15.6 %collective-permute-start = (bf16[8,32,2048]{2,1,0:T(8,128)(2,1)S(1)}, bf16[8,32,2048]{2,1,0:T(8,128)(2,1)S(1)}, u32[]{:S(2)}, u32[]{:S(2)}) collective-permute-start(bf16[8,32,2048]{2,1,0:T(8,128)(2,1)S(1)} %all_to_all.47), channel_id=1, source_target_pairs={{0,32},{32,0},{64,96},{96,64},{128,160},{160,128},{192,224},{224,1... | collective-permute-start | bytes 3145736 | tf_op jit(solution)/shard_map/ppermute | solution.py:15
  69.8 1.1 copy-start.4
  70.4 5.3 %copy-start.7 = (s32[32,6]{0,1:T(8,128)S(1)}, s32[32,6]{0,1:T(8,128)}, u32[]{:S(2)}) copy-start(s32[32,6]{0,1:T(8,128)} %select_reduce_fusion) | copy-start | bytes 2308
  70.4 5.3 %copy-start.10 = (s32[32,6]{0,1:T(8,128)S(1)}, s32[32,6]{0,1:T(8,128)}, u32[]{:S(2)}) copy-start(s32[32,6]{0,1:T(8,128)} %copy.31) | copy-start | bytes 2308
  70.4 15.8 %copy-start.6 = (bf16[32,2048]{1,0:T(8,128)(2,1)S(1)}, bf16[32,2048]{1,0:T(8,128)(2,1)}, u32[]{:S(2)}) copy-start(bf16[32,2048]{1,0:T(8,128)(2,1)} %param.12) | copy-start | bytes 393220
  70.4 16.0 %copy-start.8 = (f32[2048]{0:T(1024)S(1)}, f32[2048]{0:T(1024)}, u32[]{:S(2)}) copy-start(f32[2048]{0:T(1024)} %param.15) | copy-start | bytes 24580
  72.3 13.9 %all-to-all-start.1 = ((bf16[16,32,128]{2,1,0:T(8,128)(2,1)}), bf16[16,32,128]{2,1,0:T(8,128)(2,1)S(1)}, u32[]{:S(2)}, u32[]{:S(2)}) async-start(bf16[16,32,128]{2,1,0:T(8,128)(2,1)} %bitcast.4), calls=%async_computation.1 | async-start | bytes 262144 | tf_op jit(solution)/shard_map/all_to_all | solution.py:86
  75.7 62.5 %all-gather.6.cloned.1.call-start = ((), (), s32[]{:S(2)}) async-start(), calls=%async_computation.6 | async-start | bytes 2228224 | tf_op jit(solution)/shard_map/all_gather | solution.py:120
  86.4 9.1 %copy-start.2 = (bf16[32,2048]{1,0:T(8,128)(2,1)}, bf16[32,2048]{1,0:T(8,128)(2,1)S(1)}, u32[]{:S(2)}) copy-start(bf16[32,2048]{1,0:T(8,128)(2,1)S(1)} %get-tuple-element.8) | copy-start | bytes 393220
  86.4 9.1 %copy-start.13 = (f32[32]{0:T(128)}, f32[32]{0:T(128)S(1)}, u32[]{:S(2)}) copy-start(f32[32]{0:T(128)S(1)} %add_rsqrt_fusion.1) | copy-start | bytes 388
  96.3 58.6 %all-to-all-start.2 = ((bf16[32,12,2048]{2,1,0:T(8,128)(2,1)}), bf16[32,12,2048]{2,1,0:T(8,128)(2,1)S(1)}, u32[]{:S(2)}, u32[]{:S(2)}) async-start(bf16[32,12,2048]{2,1,0:T(8,128)(2,1)} %reshape.147), calls=%async_computation.2 | async-start | bytes 4194304 | tf_op jit(solution)/shard_map/all_to_all | solution.py:108
  105.9 78.0 %all-gather.8.cloned.1.call-start = ((), (), s32[]{:S(2)}) async-start(), calls=%async_computation.7 | async-start | bytes 3063808 | tf_op jit(solution)/shard_map/all_gather | solution.py:128
  167.0 56.5 %all-to-all-start.3 = ((bf16[32,12,2048]{2,1,0:T(8,128)(2,1)}), bf16[32,12,2048]{2,1,0:T(8,128)(2,1)S(1)}, u32[]{:S(2)}, u32[]{:S(2)}) async-start(bf16[32,12,2048]{2,1,0:T(8,128)(2,1)} %reshape.151), calls=%async_computation.3 | async-start | bytes 4194304 | tf_op jit(solution)/shard_map/all_to_all | solution.py:115
  223.4 7.3 %copy-start.1 = (bf16[32,12,2048]{2,1,0:T(8,128)(2,1)}, bf16[32,12,2048]{2,1,0:T(8,128)(2,1)S(1)}, u32[]{:S(2)}) copy-start(bf16[32,12,2048]{2,1,0:T(8,128)(2,1)S(1)} %all-to-all-done.3) | copy-start | bytes 4718596
  223.4 18.5 %all-to-all-start.4 = ((f32[16,32,128]{2,1,0:T(8,128)}), f32[16,32,128]{2,1,0:T(8,128)}, u32[]{:S(2)}, u32[]{:S(2)}) async-start(f32[16,32,128]{2,1,0:T(8,128)} %bitcast.71), calls=%async_computation.4 | async-start | bytes 524288 | tf_op jit(solution)/shard_map/all_to_all | solution.py:132
  234.0 3.6 %copy-start.9 = (pred[32,6]{1,0:T(8,128)(4,1)S(1)}, pred[32,6]{1,0:T(8,128)(4,1)}, u32[]{:S(2)}) copy-start(pred[32,6]{1,0:T(8,128)(4,1)} %copy.32) | copy-start | bytes 580
  236.2 5.8 %copy-start.3 = (bf16[32,2048]{1,0:T(8,128)(2,1)S(1)}, bf16[32,2048]{1,0:T(8,128)(2,1)}, u32[]{:S(2)}) copy-start(bf16[32,2048]{1,0:T(8,128)(2,1)} %copy-done.2) | copy-start | bytes 393220
  236.2 6.9 %copy-start.12 = (f32[2048]{0:T(1024)S(1)}, f32[2048]{0:T(1024)}, u32[]{:S(2)}) copy-start(f32[2048]{0:T(1024)} %param.23) | copy-start | bytes 24580
Sparse Core Ops, SparseCore 0:
  9.7 83.6 all-gather.3
  96.4 41.7 all-gather.5
  141.6 42.2 all-gather.7

commit v6 on v5

--- a/solution.py
+++ b/solution.py
@@ -130,9 +130,15 @@
         preferred_element_type=jnp.float32,
     )
     shared_out = lax.all_to_all(out_cols, "dp", split_axis=0, concat_axis=1, tiled=True)
-    back_rows = jnp.take(returned.reshape(experts * capacity, width), target, axis=0)
-    back_rows = back_rows.reshape(rows, choose, width).astype(jnp.float32)
-    routed = jnp.sum(gates[:, :, None] * back_rows, axis=1)
+    weighted = jnp.sum(
+        placed.reshape(rows, choose, experts * capacity) * gates[:, :, None], axis=1
+    )
+    routed = jnp.dot(
+        weighted,
+        returned.reshape(experts * capacity, width).astype(jnp.float32),
+        precision=lax.Precision.HIGHEST,
+        preferred_element_type=jnp.float32,
+    )
     total = resid.astype(jnp.float32) + routed + shared_out
     return rms_scale(total, final_gain).astype(jnp.bfloat16)
 

time: 253 us -> 253 us (level)
  waiting for transfers between devices: 99.6 us -> 111 us
  local copies, waits for them, and re-layouts: 22.1 us -> 14 us
  other arithmetic: 19 us -> 13 us
  matrix products: 18.5 us -> 21.5 us
    all_to_all x1, waiting for transfers between devices: 2.63 us -> 8.8 us  [per_device(): lax.all_to_all(out_cols, 'dp', split_axis=0, concat_axis=1, tiled=True)]
    all_gather x1, waiting for transfers between devices: 2.78 us -> 7.59 us  [per_device(): lax.all_gather(shared_hidden, 'dp', axis=1, tiled=True)]
    gather x2 -> x0, local copies, waits for them, and re-layouts: 3.55 us -> none  [per_device(): jnp.take(returned.reshape(experts * capacity, width), target, axis=0)]
  transfers between devices with their start and end apart: 8 -> 8, of which waited for: 7 -> 7; matrix products, arithmetic and copies ran while one was open for 20% -> 16% of each run, Pallas kernels for 0% -> 0%
where the time goes in v6:
time: 253 us; the launch traced here: 252 us
  waiting for transfers between devices  111 us (44%)
  blocking collectives  44.2 us (17%)
  starting transfers between devices  33 us (13%)
  matrix products  21.5 us (8%)
  between operations  14.7 us (6%)
  local copies, waits for them, and re-layouts  14 us (6%)
  other arithmetic  13 us (5%)
    all_to_all x1, blocking collectives, pair_collect(): lax.all_to_all(copies, axis, 0, 0, tiled=True, axis_index_groups=core_gro...  44.2 us
    all_to_all x1, waiting for transfers between devices, per_device(): lax.all_to_all(result, 'expert', split_axis=0, concat_axis=0, tiled=True)  35.8 us
    all_gather x1, waiting for transfers between devices, per_device(): lax.all_gather(normed_shared, 'dp', axis=0, tiled=True)  32.2 us
    all_to_all x1, waiting for transfers between devices, per_device(): lax.all_to_all(outgoing, 'expert', split_axis=0, concat_axis=0, tiled=True)  13.3 us
    all_to_all x1, waiting for transfers between devices, per_device(): lax.all_to_all(proj_cols, 'dp', split_axis=0, concat_axis=1, tiled=True)  10.3 us
    all_to_all x1, starting transfers between devices, per_device(): lax.all_to_all(outgoing, 'expert', split_axis=0, concat_axis=0, tiled=True)  9.69 us
    all_to_all x1, waiting for transfers between devices, per_device(): lax.all_to_all(out_cols, 'dp', split_axis=0, concat_axis=1, tiled=True)  8.8 us
    all_gather x1, waiting for transfers between devices, per_device(): lax.all_gather(shared_hidden, 'dp', axis=1, tiled=True)  7.59 us
  transfers between devices with their start and end apart: 8, of which 7 were waited for; matrix products, arithmetic and copies ran while one was open for 16% of the time, Pallas kernels for 0%

profile of v6, /device:TPU:1, one launch (start us, length us, event | category | flops | bytes accessed | tf_op | source)
XLA Modules:
  0.0 251.6 jit_solution(15266959255401992408)
XLA Ops:
  6.5 1.2 copy.38
  7.7 1.9 pad_maximum_fusion.1
  9.8 44.2 %all_to_all.47 = bf16[8,32,2048]{2,1,0:T(8,128)(2,1)S(1)} all-to-all(bf16[8,32,2048]{2,1,0:T(8,128)(2,1)S(1)} %broadcast_in_dim.26), channel_id=1, replica_groups={{0,64,128,192,256,320,384,448},{32,96,160,224,288,352,416,480},{1,65,12..., dimensions={0} | all-to-all | bytes 2097152 | tf_op jit(solution)/shard_map/all_to_all | solution.py:23
  54.0 5.5 %collective-permute-start = (bf16[8,32,2048]{2,1,0:T(8,128)(2,1)S(1)}, bf16[8,32,2048]{2,1,0:T(8,128)(2,1)S(1)}, u32[]{:S(2)}, u32[]{:S(2)}) collective-permute-start(bf16[8,32,2048]{2,1,0:T(8,128)(2,1)S(1)} %all_to_all.47), channel_id=1, source_target_pairs={{0,32},{32,0},{64,96},{96,64},{128,160},{160,128},{192,224},{224,1... | collective-permute-start | bytes 3145736 | tf_op jit(solution)/shard_map/ppermute | solution.py:15
  63.1 1.9 reduce-window.6
  65.0 0.9 slice_reduce_fusion
  66.8 1.2 fusion.15
  70.8 1.4 convolution_convert_fusion.1
  72.2 3.4 %all-to-all-start.1 = ((bf16[16,32,128]{2,1,0:T(8,128)(2,1)}), bf16[16,32,128]{2,1,0:T(8,128)(2,1)S(1)}, u32[]{:S(2)}, u32[]{:S(2)}) async-start(bf16[16,32,128]{2,1,0:T(8,128)(2,1)} %bitcast.4), calls=%async_computation.1 | async-start | bytes 262144 | tf_op jit(solution)/shard_map/all_to_all | solution.py:86
  75.8 10.3 %all-to-all-done.1 = bf16[16,32,128]{2,1,0:T(8,128)(2,1)S(1)} async-done(((bf16[16,32,128]{2,1,0:T(8,128)(2,1)}), bf16[16,32,128]{2,1,0:T(8,128)(2,1)S(1)}, u32[]{:S(2)}, u32[]{:S(2)}) %all-to-all-start.1) | async-done | bytes 131104 | tf_op jit(solution)/shard_map/all_to_all | solution.py:86
  86.9 1.6 reshape.106
  88.6 1.2 slice.42
  90.5 3.0 %all-gather.4.cloned.1.call-done = bf16[2048,2112]{1,0:T(8,128)(2,1)} async-done(((bf16[128,2112]{1,0:T(8,128)(2,1)}), bf16[2048,2112]{1,0:T(8,128)(2,1)}) %all-gather.4.cloned.1.call-update) | async-done | bytes 8650768 | tf_op jit(solution)/shard_map/all_gather | solution.py:48
  93.5 1.2 slice.41
  96.2 9.7 %all-to-all-start.2 = ((bf16[32,12,2048]{2,1,0:T(8,128)(2,1)}), bf16[32,12,2048]{2,1,0:T(8,128)(2,1)S(1)}, u32[]{:S(2)}, u32[]{:S(2)}) async-start(bf16[32,12,2048]{2,1,0:T(8,128)(2,1)} %reshape.106), calls=%async_computation.2 | async-start | bytes 4194304 | tf_op jit(solution)/shard_map/all_to_all | solution.py:108
  105.9 32.2 %all-gather.6.cloned.1.call-done = bf16[512,2048]{1,0:T(8,128)(2,1)} async-done(((bf16[32,2048]{1,0:T(8,128)(2,1)}), bf16[512,2048]{1,0:T(8,128)(2,1)}) %all-gather.6.cloned.1.call-update) | async-done | bytes 2097168 | tf_op jit(solution)/shard_map/all_gather | solution.py:120
  138.1 2.5 %fusion.21 = f32[512,352]{0,1:T(8,128)S(1)} fusion(bf16[512,2048]{1,0:T(8,128)(2,1)} %all-gather.6.cloned.1.call-done, bf16[2048,352]{0,1:T(8,128)(2,1)S(1)} %bitcast.61), kind=kOutput, calls=%fused_computation.51 | convolution fusion | flops 738197504 | bytes 4259840 | tf_op jit(solution)/shard_map/dot_general | solution.py:119
  141.4 13.3 %all-to-all-done.2 = bf16[32,12,2048]{2,1,0:T(8,128)(2,1)S(1)} async-done(((bf16[32,12,2048]{2,1,0:T(8,128)(2,1)}), bf16[32,12,2048]{2,1,0:T(8,128)(2,1)S(1)}, u32[]{:S(2)}, u32[]{:S(2)}) %all-to-all-start.2) | async-done | bytes 1572896 | tf_op jit(solution)/shard_map/all_to_all | solution.py:108
  154.8 1.4 reshape.107
  156.2 5.7 %fusion = f32[384,1408]{1,0:T(8,128)S(1)} fusion(bf16[384,2048]{1,0:T(8,128)(2,1)} %reshape.107, bf16[2048,2112]{1,0:T(8,128)(2,1)} %all-gather.4.cloned.1.call-done), kind=kOutput, calls=%fused_computation | convolution fusion | flops 2214592512 | bytes 9502720 | tf_op jit(solution)/shard_map/dot_general | solution.py:111
  161.9 3.4 %fusion.3 = bf16[384,2048]{1,0:T(8,128)(2,1)S(1)} fusion(bf16[2048,2112]{1,0:T(8,128)(2,1)} %all-gather.4.cloned.1.call-done, f32[384,1408]{1,0:T(8,128)S(1)} %fusion), kind=kOutput, calls=%fused_computation.5 | convolution fusion | flops 1109704704 | bytes 7077888 | tf_op jit(solution)/shard_map/dot_general | solution.py:113
  165.3 1.6 reshape.110
  166.9 7.6 %all-to-all-start.3 = ((bf16[32,12,2048]{2,1,0:T(8,128)(2,1)}), bf16[32,12,2048]{2,1,0:T(8,128)(2,1)S(1)}, u32[]{:S(2)}, u32[]{:S(2)}) async-start(bf16[32,12,2048]{2,1,0:T(8,128)(2,1)} %reshape.110), calls=%async_computation.3 | async-start | bytes 4194304 | tf_op jit(solution)/shard_map/all_to_all | solution.py:115
  174.4 1.8 fusion.18
  176.2 7.6 %all-gather.8.cloned.1.call-done = bf16[512,2816]{0,1:T(8,128)(2,1)} async-done(((bf16[512,176]{0,1:T(8,128)(2,1)}), bf16[512,2816]{0,1:T(8,128)(2,1)}) %all-gather.8.cloned.1.call-update) | async-done | bytes 2883600 | tf_op jit(solution)/shard_map/all_gather | solution.py:128
  183.8 3.6 %fusion.22 = f32[512,128]{1,0:T(8,128)} fusion(bf16[512,2816]{0,1:T(8,128)(2,1)} %all-gather.8.cloned.1.call-done, bf16[2816,128]{1,0:T(8,128)(2,1)} %param.22), kind=kOutput, calls=%fused_computation.52 | convolution fusion | flops 369098752 | bytes 3866624 | tf_op jit(solution)/shard_map/dot_general | solution.py:127
  187.5 35.8 %all-to-all-done.3 = bf16[32,12,2048]{2,1,0:T(8,128)(2,1)S(1)} async-done(((bf16[32,12,2048]{2,1,0:T(8,128)(2,1)}), bf16[32,12,2048]{2,1,0:T(8,128)(2,1)S(1)}, u32[]{:S(2)}, u32[]{:S(2)}) %all-to-all-start.3) | async-done | bytes 1572896 | tf_op jit(solution)/shard_map/all_to_all | solution.py:115
  223.3 6.8 %all-to-all-start.4 = ((f32[16,32,128]{2,1,0:T(8,128)}), f32[16,32,128]{2,1,0:T(8,128)}, u32[]{:S(2)}, u32[]{:S(2)}) async-start(f32[16,32,128]{2,1,0:T(8,128)} %bitcast.65), calls=%async_computation.4 | async-start | bytes 524288 | tf_op jit(solution)/shard_map/all_to_all | solution.py:132
  230.0 0.9 select_reduce_fusion.1
  231.7 1.3 reshape.111
  233.0 8.8 %all-to-all-done.4 = f32[16,32,128]{2,1,0:T(8,128)} async-done(((f32[16,32,128]{2,1,0:T(8,128)}), f32[16,32,128]{2,1,0:T(8,128)}, u32[]{:S(2)}, u32[]{:S(2)}) %all-to-all-start.4) | async-done | bytes 262176 | tf_op jit(solution)/shard_map/all_to_all | solution.py:132
  241.8 2.4 multiply_reduce_fusion
  (56 shorter events, 11.3 us)
Async XLA Ops:
  6.5 131.6 %copy-start = (bf16[2048,2,176]{0,2,1:T(8,128)(2,1)S(1)}, bf16[2048,2,176]{0,2,1:T(8,128)(2,1)}, u32[]{:S(2)}) copy-start(bf16[2048,2,176]{0,2,1:T(8,128)(2,1)} %param.21) | copy-start | bytes 4325380
  6.5 3.1 %copy-start.3 = (bf16[32,2048]{1,0:T(8,128)(2,1)S(1)}, bf16[32,2048]{1,0:T(8,128)(2,1)}, u32[]{:S(2)}) copy-start(bf16[32,2048]{1,0:T(8,128)(2,1)} %param.13) | copy-start | bytes 393220
  6.5 86.9 %all-gather.4.cloned.1.call-start = ((), (), s32[]{:S(2)}) async-start(), calls=%async_computation.5 | async-start | bytes 9469952 | tf_op jit(solution)/shard_map/all_gather | solution.py:48
  9.6 50.0 %copy-start.8 = (s32[32,6]{0,1:T(8,128)S(1)}, s32[32,6]{0,1:T(8,128)}, u32[]{:S(2)}) copy-start(s32[32,6]{0,1:T(8,128)} %param.17) | copy-start | bytes 2308
  9.6 50.0 %copy-start.11 = (s32[32]{0:T(128)S(1)}, s32[32]{0:T(128)}, u32[]{:S(2)}) copy-start(s32[32]{0:T(128)} %param.18) | copy-start | bytes 388
  54.0 15.5 %collective-permute-start = (bf16[8,32,2048]{2,1,0:T(8,128)(2,1)S(1)}, bf16[8,32,2048]{2,1,0:T(8,128)(2,1)S(1)}, u32[]{:S(2)}, u32[]{:S(2)}) collective-permute-start(bf16[8,32,2048]{2,1,0:T(8,128)(2,1)S(1)} %all_to_all.47), channel_id=1, source_target_pairs={{0,32},{32,0},{64,96},{96,64},{128,160},{160,128},{192,224},{224,1... | collective-permute-start | bytes 3145736 | tf_op jit(solution)/shard_map/ppermute | solution.py:15
  69.7 1.1 copy-start.2
  70.3 5.3 %copy-start.5 = (s32[32,6]{0,1:T(8,128)S(1)}, s32[32,6]{0,1:T(8,128)}, u32[]{:S(2)}) copy-start(s32[32,6]{0,1:T(8,128)} %select_reduce_fusion.2) | copy-start | bytes 2308
  70.3 5.3 %copy-start.7 = (s32[32,6]{0,1:T(8,128)S(1)}, s32[32,6]{0,1:T(8,128)}, u32[]{:S(2)}) copy-start(s32[32,6]{0,1:T(8,128)} %copy.37) | copy-start | bytes 2308
  70.3 15.8 %copy-start.4 = (bf16[32,2048]{1,0:T(8,128)(2,1)S(1)}, bf16[32,2048]{1,0:T(8,128)(2,1)}, u32[]{:S(2)}) copy-start(bf16[32,2048]{1,0:T(8,128)(2,1)} %param.12) | copy-start | bytes 393220
  70.3 16.0 %copy-start.6 = (f32[2048]{0:T(1024)S(1)}, f32[2048]{0:T(1024)}, u32[]{:S(2)}) copy-start(f32[2048]{0:T(1024)} %param.15) | copy-start | bytes 24580
  72.2 14.0 %all-to-all-start.1 = ((bf16[16,32,128]{2,1,0:T(8,128)(2,1)}), bf16[16,32,128]{2,1,0:T(8,128)(2,1)S(1)}, u32[]{:S(2)}, u32[]{:S(2)}) async-start(bf16[16,32,128]{2,1,0:T(8,128)(2,1)} %bitcast.4), calls=%async_computation.1 | async-start | bytes 262144 | tf_op jit(solution)/shard_map/all_to_all | solution.py:86
  75.6 62.5 %all-gather.6.cloned.1.call-start = ((), (), s32[]{:S(2)}) async-start(), calls=%async_computation.6 | async-start | bytes 2228224 | tf_op jit(solution)/shard_map/all_gather | solution.py:120
  86.3 9.1 %copy-start.1 = (bf16[32,2048]{1,0:T(8,128)(2,1)}, bf16[32,2048]{1,0:T(8,128)(2,1)S(1)}, u32[]{:S(2)}) copy-start(bf16[32,2048]{1,0:T(8,128)(2,1)S(1)} %get-tuple-element.6) | copy-start | bytes 393220
  96.2 58.6 %all-to-all-start.2 = ((bf16[32,12,2048]{2,1,0:T(8,128)(2,1)}), bf16[32,12,2048]{2,1,0:T(8,128)(2,1)S(1)}, u32[]{:S(2)}, u32[]{:S(2)}) async-start(bf16[32,12,2048]{2,1,0:T(8,128)(2,1)} %reshape.106), calls=%async_computation.2 | async-start | bytes 4194304 | tf_op jit(solution)/shard_map/all_to_all | solution.py:108
  105.9 78.0 %all-gather.8.cloned.1.call-start = ((), (), s32[]{:S(2)}) async-start(), calls=%async_computation.7 | async-start | bytes 3063808 | tf_op jit(solution)/shard_map/all_gather | solution.py:128
  166.9 56.4 %all-to-all-start.3 = ((bf16[32,12,2048]{2,1,0:T(8,128)(2,1)}), bf16[32,12,2048]{2,1,0:T(8,128)(2,1)S(1)}, u32[]{:S(2)}, u32[]{:S(2)}) async-start(bf16[32,12,2048]{2,1,0:T(8,128)(2,1)} %reshape.110), calls=%async_computation.3 | async-start | bytes 4194304 | tf_op jit(solution)/shard_map/all_to_all | solution.py:115
  176.2 53.8 %copy-start.9 = (s32[32,6]{0,1:T(8,128)S(1)}, s32[32,6]{0,1:T(8,128)}, u32[]{:S(2)}) copy-start(s32[32,6]{0,1:T(8,128)} %param.17) | copy-start | bytes 2308
  223.3 18.6 %all-to-all-start.4 = ((f32[16,32,128]{2,1,0:T(8,128)}), f32[16,32,128]{2,1,0:T(8,128)}, u32[]{:S(2)}, u32[]{:S(2)}) async-start(f32[16,32,128]{2,1,0:T(8,128)} %bitcast.65), calls=%async_computation.4 | async-start | bytes 524288 | tf_op jit(solution)/shard_map/all_to_all | solution.py:132
  231.7 12.6 %copy-start.10 = (f32[2048]{0:T(1024)S(1)}, f32[2048]{0:T(1024)}, u32[]{:S(2)}) copy-start(f32[2048]{0:T(1024)} %param.23) | copy-start | bytes 24580
Sparse Core Ops, SparseCore 0:
  9.8 83.6 all-gather.3
  96.3 41.7 all-gather.5
  141.5 42.2 all-gather.7

commit v7 on v6

--- a/solution.py
+++ b/solution.py
@@ -129,7 +129,9 @@
         shared_down,
         preferred_element_type=jnp.float32,
     )
-    shared_out = lax.all_to_all(out_cols, "dp", split_axis=0, concat_axis=1, tiled=True)
+    shared_out = lax.all_to_all(
+        out_cols.astype(jnp.bfloat16), "dp", split_axis=0, concat_axis=1, tiled=True
+    ).astype(jnp.float32)
     weighted = jnp.sum(
         placed.reshape(rows, choose, experts * capacity) * gates[:, :, None], axis=1
     )

time: 253 us -> 250 us (0.988)
  transfers between devices with their start and end apart: 8 -> 8, of which waited for: 7 -> 7; matrix products, arithmetic and copies ran while one was open for 16% -> 15% of each run, Pallas kernels for 0% -> 0%
where the time goes in v7:
time: 250 us; the launch traced here: 249 us
  waiting for transfers between devices  110 us (44%)
  blocking collectives  44.2 us (18%)
  starting transfers between devices  33.1 us (13%)
  matrix products  20.8 us (8%)
  between operations  14.6 us (6%)
  local copies, waits for them, and re-layouts  14 us (6%)
  other arithmetic  12.3 us (5%)
    all_to_all x1, blocking collectives, pair_collect(): lax.all_to_all(copies, axis, 0, 0, tiled=True, axis_index_groups=core_gro...  44.2 us
    all_to_all x1, waiting for transfers between devices, per_device(): lax.all_to_all(result, 'expert', split_axis=0, concat_axis=0, tiled=True)  36 us
    all_gather x1, waiting for transfers between devices, per_device(): lax.all_gather(normed_shared, 'dp', axis=0, tiled=True)  32.2 us
    all_to_all x1, waiting for transfers between devices, per_device(): lax.all_to_all(outgoing, 'expert', split_axis=0, concat_axis=0, tiled=True)  13.3 us
    all_to_all x1, waiting for transfers between devices, per_device(): lax.all_to_all(proj_cols, 'dp', split_axis=0, concat_axis=1, tiled=True)  10.3 us
    all_to_all x1, starting transfers between devices, per_device(): lax.all_to_all(outgoing, 'expert', split_axis=0, concat_axis=0, tiled=True)  9.68 us
    all_gather x1, waiting for transfers between devices, per_device(): lax.all_gather(shared_hidden, 'dp', axis=1, tiled=True)  7.85 us
    all_to_all x1, starting transfers between devices, per_device(): lax.all_to_all(result, 'expert', split_axis=0, concat_axis=0, tiled=True)  7.69 us
  transfers between devices with their start and end apart: 8, of which 7 were waited for; matrix products, arithmetic and copies ran while one was open for 15% of the time, Pallas kernels for 0%

profile of v7, /device:TPU:1, one launch (start us, length us, event | category | flops | bytes accessed | tf_op | source)
XLA Modules:
  0.0 249.0 jit_solution(4289280454807596238)
XLA Ops:
  6.5 1.2 copy.38
  7.7 1.9 pad_maximum_fusion.1
  9.8 44.2 %all_to_all.41 = bf16[8,32,2048]{2,1,0:T(8,128)(2,1)S(1)} all-to-all(bf16[8,32,2048]{2,1,0:T(8,128)(2,1)S(1)} %broadcast_in_dim.26), channel_id=1, replica_groups={{0,64,128,192,256,320,384,448},{32,96,160,224,288,352,416,480},{1,65,12..., dimensions={0} | all-to-all | bytes 2097152 | tf_op jit(solution)/shard_map/all_to_all | solution.py:23
  54.0 5.5 %collective-permute-start = (bf16[8,32,2048]{2,1,0:T(8,128)(2,1)S(1)}, bf16[8,32,2048]{2,1,0:T(8,128)(2,1)S(1)}, u32[]{:S(2)}, u32[]{:S(2)}) collective-permute-start(bf16[8,32,2048]{2,1,0:T(8,128)(2,1)S(1)} %all_to_all.41), channel_id=1, source_target_pairs={{0,32},{32,0},{64,96},{96,64},{128,160},{160,128},{192,224},{224,1... | collective-permute-start | bytes 3145736 | tf_op jit(solution)/shard_map/ppermute | solution.py:15
  59.6 0.8 select_reduce_fusion.2
  63.2 1.9 reduce-window.6
  65.1 0.9 slice_reduce_fusion
  66.9 1.3 fusion.15
  70.9 1.4 convolution_convert_fusion.1
  72.3 3.4 %all-to-all-start.1 = ((bf16[16,32,128]{2,1,0:T(8,128)(2,1)}), bf16[16,32,128]{2,1,0:T(8,128)(2,1)S(1)}, u32[]{:S(2)}, u32[]{:S(2)}) async-start(bf16[16,32,128]{2,1,0:T(8,128)(2,1)} %bitcast.4), calls=%async_computation.1 | async-start | bytes 262144 | tf_op jit(solution)/shard_map/all_to_all | solution.py:86
  75.9 10.3 %all-to-all-done.1 = bf16[16,32,128]{2,1,0:T(8,128)(2,1)S(1)} async-done(((bf16[16,32,128]{2,1,0:T(8,128)(2,1)}), bf16[16,32,128]{2,1,0:T(8,128)(2,1)S(1)}, u32[]{:S(2)}, u32[]{:S(2)}) %all-to-all-start.1) | async-done | bytes 131104 | tf_op jit(solution)/shard_map/all_to_all | solution.py:86
  87.1 1.6 reshape.108
  88.7 1.2 slice.42
  90.6 2.9 %all-gather.4.cloned.1.call-done = bf16[2048,2112]{1,0:T(8,128)(2,1)} async-done(((bf16[128,2112]{1,0:T(8,128)(2,1)}), bf16[2048,2112]{1,0:T(8,128)(2,1)}) %all-gather.4.cloned.1.call-update) | async-done | bytes 8650768 | tf_op jit(solution)/shard_map/all_gather | solution.py:48
  93.5 1.2 slice.41
  96.0 9.7 %all-to-all-start.2 = ((bf16[32,12,2048]{2,1,0:T(8,128)(2,1)}), bf16[32,12,2048]{2,1,0:T(8,128)(2,1)S(1)}, u32[]{:S(2)}, u32[]{:S(2)}) async-start(bf16[32,12,2048]{2,1,0:T(8,128)(2,1)} %reshape.108), calls=%async_computation.2 | async-start | bytes 4194304 | tf_op jit(solution)/shard_map/all_to_all | solution.py:108
  105.8 32.2 %all-gather.6.cloned.1.call-done = bf16[512,2048]{1,0:T(8,128)(2,1)} async-done(((bf16[32,2048]{1,0:T(8,128)(2,1)}), bf16[512,2048]{1,0:T(8,128)(2,1)}) %all-gather.6.cloned.1.call-update) | async-done | bytes 2097168 | tf_op jit(solution)/shard_map/all_gather | solution.py:120
  138.0 2.5 %fusion.21 = f32[512,352]{0,1:T(8,128)S(1)} fusion(bf16[512,2048]{1,0:T(8,128)(2,1)} %all-gather.6.cloned.1.call-done, bf16[2048,352]{0,1:T(8,128)(2,1)S(1)} %bitcast.61), kind=kOutput, calls=%fused_computation.53 | convolution fusion | flops 738197504 | bytes 4259840 | tf_op jit(solution)/shard_map/dot_general | solution.py:119
  141.3 13.3 %all-to-all-done.2 = bf16[32,12,2048]{2,1,0:T(8,128)(2,1)S(1)} async-done(((bf16[32,12,2048]{2,1,0:T(8,128)(2,1)}), bf16[32,12,2048]{2,1,0:T(8,128)(2,1)S(1)}, u32[]{:S(2)}, u32[]{:S(2)}) %all-to-all-start.2) | async-done | bytes 1572896 | tf_op jit(solution)/shard_map/all_to_all | solution.py:108
  154.6 1.4 reshape.109
  156.1 5.7 %fusion = f32[384,1408]{1,0:T(8,128)S(1)} fusion(bf16[384,2048]{1,0:T(8,128)(2,1)} %reshape.109, bf16[2048,2112]{1,0:T(8,128)(2,1)} %all-gather.4.cloned.1.call-done), kind=kOutput, calls=%fused_computation | convolution fusion | flops 2214592512 | bytes 9502720 | tf_op jit(solution)/shard_map/dot_general | solution.py:111
  161.8 3.4 %fusion.3 = bf16[384,2048]{1,0:T(8,128)(2,1)S(1)} fusion(bf16[2048,2112]{1,0:T(8,128)(2,1)} %all-gather.4.cloned.1.call-done, f32[384,1408]{1,0:T(8,128)S(1)} %fusion), kind=kOutput, calls=%fused_computation.5 | convolution fusion | flops 1109704704 | bytes 7077888 | tf_op jit(solution)/shard_map/dot_general | solution.py:113
  165.2 1.6 reshape.112
  166.7 7.7 %all-to-all-start.3 = ((bf16[32,12,2048]{2,1,0:T(8,128)(2,1)}), bf16[32,12,2048]{2,1,0:T(8,128)(2,1)S(1)}, u32[]{:S(2)}, u32[]{:S(2)}) async-start(bf16[32,12,2048]{2,1,0:T(8,128)(2,1)} %reshape.112), calls=%async_computation.3 | async-start | bytes 4194304 | tf_op jit(solution)/shard_map/all_to_all | solution.py:115
  174.4 1.2 fusion.18
  175.8 7.9 %all-gather.8.cloned.1.call-done = bf16[512,2816]{0,1:T(8,128)(2,1)} async-done(((bf16[512,176]{0,1:T(8,128)(2,1)}), bf16[512,2816]{0,1:T(8,128)(2,1)}) %all-gather.8.cloned.1.call-update) | async-done | bytes 2883600 | tf_op jit(solution)/shard_map/all_gather | solution.py:128
  183.7 3.6 %convolution_convert_fusion.2 = bf16[512,128]{1,0:T(8,128)(2,1)} fusion(bf16[512,2816]{0,1:T(8,128)(2,1)} %all-gather.8.cloned.1.call-done, bf16[2816,128]{1,0:T(8,128)(2,1)} %param.22), kind=kOutput, calls=%fused_computation.13 | convolution fusion | flops 369164288 | bytes 3735552 | tf_op jit(solution)/shard_map/dot_general | solution.py:127
  187.3 36.0 %all-to-all-done.3 = bf16[32,12,2048]{2,1,0:T(8,128)(2,1)S(1)} async-done(((bf16[32,12,2048]{2,1,0:T(8,128)(2,1)}), bf16[32,12,2048]{2,1,0:T(8,128)(2,1)S(1)}, u32[]{:S(2)}, u32[]{:S(2)}) %all-to-all-start.3) | async-done | bytes 1572896 | tf_op jit(solution)/shard_map/all_to_all | solution.py:115
  223.3 6.7 %all-to-all-start.4 = ((bf16[16,32,128]{2,1,0:T(8,128)(2,1)}), bf16[16,32,128]{2,1,0:T(8,128)(2,1)}, u32[]{:S(2)}, u32[]{:S(2)}) async-start(bf16[16,32,128]{2,1,0:T(8,128)(2,1)} %bitcast.65), calls=%async_computation.4 | async-start | bytes 262144 | tf_op jit(solution)/shard_map/all_to_all | solution.py:132
  230.8 1.3 reshape.113
  232.1 7.2 %all-to-all-done.4 = bf16[16,32,128]{2,1,0:T(8,128)(2,1)} async-done(((bf16[16,32,128]{2,1,0:T(8,128)(2,1)}), bf16[16,32,128]{2,1,0:T(8,128)(2,1)}, u32[]{:S(2)}, u32[]{:S(2)}) %all-to-all-start.4) | async-done | bytes 131104 | tf_op jit(solution)/shard_map/all_to_all | solution.py:132
  239.3 2.4 multiply_reduce_fusion
  (58 shorter events, 10.7 us)
Async XLA Ops:
  6.5 131.4 %copy-start = (bf16[2048,2,176]{0,2,1:T(8,128)(2,1)S(1)}, bf16[2048,2,176]{0,2,1:T(8,128)(2,1)}, u32[]{:S(2)}) copy-start(bf16[2048,2,176]{0,2,1:T(8,128)(2,1)} %param.21) | copy-start | bytes 4325380
  6.5 3.1 %copy-start.3 = (bf16[32,2048]{1,0:T(8,128)(2,1)S(1)}, bf16[32,2048]{1,0:T(8,128)(2,1)}, u32[]{:S(2)}) copy-start(bf16[32,2048]{1,0:T(8,128)(2,1)} %param.13) | copy-start | bytes 393220
  6.5 87.0 %all-gather.4.cloned.1.call-start = ((), (), s32[]{:S(2)}) async-start(), calls=%async_computation.5 | async-start | bytes 9469952 | tf_op jit(solution)/shard_map/all_gather | solution.py:48
  9.6 50.0 %copy-start.8 = (s32[32,6]{0,1:T(8,128)S(1)}, s32[32,6]{0,1:T(8,128)}, u32[]{:S(2)}) copy-start(s32[32,6]{0,1:T(8,128)} %param.17) | copy-start | bytes 2308
  9.6 50.0 %copy-start.12 = (s32[32]{0:T(128)S(1)}, s32[32]{0:T(128)}, u32[]{:S(2)}) copy-start(s32[32]{0:T(128)} %param.18) | copy-start | bytes 388
  54.0 15.6 %collective-permute-start = (bf16[8,32,2048]{2,1,0:T(8,128)(2,1)S(1)}, bf16[8,32,2048]{2,1,0:T(8,128)(2,1)S(1)}, u32[]{:S(2)}, u32[]{:S(2)}) collective-permute-start(bf16[8,32,2048]{2,1,0:T(8,128)(2,1)S(1)} %all_to_all.41), channel_id=1, source_target_pairs={{0,32},{32,0},{64,96},{96,64},{128,160},{160,128},{192,224},{224,1... | collective-permute-start | bytes 3145736 | tf_op jit(solution)/shard_map/ppermute | solution.py:15
  69.8 1.1 copy-start.2
  70.4 5.4 %copy-start.5 = (s32[32,6]{0,1:T(8,128)S(1)}, s32[32,6]{0,1:T(8,128)}, u32[]{:S(2)}) copy-start(s32[32,6]{0,1:T(8,128)} %select_reduce_fusion.2) | copy-start | bytes 2308
  70.4 5.4 %copy-start.7 = (s32[32,6]{0,1:T(8,128)S(1)}, s32[32,6]{0,1:T(8,128)}, u32[]{:S(2)}) copy-start(s32[32,6]{0,1:T(8,128)} %copy.37) | copy-start | bytes 2308
  70.4 15.8 %copy-start.4 = (bf16[32,2048]{1,0:T(8,128)(2,1)S(1)}, bf16[32,2048]{1,0:T(8,128)(2,1)}, u32[]{:S(2)}) copy-start(bf16[32,2048]{1,0:T(8,128)(2,1)} %param.12) | copy-start | bytes 393220
  70.5 16.0 %copy-start.6 = (f32[2048]{0:T(1024)S(1)}, f32[2048]{0:T(1024)}, u32[]{:S(2)}) copy-start(f32[2048]{0:T(1024)} %param.15) | copy-start | bytes 24580
  72.3 13.9 %all-to-all-start.1 = ((bf16[16,32,128]{2,1,0:T(8,128)(2,1)}), bf16[16,32,128]{2,1,0:T(8,128)(2,1)S(1)}, u32[]{:S(2)}, u32[]{:S(2)}) async-start(bf16[16,32,128]{2,1,0:T(8,128)(2,1)} %bitcast.4), calls=%async_computation.1 | async-start | bytes 262144 | tf_op jit(solution)/shard_map/all_to_all | solution.py:86
  75.7 62.2 %all-gather.6.cloned.1.call-start = ((), (), s32[]{:S(2)}) async-start(), calls=%async_computation.6 | async-start | bytes 2228224 | tf_op jit(solution)/shard_map/all_gather | solution.py:120
  86.4 8.8 %copy-start.1 = (bf16[32,2048]{1,0:T(8,128)(2,1)}, bf16[32,2048]{1,0:T(8,128)(2,1)S(1)}, u32[]{:S(2)}) copy-start(bf16[32,2048]{1,0:T(8,128)(2,1)S(1)} %get-tuple-element.6) | copy-start | bytes 393220
  86.4 8.8 %copy-start.11 = (f32[32]{0:T(128)}, f32[32]{0:T(128)S(1)}, u32[]{:S(2)}) copy-start(f32[32]{0:T(128)S(1)} %add_rsqrt_fusion.1) | copy-start | bytes 388
  96.0 58.6 %all-to-all-start.2 = ((bf16[32,12,2048]{2,1,0:T(8,128)(2,1)}), bf16[32,12,2048]{2,1,0:T(8,128)(2,1)S(1)}, u32[]{:S(2)}, u32[]{:S(2)}) async-start(bf16[32,12,2048]{2,1,0:T(8,128)(2,1)} %reshape.108), calls=%async_computation.2 | async-start | bytes 4194304 | tf_op jit(solution)/shard_map/all_to_all | solution.py:108
  105.7 78.0 %all-gather.8.cloned.1.call-start = ((), (), s32[]{:S(2)}) async-start(), calls=%async_computation.7 | async-start | bytes 3063808 | tf_op jit(solution)/shard_map/all_gather | solution.py:128
  166.7 8.9 %copy-start.9 = (s32[32,6]{0,1:T(8,128)S(1)}, s32[32,6]{0,1:T(8,128)}, u32[]{:S(2)}) copy-start(s32[32,6]{0,1:T(8,128)} %param.17) | copy-start | bytes 2308
  166.7 56.6 %all-to-all-start.3 = ((bf16[32,12,2048]{2,1,0:T(8,128)(2,1)}), bf16[32,12,2048]{2,1,0:T(8,128)(2,1)S(1)}, u32[]{:S(2)}, u32[]{:S(2)}) async-start(bf16[32,12,2048]{2,1,0:T(8,128)(2,1)} %reshape.112), calls=%async_computation.3 | async-start | bytes 4194304 | tf_op jit(solution)/shard_map/all_to_all | solution.py:115
  223.3 16.0 %all-to-all-start.4 = ((bf16[16,32,128]{2,1,0:T(8,128)(2,1)}), bf16[16,32,128]{2,1,0:T(8,128)(2,1)}, u32[]{:S(2)}, u32[]{:S(2)}) async-start(bf16[16,32,128]{2,1,0:T(8,128)(2,1)} %bitcast.65), calls=%async_computation.4 | async-start | bytes 262144 | tf_op jit(solution)/shard_map/all_to_all | solution.py:132
  230.8 10.9 %copy-start.10 = (f32[2048]{0:T(1024)S(1)}, f32[2048]{0:T(1024)}, u32[]{:S(2)}) copy-start(f32[2048]{0:T(1024)} %param.23) | copy-start | bytes 24580
Sparse Core Ops, SparseCore 0:
  9.8 83.6 all-gather.3
  96.2 41.7 all-gather.5
  141.4 42.2 all-gather.7

commit v8 on v7

--- a/solution.py
+++ b/solution.py
@@ -79,6 +79,8 @@
     width = residual_in.shape[1]
     experts = router_weight.shape[1]
     choose = expert_ids.shape[1]
+    groups = lax.axis_size("dp")
+    me = lax.axis_index("dp")
     capacity = max(2, min(rows, 2 * rows * choose // experts))
     proj_cols = jnp.dot(
         in_order(pair_collect(attention_out, "dp"), 0), out_weight, preferred_element_type=jnp.float32
@@ -101,21 +103,46 @@
     select = jnp.any(placed.reshape(rows, choose, experts * capacity), axis=1).astype(jnp.bfloat16)
     outgoing = jnp.einsum("rs,rd->sd", select, normed, preferred_element_type=jnp.float32)
     outgoing = outgoing.astype(jnp.bfloat16).reshape(experts, capacity, width)
-    gate_up_all, down_all = turned_gather((expert_gate_up, expert_down), "dp", (1, 2))
-    gate_up_full = gate_up_all[0]
-    down_full = down_all[0]
-    hidden_units = gate_up_full.shape[1] // 2
+    hidden_units = expert_down.shape[1]
+    weights_part = jnp.concatenate([expert_gate_up[0], expert_down[0].T], axis=1)
+    own_blocks = lax.all_gather(
+        weights_part, "dp", axis=0, tiled=True, axis_index_groups=core_groups("dp")
+    )
+    core = me % 2
     received = lax.all_to_all(outgoing, "expert", split_axis=0, concat_axis=0, tiled=True)
     sources, count, _ = received.shape
     flat = received.reshape(sources * count, width)
-    both = jnp.dot(flat, gate_up_full, preferred_element_type=jnp.float32)
+    sib_blocks = lax.ppermute(own_blocks, "dp", [(i, i ^ 1) for i in range(groups)])
+    split = flat.reshape(flat.shape[0], groups // 2, 2, -1)
+    own_cols = lax.dynamic_index_in_dim(split, core, axis=2, keepdims=False)
+    sib_cols = lax.dynamic_index_in_dim(split, 1 - core, axis=2, keepdims=False)
+    gate_up_width = 2 * hidden_units
+    both = jnp.dot(
+        own_cols.reshape(flat.shape[0], -1),
+        own_blocks[:, :gate_up_width],
+        preferred_element_type=jnp.float32,
+    ) + jnp.dot(
+        sib_cols.reshape(flat.shape[0], -1),
+        sib_blocks[:, :gate_up_width],
+        preferred_element_type=jnp.float32,
+    )
     active = (jax.nn.silu(both[:, :hidden_units]) * both[:, hidden_units:]).astype(jnp.bfloat16)
-    result = jnp.dot(active, down_full, preferred_element_type=jnp.float32).astype(jnp.bfloat16)
+
+    def down(blocks):
+        part = lax.dot_general(
+            active, blocks[:, gate_up_width:], (((1,), (1,)), ((), ())),
+            preferred_element_type=jnp.float32,
+        ).astype(jnp.bfloat16)
+        return part.reshape(part.shape[0], groups // 2, -1)
+
+    pair = jnp.stack([down(own_blocks), down(sib_blocks)], axis=2)
+    pair = jnp.where(core == 0, pair, jnp.flip(pair, axis=2))
+    result = pair.reshape(pair.shape[0], -1)
     result = result.reshape(sources, count, width)
     returned = lax.all_to_all(result, "expert", split_axis=0, concat_axis=0, tiled=True)
     shared_units = shared_gate_up.shape[2]
     shared_pair = shared_gate_up.reshape(width, 2 * shared_units)
-    normed_shared = normed + (gate_up_full[0, 0] * 0 + outgoing[0, 0, 0] * 0).astype(normed.dtype)
+    normed_shared = normed + (own_blocks[0, 0] * 0 + outgoing[0, 0, 0] * 0).astype(normed.dtype)
     both = jnp.dot(
         lax.all_gather(normed_shared, "dp", axis=0, tiled=True),
         shared_pair,

time: 250 us -> 324 us (1.30)
  local copies, waits for them, and re-layouts: 14 us -> 56.4 us
  other arithmetic: 12.3 us -> 24 us
  waiting for transfers between devices: 110 us -> 120 us
  matrix products: 20.8 us -> 24.9 us
  starting transfers between devices: 33.1 us -> 36.9 us
    all_to_all x1, waiting for transfers between devices: 13.3 us -> 48.9 us  [per_device(): lax.all_to_all(outgoing, 'expert', split_axis=0, concat_axis=0, tiled=True)]
    all_gather x1, waiting for transfers between devices: 32.2 us -> 0.02 us  [per_device(): lax.all_gather(normed_shared, 'dp', axis=0, tiled=True)]
    another operation x1 -> x5, local copies, waits for them, and re-layouts: 0.01 us -> 17 us  [the longest x2 7.72 us: per_device(): pair = jnp.stack([down(own_blocks), down(sib_blocks)], axis=2)]
    rev x0 -> x1, local copies, waits for them, and re-layouts: none -> 14.8 us  [per_device(): pair = jnp.where(core == 0, pair, jnp.flip(pair, axis=2))]
    dynamic_slice x0 -> x3, local copies, waits for them, and re-layouts: none -> 12.6 us  [the longest x2 9.81 us: per_device(): sib_cols = lax.dynamic_index_in_dim(split, 1 - core, axis=2, keepdims=False)]
    all_gather x1, waiting for transfers between devices: 7.85 us -> 0.02 us  [per_device(): lax.all_gather(shared_hidden, 'dp', axis=1, tiled=True)]
    all_gather x1, waiting for transfers between devices: 2.92 us -> 10.5 us  [per_device(): lax.all_gather(weights_part, 'dp', axis=0, tiled=True, axis_index_groups=...]
    all_to_all x1, waiting for transfers between devices: 36 us -> 43.5 us  [per_device(): lax.all_to_all(result, 'expert', split_axis=0, concat_axis=0, tiled=True)]
  transfers between devices with their start and end apart: 8 -> 9, of which waited for: 7 -> 5; matrix products, arithmetic and copies ran while one was open for 15% -> 30% of each run, Pallas kernels for 0% -> 0%
where the time goes in v8:
time: 324 us; the launch traced here: 321 us
  waiting for transfers between devices  120 us (37%)
  local copies, waits for them, and re-layouts  56.4 us (17%)
  blocking collectives  44.1 us (14%)
  starting transfers between devices  36.9 us (11%)
  matrix products  24.9 us (8%)
  other arithmetic  24 us (7%)
  between operations  14.9 us (5%)
    all_to_all x1, waiting for transfers between devices, per_device(): lax.all_to_all(outgoing, 'expert', split_axis=0, concat_axis=0, tiled=True)  48.9 us
    all_to_all x1, blocking collectives, pair_collect(): lax.all_to_all(copies, axis, 0, 0, tiled=True, axis_index_groups=core_gro...  44.1 us
    all_to_all x1, waiting for transfers between devices, per_device(): lax.all_to_all(result, 'expert', split_axis=0, concat_axis=0, tiled=True)  43.5 us
    rev x1, local copies, waits for them, and re-layouts, per_device(): pair = jnp.where(core == 0, pair, jnp.flip(pair, axis=2))  14.8 us
    all_gather x1, waiting for transfers between devices, per_device(): lax.all_gather(weights_part, 'dp', axis=0, tiled=True, axis_index_groups=...  10.5 us
    all_to_all x1, starting transfers between devices, per_device(): lax.all_to_all(outgoing, 'expert', split_axis=0, concat_axis=0, tiled=True)  10 us
    all_to_all x1, waiting for transfers between devices, per_device(): lax.all_to_all(proj_cols, 'dp', split_axis=0, concat_axis=1, tiled=True)  9.84 us
    dynamic_slice x2, local copies, waits for them, and re-layouts, per_device(): sib_cols = lax.dynamic_index_in_dim(split, 1 - core, axis=2, keepdims=False)  9.81 us
  transfers between devices with their start and end apart: 9, of which 5 were waited for; matrix products, arithmetic and copies ran while one was open for 30% of the time, Pallas kernels for 0%

profile of v8, /device:TPU:1, one launch (start us, length us, event | category | flops | bytes accessed | tf_op | source)
XLA Modules:
  0.0 321.2 jit_solution(10281446801346896353)
XLA Ops:
  7.9 1.8 pad_maximum_fusion.2
  9.8 44.1 %all_to_all.41 = bf16[8,32,2048]{2,1,0:T(8,128)(2,1)S(1)} all-to-all(bf16[8,32,2048]{2,1,0:T(8,128)(2,1)S(1)} %broadcast_in_dim.26), channel_id=1, replica_groups={{0,64,128,192,256,320,384,448},{32,96,160,224,288,352,416,480},{1,65,12..., dimensions={0} | all-to-all | bytes 2097152 | tf_op jit(solution)/shard_map/all_to_all | solution.py:23
  53.9 4.0 %collective-permute-start = (bf16[8,32,2048]{2,1,0:T(8,128)(2,1)S(1)}, bf16[8,32,2048]{2,1,0:T(8,128)(2,1)S(1)}, u32[]{:S(2)}, u32[]{:S(2)}) collective-permute-start(bf16[8,32,2048]{2,1,0:T(8,128)(2,1)S(1)} %all_to_all.41), channel_id=1, source_target_pairs={{0,32},{32,0},{64,96},{96,64},{128,160},{160,128},{192,224},{224,1... | collective-permute-start | bytes 3145736 | tf_op jit(solution)/shard_map/ppermute | solution.py:15
  61.4 1.9 reduce-window.6
  70.4 3.4 %all-to-all-start.1 = ((bf16[16,32,128]{2,1,0:T(8,128)(2,1)}), bf16[16,32,128]{2,1,0:T(8,128)(2,1)S(1)}, u32[]{:S(2)}, u32[]{:S(2)}) async-start(bf16[16,32,128]{2,1,0:T(8,128)(2,1)} %bitcast.4), calls=%async_computation.1 | async-start | bytes 262144 | tf_op jit(solution)/shard_map/all_to_all | solution.py:88
  74.0 9.8 %all-to-all-done.1 = bf16[16,32,128]{2,1,0:T(8,128)(2,1)S(1)} async-done(((bf16[16,32,128]{2,1,0:T(8,128)(2,1)}), bf16[16,32,128]{2,1,0:T(8,128)(2,1)S(1)}, u32[]{:S(2)}, u32[]{:S(2)}) %all-to-all-start.1) | async-done | bytes 131104 | tf_op jit(solution)/shard_map/all_to_all | solution.py:88
  84.7 1.6 reshape.104
  88.2 10.5 %all-gather.4.cloned.1.call-done = bf16[1024,2112]{0,1:T(8,128)(2,1)} async-done(((bf16[128,2112]{0,1:T(8,128)(2,1)}), bf16[1024,2112]{0,1:T(8,128)(2,1)}) %all-gather.4.cloned.1.call-update) | async-done | bytes 4325392 | tf_op jit(solution)/shard_map/all_gather | solution.py:108
  101.4 5.1 %collective-permute-start.1 = (bf16[1024,2112]{0,1:T(8,128)(2,1)}, bf16[1024,2112]{0,1:T(8,128)(2,1)}, u32[]{:S(2)}, u32[]{:S(2)}) collective-permute-start(bf16[1024,2112]{0,1:T(8,128)(2,1)} %all-gather.4.cloned.1.call-done), channel_id=1, source_target_pairs={{0,32},{32,0},{64,96},{96,64},{128,160},{160,128},{192,224},{224,1... | collective-permute-start | bytes 12976136 | tf_op jit(solution)/shard_map/ppermute | solution.py:115
  106.5 10.0 %all-to-all-start.2 = ((bf16[32,12,2048]{2,1,0:T(8,128)(2,1)}), bf16[32,12,2048]{2,1,0:T(8,128)(2,1)}, u32[]{:S(2)}, u32[]{:S(2)}) async-start(bf16[32,12,2048]{2,1,0:T(8,128)(2,1)} %reshape.104), calls=%async_computation.2 | async-start | bytes 4194304 | tf_op jit(solution)/shard_map/all_to_all | solution.py:112
  116.8 48.9 %all-to-all-done.2 = bf16[32,12,2048]{2,1,0:T(8,128)(2,1)} async-done(((bf16[32,12,2048]{2,1,0:T(8,128)(2,1)}), bf16[32,12,2048]{2,1,0:T(8,128)(2,1)}, u32[]{:S(2)}, u32[]{:S(2)}) %all-to-all-start.2) | async-done | bytes 1572896 | tf_op jit(solution)/shard_map/all_to_all | solution.py:112
  165.7 4.3 %reshape_reshape.10 = bf16[384,8,2,128]{3,2,1,0:T(2,128)(2,1)S(1)} reshape(bf16[32,12,2048]{2,1,0:T(8,128)(2,1)} %all-to-all-done.2) | data formatting | bytes 3145728 | tf_op jit(solution)/shard_map/reshape;reshape | solution.py:116
  170.0 2.5 fusion.27
  173.4 5.0 %constant_dynamic-slice_fusion.1 = (bf16[384,8,1,128]{3,2,1,0:T(2,128)(2,1)}, bf16[384,8,1,128]{3,2,1,0:T(2,128)(2,1)}) fusion(bf16[384,8,2,128]{3,2,1,0:T(2,128)(2,1)S(1)} %reshape_reshape.10, s32[]{:T(128)S(6)} %select_n.47, s32[]{:T(128)S(6)} %select_n.46), kind=kLoop, calls=%fused_computation.58 | loop fusion | bytes 3145736 | tf_op jit(solution)/shard_map/jit(dynamic_index_in_dim)/dynamic_slice | solution.py:118
  178.4 4.8 %copy.48 = bf16[384,8,1,128]{0,3,1,2:T(8,128)(2,1)} copy(bf16[384,8,1,128]{3,2,1,0:T(2,128)(2,1)} %get-tuple-element.7) | data formatting | bytes 1572864 | tf_op jit(solution)/shard_map/jit(dynamic_index_in_dim)/dynamic_slice | solution.py:118
  183.2 2.8 copy.46
  186.0 3.5 %fusion.1 = f32[384,1408]{1,0:T(8,128)S(1)} fusion(bf16[384,1024]{0,1:T(8,128)(2,1)} %bitcast.63, bf16[1024,2112]{0,1:T(8,128)(2,1)} %all-gather.4.cloned.1.call-done), kind=kOutput, calls=%fused_computation.4 | convolution fusion | flops 1107296256 | bytes 5832704 | tf_op jit(solution)/shard_map/dot_general | solution.py:120
  189.5 3.4 %convolution_add_fusion = f32[384,1408]{1,0:T(8,128)S(1)} fusion(f32[384,1408]{1,0:T(8,128)S(1)} %fusion.1, bf16[384,1024]{0,1:T(8,128)(2,1)S(1)} %bitcast.62, bf16[1024,2112]{0,1:T(8,128)(2,1)} %collective-permute-done.1), kind=kOutput, calls=%fused_computation.2 | convolution fusion | flops 1107836928 | bytes 7995392 | tf_op jit(solution)/shard_map/dot_general | solution.py:124
  194.1 3.0 fusion.8
  197.2 3.2 stack_reshape.8
  200.3 3.3 %fusion.11 = bf16[384,1024]{1,0:T(8,128)(2,1)} fusion(bf16[384,704]{1,0:T(8,128)(2,1)} %copy-done.4, bf16[1024,2112]{0,1:T(8,128)(2,1)} %collective-permute-done.1), kind=kOutput, calls=%fused_computation.16 | convolution fusion | flops 554041344 | bytes 2818048 | tf_op jit(solution)/shard_map/dot_general | solution.py:132
  203.6 4.6 %stack_reshape.9 = bf16[384,8,1,128]{3,2,1,0:T(2,128)(2,1)} reshape(bf16[384,1024]{1,0:T(8,128)(2,1)} %fusion.11) | data formatting | bytes 1572864 | tf_op jit(solution)/shard_map/stack;reshape | solution.py:138
  208.1 5.5 %pad_maximum_fusion.1 = bf16[384,8,2,128]{3,2,1,0:T(2,128)(2,1)} fusion(bf16[384,8,1,128]{3,2,1,0:T(2,128)(2,1)} %stack_reshape.9, bf16[384,8,1,128]{3,2,1,0:T(2,128)(2,1)S(1)} %stack_reshape.8), kind=kLoop, calls=%fused_computation.10 | loop fusion | flops 3145728 | bytes 3145728 | tf_op jit(solution)/shard_map/stack | solution.py:138
  213.6 14.8 %rev.9 = bf16[384,8,2,128]{3,2,1,0:T(2,128)(2,1)} reverse(bf16[384,8,2,128]{3,2,1,0:T(2,128)(2,1)} %pad_maximum_fusion.1), dimensions={2} | reverse | bytes 3145728 | tf_op jit(solution)/shard_map/jit(_flip)/rev | solution.py:139
  228.4 6.1 %broadcast_select_fusion = bf16[384,8,2,128]{3,2,1,0:T(2,128)(2,1)} fusion(bf16[384,8,2,128]{3,2,1,0:T(2,128)(2,1)} %rev.9, pred[]{:T(512)S(6)} %eq.56, bf16[384,8,1,128]{3,2,1,0:T(2,128)(2,1)} %stack_reshape.9, bf16[384,8,1,128]{3,2,1,0:T(2,128)(2,1)S(1)} %stack_reshape.8), kind=kLoop, calls=%fused_computation.1 | loop fusion | flops 3932160 | bytes 4718593 | tf_op jit(solution)/shard_map/jit(_where)/select_n | solution.py:139
  234.6 5.0 %reshape_reshape.11 = bf16[32,12,2048]{2,1,0:T(8,128)(2,1)} reshape(bf16[384,8,2,128]{3,2,1,0:T(2,128)(2,1)} %broadcast_select_fusion) | data formatting | bytes 3145728 | tf_op jit(solution)/shard_map/reshape;reshape | solution.py:141
  239.5 7.7 %all-to-all-start.3 = ((bf16[32,12,2048]{2,1,0:T(8,128)(2,1)}), bf16[32,12,2048]{2,1,0:T(8,128)(2,1)S(1)}, u32[]{:S(2)}, u32[]{:S(2)}) async-start(bf16[32,12,2048]{2,1,0:T(8,128)(2,1)} %reshape_reshape.11), calls=%async_computation.3 | async-start | bytes 4194304 | tf_op jit(solution)/shard_map/all_to_all | solution.py:142
  248.7 3.6 %convolution_convert_fusion.2 = bf16[512,128]{1,0:T(8,128)(2,1)} fusion(bf16[512,2816]{0,1:T(8,128)(2,1)} %all-gather.8.cloned.1.call-done, bf16[2816,128]{1,0:T(8,128)(2,1)} %param.22), kind=kOutput, calls=%fused_computation.20 | convolution fusion | flops 369164288 | bytes 3735552 | tf_op jit(solution)/shard_map/dot_general | solution.py:154
  252.3 43.5 %all-to-all-done.3 = bf16[32,12,2048]{2,1,0:T(8,128)(2,1)S(1)} async-done(((bf16[32,12,2048]{2,1,0:T(8,128)(2,1)}), bf16[32,12,2048]{2,1,0:T(8,128)(2,1)S(1)}, u32[]{:S(2)}, u32[]{:S(2)}) %all-to-all-start.3) | async-done | bytes 1572896 | tf_op jit(solution)/shard_map/all_to_all | solution.py:142
  295.8 6.4 %all-to-all-start.4 = ((bf16[16,32,128]{2,1,0:T(8,128)(2,1)}), bf16[16,32,128]{2,1,0:T(8,128)(2,1)}, u32[]{:S(2)}, u32[]{:S(2)}) async-start(bf16[16,32,128]{2,1,0:T(8,128)(2,1)} %bitcast.64), calls=%async_computation.4 | async-start | bytes 262144 | tf_op jit(solution)/shard_map/all_to_all | solution.py:159
  304.2 7.2 %all-to-all-done.4 = bf16[16,32,128]{2,1,0:T(8,128)(2,1)} async-done(((bf16[16,32,128]{2,1,0:T(8,128)(2,1)}), bf16[16,32,128]{2,1,0:T(8,128)(2,1)}, u32[]{:S(2)}, u32[]{:S(2)}) %all-to-all-start.4) | async-done | bytes 131104 | tf_op jit(solution)/shard_map/all_to_all | solution.py:159
  311.5 2.4 multiply_reduce_fusion
  (77 shorter events, 22.8 us)
Async XLA Ops:
  6.5 163.5 %copy-start = (bf16[2048,2,176]{0,2,1:T(8,128)(2,1)S(1)}, bf16[2048,2,176]{0,2,1:T(8,128)(2,1)}, u32[]{:S(2)}) copy-start(bf16[2048,2,176]{0,2,1:T(8,128)(2,1)} %param.21) | copy-start | bytes 4325380
  6.5 3.1 copy-start.6
  6.5 92.1 %all-gather.4.cloned.1.call-start = ((), (), s32[]{:S(2)}) async-start(), calls=%async_computation.5 | async-start | bytes 4866048 | tf_op jit(solution)/shard_map/all_gather | solution.py:108
  9.7 48.2 %copy-start.11 = (s32[32,6]{0,1:T(8,128)S(1)}, s32[32,6]{0,1:T(8,128)}, u32[]{:S(2)}) copy-start(s32[32,6]{0,1:T(8,128)} %param.17) | copy-start | bytes 2308
  9.7 48.2 %copy-start.15 = (s32[32]{0:T(128)S(1)}, s32[32]{0:T(128)}, u32[]{:S(2)}) copy-start(s32[32]{0:T(128)} %param.18) | copy-start | bytes 388
  53.9 13.9 %collective-permute-start = (bf16[8,32,2048]{2,1,0:T(8,128)(2,1)S(1)}, bf16[8,32,2048]{2,1,0:T(8,128)(2,1)S(1)}, u32[]{:S(2)}, u32[]{:S(2)}) collective-permute-start(bf16[8,32,2048]{2,1,0:T(8,128)(2,1)S(1)} %all_to_all.41), channel_id=1, source_target_pairs={{0,32},{32,0},{64,96},{96,64},{128,160},{160,128},{192,224},{224,1... | collective-permute-start | bytes 3145736 | tf_op jit(solution)/shard_map/ppermute | solution.py:15
  68.0 1.1 copy-start.5
  68.5 5.3 %copy-start.8 = (s32[32,6]{0,1:T(8,128)S(1)}, s32[32,6]{0,1:T(8,128)}, u32[]{:S(2)}) copy-start(s32[32,6]{0,1:T(8,128)} %select_reduce_fusion.2) | copy-start | bytes 2308
  68.5 5.3 %copy-start.10 = (s32[32,6]{0,1:T(8,128)S(1)}, s32[32,6]{0,1:T(8,128)}, u32[]{:S(2)}) copy-start(s32[32,6]{0,1:T(8,128)} %copy.45) | copy-start | bytes 2308
  68.6 15.3 %copy-start.7 = (bf16[32,2048]{1,0:T(8,128)(2,1)S(1)}, bf16[32,2048]{1,0:T(8,128)(2,1)}, u32[]{:S(2)}) copy-start(bf16[32,2048]{1,0:T(8,128)(2,1)} %param.12) | copy-start | bytes 393220
  69.0 15.0 %copy-start.9 = (f32[2048]{0:T(1024)S(1)}, f32[2048]{0:T(1024)}, u32[]{:S(2)}) copy-start(f32[2048]{0:T(1024)} %param.15) | copy-start | bytes 24580
  70.4 13.4 %all-to-all-start.1 = ((bf16[16,32,128]{2,1,0:T(8,128)(2,1)}), bf16[16,32,128]{2,1,0:T(8,128)(2,1)S(1)}, u32[]{:S(2)}, u32[]{:S(2)}) async-start(bf16[16,32,128]{2,1,0:T(8,128)(2,1)} %bitcast.4), calls=%async_computation.1 | async-start | bytes 262144 | tf_op jit(solution)/shard_map/all_to_all | solution.py:88
  73.8 96.2 %all-gather.6.cloned.1.call-start = ((), (), s32[]{:S(2)}) async-start(), calls=%async_computation.6 | async-start | bytes 2228224 | tf_op jit(solution)/shard_map/all_gather | solution.py:147
  84.0 16.6 %copy-start.2 = (bf16[32,2048]{1,0:T(8,128)(2,1)}, bf16[32,2048]{1,0:T(8,128)(2,1)S(1)}, u32[]{:S(2)}) copy-start(bf16[32,2048]{1,0:T(8,128)(2,1)S(1)} %get-tuple-element.6) | copy-start | bytes 393220
  84.0 16.6 %copy-start.14 = (f32[32]{0:T(128)}, f32[32]{0:T(128)S(1)}, u32[]{:S(2)}) copy-start(f32[32]{0:T(128)S(1)} %add_rsqrt_fusion.1) | copy-start | bytes 388
  101.4 88.1 %collective-permute-start.1 = (bf16[1024,2112]{0,1:T(8,128)(2,1)}, bf16[1024,2112]{0,1:T(8,128)(2,1)}, u32[]{:S(2)}, u32[]{:S(2)}) collective-permute-start(bf16[1024,2112]{0,1:T(8,128)(2,1)} %all-gather.4.cloned.1.call-done), channel_id=1, source_target_pairs={{0,32},{32,0},{64,96},{96,64},{128,160},{160,128},{192,224},{224,1... | collective-permute-start | bytes 12976136 | tf_op jit(solution)/shard_map/ppermute | solution.py:115
  106.5 59.2 %all-to-all-start.2 = ((bf16[32,12,2048]{2,1,0:T(8,128)(2,1)}), bf16[32,12,2048]{2,1,0:T(8,128)(2,1)}, u32[]{:S(2)}, u32[]{:S(2)}) async-start(bf16[32,12,2048]{2,1,0:T(8,128)(2,1)} %reshape.104), calls=%async_computation.2 | async-start | bytes 4194304 | tf_op jit(solution)/shard_map/all_to_all | solution.py:112
  116.5 132.1 %all-gather.8.cloned.1.call-start = ((), (), s32[]{:S(2)}) async-start(), calls=%async_computation.7 | async-start | bytes 3063808 | tf_op jit(solution)/shard_map/all_gather | solution.py:155
  178.4 4.8 %copy-start.1 = (bf16[384,8,1,128]{3,2,1,0:T(2,128)(2,1)S(1)}, bf16[384,8,1,128]{3,2,1,0:T(2,128)(2,1)}, u32[]{:S(2)}) copy-start(bf16[384,8,1,128]{3,2,1,0:T(2,128)(2,1)} %get-tuple-element.8) | copy-start | bytes 2359300
  186.0 3.6 %copy-start.3 = (bf16[384,8,1,128]{0,3,1,2:T(8,128)(2,1)S(1)}, bf16[384,8,1,128]{0,3,1,2:T(8,128)(2,1)}, u32[]{:S(2)}) copy-start(bf16[384,8,1,128]{0,3,1,2:T(8,128)(2,1)} %copy.48) | copy-start | bytes 2359300
  193.3 0.8 copy-start.4
  239.5 8.9 %copy-start.12 = (s32[32,6]{0,1:T(8,128)S(1)}, s32[32,6]{0,1:T(8,128)}, u32[]{:S(2)}) copy-start(s32[32,6]{0,1:T(8,128)} %param.17) | copy-start | bytes 2308
  239.5 56.3 %all-to-all-start.3 = ((bf16[32,12,2048]{2,1,0:T(8,128)(2,1)}), bf16[32,12,2048]{2,1,0:T(8,128)(2,1)S(1)}, u32[]{:S(2)}, u32[]{:S(2)}) async-start(bf16[32,12,2048]{2,1,0:T(8,128)(2,1)} %reshape_reshape.11), calls=%async_computation.3 | async-start | bytes 4194304 | tf_op jit(solution)/shard_map/all_to_all | solution.py:142
  295.8 15.7 %all-to-all-start.4 = ((bf16[16,32,128]{2,1,0:T(8,128)(2,1)}), bf16[16,32,128]{2,1,0:T(8,128)(2,1)}, u32[]{:S(2)}, u32[]{:S(2)}) async-start(bf16[16,32,128]{2,1,0:T(8,128)(2,1)} %bitcast.64), calls=%async_computation.4 | async-start | bytes 262144 | tf_op jit(solution)/shard_map/all_to_all | solution.py:159
  304.2 9.6 %copy-start.13 = (f32[2048]{0:T(1024)S(1)}, f32[2048]{0:T(1024)}, u32[]{:S(2)}) copy-start(f32[2048]{0:T(1024)} %param.23) | copy-start | bytes 24580
Sparse Core Ops, SparseCore 0:
  9.8 88.7 all-gather.3
  101.5 44.4 all-gather.5
  173.5 40.6 all-gather.7

commit v9 on v7

--- a/solution.py
+++ b/solution.py
@@ -16,6 +16,11 @@
     pair = jnp.stack([blocks, other], axis=1)
     pair = jnp.where(lax.axis_index(axis) % 2 == 0, pair, jnp.flip(pair, axis=1))
     return pair.reshape(-1, *blocks.shape[1:])
+
+
+def pair_gather(array, axis):
+    blocks = lax.all_gather(array, axis, axis=0, axis_index_groups=core_groups(axis))
+    return with_sibling(blocks, axis)
 
 
 def pair_collect(array, axis):
@@ -117,7 +122,7 @@
     shared_pair = shared_gate_up.reshape(width, 2 * shared_units)
     normed_shared = normed + (gate_up_full[0, 0] * 0 + outgoing[0, 0, 0] * 0).astype(normed.dtype)
     both = jnp.dot(
-        lax.all_gather(normed_shared, "dp", axis=0, tiled=True),
+        in_order(pair_gather(normed_shared, "dp"), 0),
         shared_pair,
         preferred_element_type=jnp.float32,
     )
@@ -125,7 +130,7 @@
         jnp.bfloat16
     )
     out_cols = jnp.dot(
-        lax.all_gather(shared_hidden, "dp", axis=1, tiled=True),
+        in_order(pair_gather(shared_hidden, "dp"), 1),
         shared_down,
         preferred_element_type=jnp.float32,
     )

time: 250 us -> 250 us (level)
  waiting for transfers between devices: 110 us -> 94.7 us
  starting transfers between devices: 33.1 us -> 46.6 us
  matrix products: 20.8 us -> 16.3 us
  local copies, waits for them, and re-layouts: 14 us -> 17 us
  other arithmetic: 12.3 us -> 15.1 us
    ppermute x1 -> x3, starting transfers between devices: 5.55 us -> 19.2 us  [with_sibling(): lax.ppermute(blocks, axis, [(i, i ^ 1) for i in range(lax.axis_size(axis))])]
    all_to_all x1, waiting for transfers between devices: 36 us -> 26.5 us  [per_device(): lax.all_to_all(result, 'expert', split_axis=0, concat_axis=0, tiled=True)]
    all_gather x2, waiting for transfers between devices: 40 us -> 34.7 us  [pair_gather(): lax.all_gather(array, axis, axis=0, axis_index_groups=core_groups(axis))]
    all_to_all x1, waiting for transfers between devices: 13.3 us -> 9.25 us  [per_device(): lax.all_to_all(outgoing, 'expert', split_axis=0, concat_axis=0, tiled=True)]
    ppermute x1 -> x3, waiting for transfers between devices: 0.01 us -> 3.59 us  [with_sibling(): lax.ppermute(blocks, axis, [(i, i ^ 1) for i in range(lax.axis_size(axis))])]
    dot_general x2, matrix products: 6.13 us -> 2.57 us  [the longest x1 1.6 us: per_device(): jnp.dot(in_order(pair_gather(shared_hidden, 'dp'), 1), shared_down, prefe...]
  transfers between devices with their start and end apart: 8 -> 10, of which waited for: 7 -> 9; matrix products, arithmetic and copies ran while one was open for 15% -> 16% of each run, Pallas kernels for 0% -> 0%
where the time goes in v9:
time: 250 us; the launch traced here: 249 us
  waiting for transfers between devices  94.7 us (38%)
  starting transfers between devices  46.6 us (19%)
  blocking collectives  44.2 us (18%)
  local copies, waits for them, and re-layouts  17 us (7%)
  matrix products  16.3 us (7%)
  other arithmetic  15.1 us (6%)
  between operations  14.7 us (6%)
    all_to_all x1, blocking collectives, pair_collect(): lax.all_to_all(copies, axis, 0, 0, tiled=True, axis_index_groups=core_gro...  44.2 us
    all_gather x2, waiting for transfers between devices, pair_gather(): lax.all_gather(array, axis, axis=0, axis_index_groups=core_groups(axis))  34.7 us
    all_to_all x1, waiting for transfers between devices, per_device(): lax.all_to_all(result, 'expert', split_axis=0, concat_axis=0, tiled=True)  26.5 us
    ppermute x3, starting transfers between devices, with_sibling(): lax.ppermute(blocks, axis, [(i, i ^ 1) for i in range(lax.axis_size(axis))])  19.2 us
    all_to_all x1, waiting for transfers between devices, per_device(): lax.all_to_all(proj_cols, 'dp', split_axis=0, concat_axis=1, tiled=True)  10.3 us
    all_to_all x1, starting transfers between devices, per_device(): lax.all_to_all(outgoing, 'expert', split_axis=0, concat_axis=0, tiled=True)  9.68 us
    all_to_all x1, waiting for transfers between devices, per_device(): lax.all_to_all(outgoing, 'expert', split_axis=0, concat_axis=0, tiled=True)  9.25 us
    all_to_all x1, starting transfers between devices, per_device(): lax.all_to_all(result, 'expert', split_axis=0, concat_axis=0, tiled=True)  7.54 us
  transfers between devices with their start and end apart: 10, of which 9 were waited for; matrix products, arithmetic and copies ran while one was open for 16% of the time, Pallas kernels for 0%

profile of v9, /device:TPU:1, one launch (start us, length us, event | category | flops | bytes accessed | tf_op | source)
XLA Modules:
  0.0 248.7 jit_solution(6113541074067765059)
XLA Ops:
  7.7 1.8 pad_maximum_fusion.3
  9.7 44.2 %all_to_all.41 = bf16[8,32,2048]{2,1,0:T(8,128)(2,1)S(1)} all-to-all(bf16[8,32,2048]{2,1,0:T(8,128)(2,1)S(1)} %broadcast_in_dim.26), channel_id=1, replica_groups={{0,64,128,192,256,320,384,448},{32,96,160,224,288,352,416,480},{1,65,12..., dimensions={0} | all-to-all | bytes 2097152 | tf_op jit(solution)/shard_map/all_to_all | solution.py:28
  53.9 5.5 %collective-permute-start = (bf16[8,32,2048]{2,1,0:T(8,128)(2,1)S(1)}, bf16[8,32,2048]{2,1,0:T(8,128)(2,1)S(1)}, u32[]{:S(2)}, u32[]{:S(2)}) collective-permute-start(bf16[8,32,2048]{2,1,0:T(8,128)(2,1)S(1)} %all_to_all.41), channel_id=1, source_target_pairs={{0,32},{32,0},{64,96},{96,64},{128,160},{160,128},{192,224},{224,1... | collective-permute-start | bytes 3145736 | tf_op jit(solution)/shard_map/ppermute | solution.py:15
  63.1 1.9 reduce-window.6
  66.8 1.3 fusion.15
  70.8 1.4 convolution_convert_fusion.1
  72.2 3.4 %all-to-all-start.1 = ((bf16[16,32,128]{2,1,0:T(8,128)(2,1)}), bf16[16,32,128]{2,1,0:T(8,128)(2,1)S(1)}, u32[]{:S(2)}, u32[]{:S(2)}) async-start(bf16[16,32,128]{2,1,0:T(8,128)(2,1)} %bitcast.4), calls=%async_computation.1 | async-start | bytes 262144 | tf_op jit(solution)/shard_map/all_to_all | solution.py:91
  75.8 10.3 %all-to-all-done.1 = bf16[16,32,128]{2,1,0:T(8,128)(2,1)S(1)} async-done(((bf16[16,32,128]{2,1,0:T(8,128)(2,1)}), bf16[16,32,128]{2,1,0:T(8,128)(2,1)S(1)}, u32[]{:S(2)}, u32[]{:S(2)}) %all-to-all-start.1) | async-done | bytes 131104 | tf_op jit(solution)/shard_map/all_to_all | solution.py:91
  87.0 1.6 reshape.114
  88.5 1.2 slice.42
  90.3 3.1 %all-gather.6.cloned.1.call-done = bf16[2048,2112]{1,0:T(8,128)(2,1)} async-done(((bf16[128,2112]{1,0:T(8,128)(2,1)}), bf16[2048,2112]{1,0:T(8,128)(2,1)}) %all-gather.6.cloned.1.call-update) | async-done | bytes 8650768 | tf_op jit(solution)/shard_map/all_gather | solution.py:53
  93.4 1.2 slice.41
  96.1 9.7 %all-to-all-start.2 = ((bf16[32,12,2048]{2,1,0:T(8,128)(2,1)}), bf16[32,12,2048]{2,1,0:T(8,128)(2,1)S(1)}, u32[]{:S(2)}, u32[]{:S(2)}) async-start(bf16[32,12,2048]{2,1,0:T(8,128)(2,1)} %reshape.114), calls=%async_computation.2 | async-start | bytes 4194304 | tf_op jit(solution)/shard_map/all_to_all | solution.py:113
  105.8 27.0 %all-gather.8.cloned.1.call-done = bf16[256,2048]{1,0:T(8,128)(2,1)} async-done(((bf16[32,2048]{1,0:T(8,128)(2,1)}), bf16[256,2048]{1,0:T(8,128)(2,1)}) %all-gather.8.cloned.1.call-update) | async-done | bytes 1048592 | tf_op jit(solution)/shard_map/all_gather | solution.py:22
  132.7 6.4 %collective-permute-start.1 = (bf16[8,32,2048]{2,1,0:T(8,128)(2,1)}, bf16[8,32,2048]{2,1,0:T(8,128)(2,1)S(1)}, u32[]{:S(2)}, u32[]{:S(2)}) collective-permute-start(bf16[8,32,2048]{2,1,0:T(8,128)(2,1)} %bitcast.93), channel_id=1, source_target_pairs={{0,32},{32,0},{64,96},{96,64},{128,160},{160,128},{192,224},{224,1... | collective-permute-start | bytes 3145736 | tf_op jit(solution)/shard_map/ppermute | solution.py:15
  139.1 2.5 collective-permute-done.1
  141.6 1.4 pad_maximum_fusion.2
  145.4 9.2 %all-to-all-done.2 = bf16[32,12,2048]{2,1,0:T(8,128)(2,1)S(1)} async-done(((bf16[32,12,2048]{2,1,0:T(8,128)(2,1)}), bf16[32,12,2048]{2,1,0:T(8,128)(2,1)S(1)}, u32[]{:S(2)}, u32[]{:S(2)}) %all-to-all-start.2) | async-done | bytes 1572896 | tf_op jit(solution)/shard_map/all_to_all | solution.py:113
  154.7 1.3 reshape.115
  156.0 5.8 %fusion = f32[384,1408]{1,0:T(8,128)S(1)} fusion(bf16[384,2048]{1,0:T(8,128)(2,1)} %reshape.115, bf16[2048,2112]{1,0:T(8,128)(2,1)} %all-gather.6.cloned.1.call-done), kind=kOutput, calls=%fused_computation | convolution fusion | flops 2214592512 | bytes 9502720 | tf_op jit(solution)/shard_map/dot_general | solution.py:116
  161.8 3.3 %fusion.3 = bf16[384,2048]{1,0:T(8,128)(2,1)S(1)} fusion(bf16[2048,2112]{1,0:T(8,128)(2,1)} %all-gather.6.cloned.1.call-done, f32[384,1408]{1,0:T(8,128)S(1)} %fusion), kind=kOutput, calls=%fused_computation.8 | convolution fusion | flops 1109704704 | bytes 7077888 | tf_op jit(solution)/shard_map/dot_general | solution.py:118
  165.1 1.6 reshape.118
  166.7 7.5 %all-to-all-start.3 = ((bf16[32,12,2048]{2,1,0:T(8,128)(2,1)}), bf16[32,12,2048]{2,1,0:T(8,128)(2,1)S(1)}, u32[]{:S(2)}, u32[]{:S(2)}) async-start(bf16[32,12,2048]{2,1,0:T(8,128)(2,1)} %reshape.118), calls=%async_computation.3 | async-start | bytes 4194304 | tf_op jit(solution)/shard_map/all_to_all | solution.py:120
  174.2 7.8 %all-gather.10.cloned.1.call-done = bf16[4096,176]{0,1:T(8,128)(2,1)} async-done(((bf16[512,176]{0,1:T(8,128)(2,1)}), bf16[4096,176]{0,1:T(8,128)(2,1)}) %all-gather.10.cloned.1.call-update) | async-done | bytes 1441808 | tf_op jit(solution)/shard_map/all_gather | solution.py:22
  182.0 1.6 copy.60
  183.6 7.3 %collective-permute-start.2 = (bf16[8,512,176]{1,2,0:T(8,128)(2,1)S(1)}, bf16[8,512,176]{1,2,0:T(8,128)(2,1)S(1)}, u32[]{:S(2)}, u32[]{:S(2)}) collective-permute-start(bf16[8,512,176]{1,2,0:T(8,128)(2,1)S(1)} %bitcast.90), channel_id=1, source_target_pairs={{0,32},{32,0},{64,96},{96,64},{128,160},{160,128},{192,224},{224,1... | collective-permute-start | bytes 4325384 | tf_op jit(solution)/shard_map/ppermute | solution.py:15
  195.0 1.6 convolution_convert_fusion.2
  196.6 26.5 %all-to-all-done.3 = bf16[32,12,2048]{2,1,0:T(8,128)(2,1)S(1)} async-done(((bf16[32,12,2048]{2,1,0:T(8,128)(2,1)}), bf16[32,12,2048]{2,1,0:T(8,128)(2,1)S(1)}, u32[]{:S(2)}, u32[]{:S(2)}) %all-to-all-start.3) | async-done | bytes 1572896 | tf_op jit(solution)/shard_map/all_to_all | solution.py:120
  223.0 6.7 %all-to-all-start.4 = ((bf16[16,32,128]{2,1,0:T(8,128)(2,1)}), bf16[16,32,128]{2,1,0:T(8,128)(2,1)}, u32[]{:S(2)}, u32[]{:S(2)}) async-start(bf16[16,32,128]{2,1,0:T(8,128)(2,1)} %bitcast.96), calls=%async_computation.4 | async-start | bytes 262144 | tf_op jit(solution)/shard_map/all_to_all | solution.py:137
  230.5 1.3 reshape.119
  231.8 7.2 %all-to-all-done.4 = bf16[16,32,128]{2,1,0:T(8,128)(2,1)} async-done(((bf16[16,32,128]{2,1,0:T(8,128)(2,1)}), bf16[16,32,128]{2,1,0:T(8,128)(2,1)}, u32[]{:S(2)}, u32[]{:S(2)}) %all-to-all-start.4) | async-done | bytes 131104 | tf_op jit(solution)/shard_map/all_to_all | solution.py:137
  239.0 2.4 multiply_reduce_fusion
  (79 shorter events, 19.0 us)
Async XLA Ops:
  6.5 137.1 %copy-start = (bf16[2048,2,176]{0,2,1:T(8,128)(2,1)S(1)}, bf16[2048,2,176]{0,2,1:T(8,128)(2,1)}, u32[]{:S(2)}) copy-start(bf16[2048,2,176]{0,2,1:T(8,128)(2,1)} %param.21) | copy-start | bytes 4325380
  6.5 3.0 %copy-start.6 = (bf16[32,2048]{1,0:T(8,128)(2,1)S(1)}, bf16[32,2048]{1,0:T(8,128)(2,1)}, u32[]{:S(2)}) copy-start(bf16[32,2048]{1,0:T(8,128)(2,1)} %param.13) | copy-start | bytes 393220
  6.5 86.9 %all-gather.6.cloned.1.call-start = ((), (), s32[]{:S(2)}) async-start(), calls=%async_computation.5 | async-start | bytes 9469952 | tf_op jit(solution)/shard_map/all_gather | solution.py:53
  9.6 50.0 %copy-start.11 = (s32[32,6]{0,1:T(8,128)S(1)}, s32[32,6]{0,1:T(8,128)}, u32[]{:S(2)}) copy-start(s32[32,6]{0,1:T(8,128)} %param.17) | copy-start | bytes 2308
  9.6 50.0 %copy-start.16 = (s32[32]{0:T(128)S(1)}, s32[32]{0:T(128)}, u32[]{:S(2)}) copy-start(s32[32]{0:T(128)} %param.18) | copy-start | bytes 388
  53.9 15.6 %collective-permute-start = (bf16[8,32,2048]{2,1,0:T(8,128)(2,1)S(1)}, bf16[8,32,2048]{2,1,0:T(8,128)(2,1)S(1)}, u32[]{:S(2)}, u32[]{:S(2)}) collective-permute-start(bf16[8,32,2048]{2,1,0:T(8,128)(2,1)S(1)} %all_to_all.41), channel_id=1, source_target_pairs={{0,32},{32,0},{64,96},{96,64},{128,160},{160,128},{192,224},{224,1... | collective-permute-start | bytes 3145736 | tf_op jit(solution)/shard_map/ppermute | solution.py:15
  69.7 1.1 copy-start.5
  70.3 5.4 %copy-start.8 = (s32[32,6]{0,1:T(8,128)S(1)}, s32[32,6]{0,1:T(8,128)}, u32[]{:S(2)}) copy-start(s32[32,6]{0,1:T(8,128)} %select_reduce_fusion.2) | copy-start | bytes 2308
  70.3 5.4 %copy-start.10 = (s32[32,6]{0,1:T(8,128)S(1)}, s32[32,6]{0,1:T(8,128)}, u32[]{:S(2)}) copy-start(s32[32,6]{0,1:T(8,128)} %copy.42) | copy-start | bytes 2308
  70.3 15.8 %copy-start.7 = (bf16[32,2048]{1,0:T(8,128)(2,1)S(1)}, bf16[32,2048]{1,0:T(8,128)(2,1)}, u32[]{:S(2)}) copy-start(bf16[32,2048]{1,0:T(8,128)(2,1)} %param.12) | copy-start | bytes 393220
  70.3 16.0 %copy-start.9 = (f32[2048]{0:T(1024)S(1)}, f32[2048]{0:T(1024)}, u32[]{:S(2)}) copy-start(f32[2048]{0:T(1024)} %param.15) | copy-start | bytes 24580
  72.2 13.9 %all-to-all-start.1 = ((bf16[16,32,128]{2,1,0:T(8,128)(2,1)}), bf16[16,32,128]{2,1,0:T(8,128)(2,1)S(1)}, u32[]{:S(2)}, u32[]{:S(2)}) async-start(bf16[16,32,128]{2,1,0:T(8,128)(2,1)} %bitcast.4), calls=%async_computation.1 | async-start | bytes 262144 | tf_op jit(solution)/shard_map/all_to_all | solution.py:91
  75.6 57.1 %all-gather.8.cloned.1.call-start = ((), (), s32[]{:S(2)}) async-start(), calls=%async_computation.6 | async-start | bytes 1179648 | tf_op jit(solution)/shard_map/all_gather | solution.py:22
  86.3 9.0 %copy-start.2 = (bf16[32,2048]{1,0:T(8,128)(2,1)}, bf16[32,2048]{1,0:T(8,128)(2,1)S(1)}, u32[]{:S(2)}) copy-start(bf16[32,2048]{1,0:T(8,128)(2,1)S(1)} %get-tuple-element.6) | copy-start | bytes 393220
  86.3 9.0 %copy-start.14 = (f32[32]{0:T(128)}, f32[32]{0:T(128)S(1)}, u32[]{:S(2)}) copy-start(f32[32]{0:T(128)S(1)} %add_rsqrt_fusion.1) | copy-start | bytes 388
  96.1 58.6 %all-to-all-start.2 = ((bf16[32,12,2048]{2,1,0:T(8,128)(2,1)}), bf16[32,12,2048]{2,1,0:T(8,128)(2,1)S(1)}, u32[]{:S(2)}, u32[]{:S(2)}) async-start(bf16[32,12,2048]{2,1,0:T(8,128)(2,1)} %reshape.114), calls=%async_computation.2 | async-start | bytes 4194304 | tf_op jit(solution)/shard_map/all_to_all | solution.py:113
  105.7 76.3 %all-gather.10.cloned.1.call-start = ((), (), s32[]{:S(2)}) async-start(), calls=%async_computation.7 | async-start | bytes 1622016 | tf_op jit(solution)/shard_map/all_gather | solution.py:22
  132.7 8.9 %collective-permute-start.1 = (bf16[8,32,2048]{2,1,0:T(8,128)(2,1)}, bf16[8,32,2048]{2,1,0:T(8,128)(2,1)S(1)}, u32[]{:S(2)}, u32[]{:S(2)}) collective-permute-start(bf16[8,32,2048]{2,1,0:T(8,128)(2,1)} %bitcast.93), channel_id=1, source_target_pairs={{0,32},{32,0},{64,96},{96,64},{128,160},{160,128},{192,224},{224,1... | collective-permute-start | bytes 3145736 | tf_op jit(solution)/shard_map/ppermute | solution.py:15
  166.7 56.4 %all-to-all-start.3 = ((bf16[32,12,2048]{2,1,0:T(8,128)(2,1)}), bf16[32,12,2048]{2,1,0:T(8,128)(2,1)S(1)}, u32[]{:S(2)}, u32[]{:S(2)}) async-start(bf16[32,12,2048]{2,1,0:T(8,128)(2,1)} %reshape.118), calls=%async_computation.3 | async-start | bytes 4194304 | tf_op jit(solution)/shard_map/all_to_all | solution.py:120
  174.2 17.0 %copy-start.12 = (s32[32,6]{0,1:T(8,128)S(1)}, s32[32,6]{0,1:T(8,128)}, u32[]{:S(2)}) copy-start(s32[32,6]{0,1:T(8,128)} %param.17) | copy-start | bytes 2308
  182.0 8.9 %copy-start.3 = (bf16[32,2048]{1,0:T(8,128)(2,1)S(1)}, bf16[32,2048]{1,0:T(8,128)(2,1)}, u32[]{:S(2)}) copy-start(bf16[32,2048]{1,0:T(8,128)(2,1)} %copy-done.2) | copy-start | bytes 393220
  182.0 8.9 %copy-start.15 = (f32[32]{0:T(128)S(1)}, f32[32]{0:T(128)}, u32[]{:S(2)}) copy-start(f32[32]{0:T(128)} %copy-done.14) | copy-start | bytes 388
  182.0 8.9 %copy-start.17 = (bf16[2048,32]{0,1:T(8,128)(2,1)S(1)}, bf16[2048,32]{0,1:T(8,128)(2,1)}, u32[]{:S(2)}) copy-start(bf16[2048,32]{0,1:T(8,128)(2,1)} %param.16) | copy-start | bytes 393220
  182.0 9.4 %copy-start.1 = (bf16[4096,176]{0,1:T(8,128)(2,1)S(1)}, bf16[4096,176]{0,1:T(8,128)(2,1)}, u32[]{:S(2)}) copy-start(bf16[4096,176]{0,1:T(8,128)(2,1)} %all-gather.10.cloned.1.call-done) | copy-start | bytes 4325380
  183.6 9.9 %collective-permute-start.2 = (bf16[8,512,176]{1,2,0:T(8,128)(2,1)S(1)}, bf16[8,512,176]{1,2,0:T(8,128)(2,1)S(1)}, u32[]{:S(2)}, u32[]{:S(2)}) collective-permute-start(bf16[8,512,176]{1,2,0:T(8,128)(2,1)S(1)} %bitcast.90), channel_id=1, source_target_pairs={{0,32},{32,0},{64,96},{96,64},{128,160},{160,128},{192,224},{224,1... | collective-permute-start | bytes 4325384 | tf_op jit(solution)/shard_map/ppermute | solution.py:15
  193.8 1.1 copy-start.4
  223.0 16.0 %all-to-all-start.4 = ((bf16[16,32,128]{2,1,0:T(8,128)(2,1)}), bf16[16,32,128]{2,1,0:T(8,128)(2,1)}, u32[]{:S(2)}, u32[]{:S(2)}) async-start(bf16[16,32,128]{2,1,0:T(8,128)(2,1)} %bitcast.96), calls=%async_computation.4 | async-start | bytes 262144 | tf_op jit(solution)/shard_map/all_to_all | solution.py:137
  230.5 10.9 %copy-start.13 = (f32[2048]{0:T(1024)S(1)}, f32[2048]{0:T(1024)}, u32[]{:S(2)}) copy-start(f32[2048]{0:T(1024)} %param.23) | copy-start | bytes 24580
Sparse Core Ops, SparseCore 0:
  9.7 83.6 all-gather.5
  96.2 36.5 all-gather.7
  145.5 36.4 all-gather.9

commit v10 on v9

--- a/solution.py
+++ b/solution.py
@@ -129,14 +129,13 @@
     shared_hidden = (jax.nn.silu(both[:, :shared_units]) * both[:, shared_units:]).astype(
         jnp.bfloat16
     )
-    out_cols = jnp.dot(
-        in_order(pair_gather(shared_hidden, "dp"), 1),
-        shared_down,
-        preferred_element_type=jnp.float32,
-    )
-    shared_out = lax.all_to_all(
-        out_cols.astype(jnp.bfloat16), "dp", split_axis=0, concat_axis=1, tiled=True
-    ).astype(jnp.float32)
+    groups_dp = lax.axis_size("dp")
+    down_blocks = shared_down.reshape(groups_dp, shared_units, -1)
+    down_rows = lax.all_to_all(down_blocks, "dp", 0, 0, tiled=True)
+    down_rows = in_order(down_rows, 1)
+    partial = jnp.dot(shared_hidden, down_rows, preferred_element_type=jnp.float32)
+    partial = partial + (result[0, 0, 0] * 0).astype(partial.dtype)
+    shared_out = lax.psum_scatter(partial, "dp", scatter_dimension=0, tiled=True)
     weighted = jnp.sum(
         placed.reshape(rows, choose, experts * capacity) * gates[:, :, None], axis=1
     )

time: 250 us -> 252 us (level)
  starting transfers between devices: 46.6 us -> 32.9 us
  waiting for transfers between devices: 94.7 us -> 107 us
  matrix products: 16.3 us -> 19.4 us
    all_to_all x1, waiting for transfers between devices: 9.25 us -> 44.2 us  [per_device(): lax.all_to_all(outgoing, 'expert', split_axis=0, concat_axis=0, tiled=True)]
    all_gather x2 -> x1, waiting for transfers between devices: 34.7 us -> 0.01 us  [pair_gather(): lax.all_gather(array, axis, axis=0, axis_index_groups=core_groups(axis))]
    all_to_all x1, waiting for transfers between devices: 26.5 us -> 47.1 us  [per_device(): lax.all_to_all(result, 'expert', split_axis=0, concat_axis=0, tiled=True)]
    ppermute x3 -> x2, starting transfers between devices: 19.2 us -> 7.73 us  [with_sibling(): lax.ppermute(blocks, axis, [(i, i ^ 1) for i in range(lax.axis_size(axis))])]
    all_to_all x1, waiting for transfers between devices: 7.2 us -> 2 us  [per_device(): down_rows = lax.all_to_all(down_blocks, 'dp', 0, 0, tiled=True)]
    ppermute x3 -> x2, waiting for transfers between devices: 3.59 us -> 0.01 us  [with_sibling(): lax.ppermute(blocks, axis, [(i, i ^ 1) for i in range(lax.axis_size(axis))])]
    all_gather x1, waiting for transfers between devices: 3.13 us -> 0.02 us  [turned_gather(): out = lax.all_gather(both, axis, axis=0, tiled=True)]
    reduce_scatter x0 -> x1, waiting for transfers between devices: none -> 2.88 us  [per_device(): lax.psum_scatter(partial, 'dp', scatter_dimension=0, tiled=True)]
  transfers between devices with their start and end apart: 10 -> 9, of which waited for: 9 -> 5; matrix products, arithmetic and copies ran while one was open for 16% -> 16% of each run, Pallas kernels for 0% -> 0%
where the time goes in v10:
time: 252 us; the launch traced here: 249 us
  waiting for transfers between devices  107 us (42%)
  blocking collectives  44.2 us (18%)
  starting transfers between devices  32.9 us (13%)
  matrix products  19.4 us (8%)
  local copies, waits for them, and re-layouts  15.7 us (6%)
  between operations  15.4 us (6%)
  other arithmetic  14.7 us (6%)
    all_to_all x1, waiting for transfers between devices, per_device(): lax.all_to_all(result, 'expert', split_axis=0, concat_axis=0, tiled=True)  47.1 us
    all_to_all x1, blocking collectives, pair_collect(): lax.all_to_all(copies, axis, 0, 0, tiled=True, axis_index_groups=core_gro...  44.2 us
    all_to_all x1, waiting for transfers between devices, per_device(): lax.all_to_all(outgoing, 'expert', split_axis=0, concat_axis=0, tiled=True)  44.2 us
    all_to_all x1, waiting for transfers between devices, per_device(): lax.all_to_all(proj_cols, 'dp', split_axis=0, concat_axis=1, tiled=True)  10.4 us
    all_to_all x1, starting transfers between devices, per_device(): lax.all_to_all(outgoing, 'expert', split_axis=0, concat_axis=0, tiled=True)  9.89 us
    ppermute x2, starting transfers between devices, with_sibling(): lax.ppermute(blocks, axis, [(i, i ^ 1) for i in range(lax.axis_size(axis))])  7.73 us
    all_to_all x1, starting transfers between devices, per_device(): lax.all_to_all(result, 'expert', split_axis=0, concat_axis=0, tiled=True)  6.53 us
    dot_general x1, matrix products, per_device(): both = jnp.dot(flat, gate_up_full, preferred_element_type=jnp.float32)  5.71 us
  transfers between devices with their start and end apart: 9, of which 5 were waited for; matrix products, arithmetic and copies ran while one was open for 16% of the time, Pallas kernels for 0%

profile of v10, /device:TPU:1, one launch (start us, length us, event | category | flops | bytes accessed | tf_op | source)
XLA Modules:
  0.0 248.9 jit_solution(6929732140985645868)
XLA Ops:
  6.5 1.2 copy.38
  7.7 1.8 pad_maximum_fusion.2
  9.7 44.2 %all_to_all.33 = bf16[8,32,2048]{2,1,0:T(8,128)(2,1)S(1)} all-to-all(bf16[8,32,2048]{2,1,0:T(8,128)(2,1)S(1)} %broadcast_in_dim.26), channel_id=1, replica_groups={{0,64,128,192,256,320,384,448},{32,96,160,224,288,352,416,480},{1,65,12..., dimensions={0} | all-to-all | bytes 2097152 | tf_op jit(solution)/shard_map/all_to_all | solution.py:28
  54.0 5.5 %collective-permute-start = (bf16[8,32,2048]{2,1,0:T(8,128)(2,1)S(1)}, bf16[8,32,2048]{2,1,0:T(8,128)(2,1)S(1)}, u32[]{:S(2)}, u32[]{:S(2)}) collective-permute-start(bf16[8,32,2048]{2,1,0:T(8,128)(2,1)S(1)} %all_to_all.33), channel_id=1, source_target_pairs={{0,32},{32,0},{64,96},{96,64},{128,160},{160,128},{192,224},{224,1... | collective-permute-start | bytes 3145736 | tf_op jit(solution)/shard_map/ppermute | solution.py:15
  63.1 1.9 reduce-window.6
  66.8 1.3 fusion.19
  70.8 1.4 convolution_convert_fusion.1
  72.2 3.4 %all-to-all-start.1 = ((bf16[16,32,128]{2,1,0:T(8,128)(2,1)}), bf16[16,32,128]{2,1,0:T(8,128)(2,1)S(1)}, u32[]{:S(2)}, u32[]{:S(2)}) async-start(bf16[16,32,128]{2,1,0:T(8,128)(2,1)} %bitcast.4), calls=%async_computation.1 | async-start | bytes 262144 | tf_op jit(solution)/shard_map/all_to_all | solution.py:91
  75.8 10.4 %all-to-all-done.1 = bf16[16,32,128]{2,1,0:T(8,128)(2,1)S(1)} async-done(((bf16[16,32,128]{2,1,0:T(8,128)(2,1)}), bf16[16,32,128]{2,1,0:T(8,128)(2,1)S(1)}, u32[]{:S(2)}, u32[]{:S(2)}) %all-to-all-start.1) | async-done | bytes 131104 | tf_op jit(solution)/shard_map/all_to_all | solution.py:91
  87.6 1.6 reshape.113
  89.2 9.9 %all-to-all-start.2 = ((bf16[32,12,2048]{2,1,0:T(8,128)(2,1)}), bf16[32,12,2048]{2,1,0:T(8,128)(2,1)S(1)}, u32[]{:S(2)}, u32[]{:S(2)}) async-start(bf16[32,12,2048]{2,1,0:T(8,128)(2,1)} %reshape.113), calls=%async_computation.2 | async-start | bytes 4194304 | tf_op jit(solution)/shard_map/all_to_all | solution.py:113
  99.1 1.2 slice.46
  101.0 1.2 slice.45
  102.7 1.7 broadcast_add_fusion
  104.4 44.2 %all-to-all-done.2 = bf16[32,12,2048]{2,1,0:T(8,128)(2,1)S(1)} async-done(((bf16[32,12,2048]{2,1,0:T(8,128)(2,1)}), bf16[32,12,2048]{2,1,0:T(8,128)(2,1)S(1)}, u32[]{:S(2)}, u32[]{:S(2)}) %all-to-all-start.2) | async-done | bytes 1572896 | tf_op jit(solution)/shard_map/all_to_all | solution.py:113
  148.6 5.3 %all-to-all-start.4 = ((bf16[16,176,128]{2,1,0:T(8,128)(2,1)}), bf16[16,176,128]{2,1,0:T(8,128)(2,1)}, u32[]{:S(2)}, u32[]{:S(2)}) async-start(bf16[16,176,128]{2,1,0:T(8,128)(2,1)} %bitcast.76), calls=%async_computation.4 | async-start | bytes 1441792 | tf_op jit(solution)/shard_map/all_to_all | solution.py:134
  153.9 1.4 reshape.114
  155.3 2.2 collective-permute-start.1
  157.5 5.7 %fusion = f32[384,1408]{1,0:T(8,128)S(1)} fusion(bf16[384,2048]{1,0:T(8,128)(2,1)} %reshape.114, bf16[2048,2112]{1,0:T(8,128)(2,1)} %all-gather.4.cloned.1.call-done), kind=kOutput, calls=%fused_computation | convolution fusion | flops 2214592512 | bytes 9502720 | tf_op jit(solution)/shard_map/dot_general | solution.py:116
  163.2 3.3 %fusion.3 = bf16[384,2048]{1,0:T(8,128)(2,1)S(1)} fusion(bf16[2048,2112]{1,0:T(8,128)(2,1)} %all-gather.4.cloned.1.call-done, f32[384,1408]{1,0:T(8,128)S(1)} %fusion), kind=kOutput, calls=%fused_computation.7 | convolution fusion | flops 1109704704 | bytes 7077888 | tf_op jit(solution)/shard_map/dot_general | solution.py:118
  166.5 1.5 reshape.117
  168.0 1.3 slice.49
  170.0 1.7 pad_maximum_fusion.1
  172.4 1.0 fusion.26
  173.3 2.0 all-to-all-done.4
  175.3 3.8 %convolution_add_fusion = f32[512,2048]{1,0:T(8,128)} fusion(f32[]{:T(128)S(6)} %convert.10, f32[512,352]{0,1:T(8,128)S(1)} %fusion.26, bf16[16,176,128]{2,1,0:T(8,128)(2,1)} %all-to-all-done.4), kind=kOutput, calls=%fused_computation.2 | convolution fusion | flops 370688000 | bytes 5636100 | tf_op jit(solution)/shard_map/dot_general | solution.py:136
  179.2 6.5 %all-to-all-start.3 = ((bf16[32,12,2048]{2,1,0:T(8,128)(2,1)}), bf16[32,12,2048]{2,1,0:T(8,128)(2,1)S(1)}, u32[]{:S(2)}, u32[]{:S(2)}) async-start(bf16[32,12,2048]{2,1,0:T(8,128)(2,1)} %reshape.117), calls=%async_computation.3 | async-start | bytes 4194304 | tf_op jit(solution)/shard_map/all_to_all | solution.py:120
  185.7 1.2 fusion.23
  187.9 47.1 %all-to-all-done.3 = bf16[32,12,2048]{2,1,0:T(8,128)(2,1)S(1)} async-done(((bf16[32,12,2048]{2,1,0:T(8,128)(2,1)}), bf16[32,12,2048]{2,1,0:T(8,128)(2,1)S(1)}, u32[]{:S(2)}, u32[]{:S(2)}) %all-to-all-start.3) | async-done | bytes 1572896 | tf_op jit(solution)/shard_map/all_to_all | solution.py:120
  234.9 1.4 reshape.118
  236.3 2.9 %reduce-scatter.2.cloned.1.call-done = f32[32,2048]{1,0:T(8,128)} async-done(((f32[512,2048]{1,0:T(8,128)}), f32[32,2048]{1,0:T(8,128)}) %reduce-scatter.2.cloned.1.call-update) | async-done | bytes 262160 | tf_op jit(solution)/shard_map/reduce_scatter | solution.py:138
  239.2 2.4 multiply_reduce_fusion
  (62 shorter events, 12.2 us)
Async XLA Ops:
  6.5 165.8 %copy-start = (bf16[2048,2,176]{0,2,1:T(8,128)(2,1)S(1)}, bf16[2048,2,176]{0,2,1:T(8,128)(2,1)}, u32[]{:S(2)}) copy-start(bf16[2048,2,176]{0,2,1:T(8,128)(2,1)} %param.21) | copy-start | bytes 4325380
  6.5 3.1 %copy-start.3 = (bf16[32,2048]{1,0:T(8,128)(2,1)S(1)}, bf16[32,2048]{1,0:T(8,128)(2,1)}, u32[]{:S(2)}) copy-start(bf16[32,2048]{1,0:T(8,128)(2,1)} %param.13) | copy-start | bytes 393220
  6.5 94.4 %all-gather.4.cloned.1.call-start = ((), (), s32[]{:S(2)}) async-start(), calls=%async_computation.6 | async-start | bytes 9469952 | tf_op jit(solution)/shard_map/all_gather | solution.py:53
  9.6 50.0 %copy-start.8 = (s32[32,6]{0,1:T(8,128)S(1)}, s32[32,6]{0,1:T(8,128)}, u32[]{:S(2)}) copy-start(s32[32,6]{0,1:T(8,128)} %param.17) | copy-start | bytes 2308
  9.6 50.0 %copy-start.12 = (s32[32]{0:T(128)S(1)}, s32[32]{0:T(128)}, u32[]{:S(2)}) copy-start(s32[32]{0:T(128)} %param.18) | copy-start | bytes 388
  54.0 15.6 %collective-permute-start = (bf16[8,32,2048]{2,1,0:T(8,128)(2,1)S(1)}, bf16[8,32,2048]{2,1,0:T(8,128)(2,1)S(1)}, u32[]{:S(2)}, u32[]{:S(2)}) collective-permute-start(bf16[8,32,2048]{2,1,0:T(8,128)(2,1)S(1)} %all_to_all.33), channel_id=1, source_target_pairs={{0,32},{32,0},{64,96},{96,64},{128,160},{160,128},{192,224},{224,1... | collective-permute-start | bytes 3145736 | tf_op jit(solution)/shard_map/ppermute | solution.py:15
  69.7 1.1 copy-start.2
  70.3 5.3 %copy-start.5 = (s32[32,6]{0,1:T(8,128)S(1)}, s32[32,6]{0,1:T(8,128)}, u32[]{:S(2)}) copy-start(s32[32,6]{0,1:T(8,128)} %select_reduce_fusion.2) | copy-start | bytes 2308
  70.3 5.3 %copy-start.7 = (s32[32,6]{0,1:T(8,128)S(1)}, s32[32,6]{0,1:T(8,128)}, u32[]{:S(2)}) copy-start(s32[32,6]{0,1:T(8,128)} %copy.37) | copy-start | bytes 2308
  70.3 15.8 %copy-start.4 = (bf16[32,2048]{1,0:T(8,128)(2,1)S(1)}, bf16[32,2048]{1,0:T(8,128)(2,1)}, u32[]{:S(2)}) copy-start(bf16[32,2048]{1,0:T(8,128)(2,1)} %param.12) | copy-start | bytes 393220
  70.4 16.6 %copy-start.6 = (f32[2048]{0:T(1024)S(1)}, f32[2048]{0:T(1024)}, u32[]{:S(2)}) copy-start(f32[2048]{0:T(1024)} %param.15) | copy-start | bytes 24580
  72.2 13.9 %all-to-all-start.1 = ((bf16[16,32,128]{2,1,0:T(8,128)(2,1)}), bf16[16,32,128]{2,1,0:T(8,128)(2,1)S(1)}, u32[]{:S(2)}, u32[]{:S(2)}) async-start(bf16[16,32,128]{2,1,0:T(8,128)(2,1)} %bitcast.4), calls=%async_computation.1 | async-start | bytes 262144 | tf_op jit(solution)/shard_map/all_to_all | solution.py:91
  86.3 0.7 copy-start.1
  86.3 16.4 %copy-start.11 = (f32[32]{0:T(128)}, f32[32]{0:T(128)S(1)}, u32[]{:S(2)}) copy-start(f32[32]{0:T(128)S(1)} %add_rsqrt_fusion.1) | copy-start | bytes 388
  89.2 59.4 %all-to-all-start.2 = ((bf16[32,12,2048]{2,1,0:T(8,128)(2,1)}), bf16[32,12,2048]{2,1,0:T(8,128)(2,1)S(1)}, u32[]{:S(2)}, u32[]{:S(2)}) async-start(bf16[32,12,2048]{2,1,0:T(8,128)(2,1)} %reshape.113), calls=%async_computation.2 | async-start | bytes 4194304 | tf_op jit(solution)/shard_map/all_to_all | solution.py:113
  99.1 56.2 %all-gather.6.cloned.1.call-start = ((), (), s32[]{:S(2)}) async-start(), calls=%async_computation.8 | async-start | bytes 1179648 | tf_op jit(solution)/shard_map/all_gather | solution.py:22
  148.6 26.7 %all-to-all-start.4 = ((bf16[16,176,128]{2,1,0:T(8,128)(2,1)}), bf16[16,176,128]{2,1,0:T(8,128)(2,1)}, u32[]{:S(2)}, u32[]{:S(2)}) async-start(bf16[16,176,128]{2,1,0:T(8,128)(2,1)} %bitcast.76), calls=%async_computation.4 | async-start | bytes 1441792 | tf_op jit(solution)/shard_map/all_to_all | solution.py:134
  153.8 85.3 %reduce-scatter.2.cloned.1.call-start = ((), (), s32[]{:S(2)}) async-start(), calls=%async_computation.7 | async-start | bytes 4456448 | tf_op jit(solution)/shard_map/reduce_scatter | solution.py:138
  155.3 14.7 %collective-permute-start.1 = (bf16[8,32,2048]{2,1,0:T(8,128)(2,1)}, bf16[8,32,2048]{2,1,0:T(8,128)(2,1)}, u32[]{:S(2)}, u32[]{:S(2)}) collective-permute-start(bf16[8,32,2048]{2,1,0:T(8,128)(2,1)} %bitcast.74), channel_id=1, source_target_pairs={{0,32},{32,0},{64,96},{96,64},{128,160},{160,128},{192,224},{224,1... | collective-permute-start | bytes 3145736 | tf_op jit(solution)/shard_map/ppermute | solution.py:15
  179.1 7.8 %copy-start.9 = (s32[32,6]{0,1:T(8,128)S(1)}, s32[32,6]{0,1:T(8,128)}, u32[]{:S(2)}) copy-start(s32[32,6]{0,1:T(8,128)} %param.17) | copy-start | bytes 2308
  179.2 55.8 %all-to-all-start.3 = ((bf16[32,12,2048]{2,1,0:T(8,128)(2,1)}), bf16[32,12,2048]{2,1,0:T(8,128)(2,1)S(1)}, u32[]{:S(2)}, u32[]{:S(2)}) async-start(bf16[32,12,2048]{2,1,0:T(8,128)(2,1)} %reshape.117), calls=%async_computation.3 | async-start | bytes 4194304 | tf_op jit(solution)/shard_map/all_to_all | solution.py:120
  187.9 53.8 %copy-start.10 = (f32[2048]{0:T(1024)S(1)}, f32[2048]{0:T(1024)}, u32[]{:S(2)}) copy-start(f32[2048]{0:T(1024)} %param.23) | copy-start | bytes 24580
Sparse Core Ops, SparseCore 0:
  9.7 83.6 all-gather.3
  104.5 34.6 all-gather.5
  179.3 59.8 reduce-scatter.1

commit v11 on v9

--- a/solution.py
+++ b/solution.py
@@ -93,7 +93,8 @@
     normed = rms_scale(resid, post_gain).astype(jnp.bfloat16)
     logits = jnp.dot(normed, router_weight, preferred_element_type=jnp.float32)
     expert_range = jnp.arange(experts, dtype=jnp.int32)
-    picked = expert_ids[:, :, None] == expert_range[None, None, :]
+    ids = expert_ids + (proj_cols[0, 0] * 0).astype(expert_ids.dtype)
+    picked = ids[:, :, None] == expert_range[None, None, :]
     chosen = jnp.sum(jnp.where(picked, logits[:, None, :], 0.0), axis=2)
     raised = jnp.exp(chosen)
     gates = raised / jnp.sum(raised, axis=1, keepdims=True)

time: 250 us -> 250 us (level)
  waiting for transfers between devices: 94.7 us -> 101 us
  other arithmetic: 15.1 us -> 9.99 us
    all_gather x1, waiting for transfers between devices: 3.13 us -> 8.74 us  [turned_gather(): out = lax.all_gather(both, axis, axis=0, tiled=True)]
    another operation x4, other arithmetic: 3.38 us -> 0.71 us
  transfers between devices with their start and end apart: 10 -> 10, of which waited for: 9 -> 10; matrix products, arithmetic and copies ran while one was open for 16% -> 13% of each run, Pallas kernels for 0% -> 0%
where the time goes in v11:
time: 250 us; the launch traced here: 249 us
  waiting for transfers between devices  101 us (40%)
  starting transfers between devices  46.9 us (19%)
  blocking collectives  44.2 us (18%)
  matrix products  16.3 us (7%)
  between operations  15.4 us (6%)
  local copies, waits for them, and re-layouts  14.8 us (6%)
  other arithmetic  9.99 us (4%)
    all_to_all x1, blocking collectives, pair_collect(): lax.all_to_all(copies, axis, 0, 0, tiled=True, axis_index_groups=core_gro...  44.2 us
    all_gather x2, waiting for transfers between devices, pair_gather(): lax.all_gather(array, axis, axis=0, axis_index_groups=core_groups(axis))  34.7 us
    all_to_all x1, waiting for transfers between devices, per_device(): lax.all_to_all(result, 'expert', split_axis=0, concat_axis=0, tiled=True)  26.5 us
    ppermute x3, starting transfers between devices, with_sibling(): lax.ppermute(blocks, axis, [(i, i ^ 1) for i in range(lax.axis_size(axis))])  19.2 us
    all_to_all x1, starting transfers between devices, per_device(): lax.all_to_all(outgoing, 'expert', split_axis=0, concat_axis=0, tiled=True)  9.68 us
    all_to_all x1, waiting for transfers between devices, per_device(): lax.all_to_all(outgoing, 'expert', split_axis=0, concat_axis=0, tiled=True)  9.27 us
    all_to_all x1, waiting for transfers between devices, per_device(): lax.all_to_all(proj_cols, 'dp', split_axis=0, concat_axis=1, tiled=True)  8.85 us
    all_gather x1, waiting for transfers between devices, turned_gather(): out = lax.all_gather(both, axis, axis=0, tiled=True)  8.74 us
  transfers between devices with their start and end apart: 10, of which 10 were waited for; matrix products, arithmetic and copies ran while one was open for 13% of the time, Pallas kernels for 0%

profile of v11, /device:TPU:1, one launch (start us, length us, event | category | flops | bytes accessed | tf_op | source)
XLA Modules:
  0.0 248.7 jit_solution(5507769714941726172)
XLA Ops:
  6.5 1.2 copy.43
  7.7 1.8 pad_maximum_fusion.3
  9.7 44.2 %all_to_all.41 = bf16[8,32,2048]{2,1,0:T(8,128)(2,1)S(1)} all-to-all(bf16[8,32,2048]{2,1,0:T(8,128)(2,1)S(1)} %broadcast_in_dim.26), channel_id=1, replica_groups={{0,64,128,192,256,320,384,448},{32,96,160,224,288,352,416,480},{1,65,12..., dimensions={0} | all-to-all | bytes 2097152 | tf_op jit(solution)/shard_map/all_to_all | solution.py:28
  53.9 5.5 %collective-permute-start = (bf16[8,32,2048]{2,1,0:T(8,128)(2,1)S(1)}, bf16[8,32,2048]{2,1,0:T(8,128)(2,1)S(1)}, u32[]{:S(2)}, u32[]{:S(2)}) collective-permute-start(bf16[8,32,2048]{2,1,0:T(8,128)(2,1)S(1)} %all_to_all.41), channel_id=1, source_target_pairs={{0,32},{32,0},{64,96},{96,64},{128,160},{160,128},{192,224},{224,1... | collective-permute-start | bytes 3145736 | tf_op jit(solution)/shard_map/ppermute | solution.py:15
  59.5 2.3 collective-permute-done
  63.0 1.4 convolution_convert_fusion.1
  64.4 1.2 slice.41
  66.1 3.7 %all-to-all-start.1 = ((bf16[16,32,128]{2,1,0:T(8,128)(2,1)}), bf16[16,32,128]{2,1,0:T(8,128)(2,1)S(1)}, u32[]{:S(2)}, u32[]{:S(2)}) async-start(bf16[16,32,128]{2,1,0:T(8,128)(2,1)} %bitcast.4), calls=%async_computation.1 | async-start | bytes 262144 | tf_op jit(solution)/shard_map/all_to_all | solution.py:91
  71.6 8.8 %all-to-all-done.1 = bf16[16,32,128]{2,1,0:T(8,128)(2,1)S(1)} async-done(((bf16[16,32,128]{2,1,0:T(8,128)(2,1)}), bf16[16,32,128]{2,1,0:T(8,128)(2,1)S(1)}, u32[]{:S(2)}, u32[]{:S(2)}) %all-to-all-start.1) | async-done | bytes 131104 | tf_op jit(solution)/shard_map/all_to_all | solution.py:91
  81.3 1.6 reshape.118
  84.7 8.7 %all-gather.6.cloned.1.call-done = bf16[2048,2112]{1,0:T(8,128)(2,1)} async-done(((bf16[128,2112]{1,0:T(8,128)(2,1)}), bf16[2048,2112]{1,0:T(8,128)(2,1)}) %all-gather.6.cloned.1.call-update) | async-done | bytes 8650768 | tf_op jit(solution)/shard_map/all_gather | solution.py:53
  93.4 1.2 slice.46
  96.1 9.7 %all-to-all-start.2 = ((bf16[32,12,2048]{2,1,0:T(8,128)(2,1)}), bf16[32,12,2048]{2,1,0:T(8,128)(2,1)S(1)}, u32[]{:S(2)}, u32[]{:S(2)}) async-start(bf16[32,12,2048]{2,1,0:T(8,128)(2,1)} %reshape.118), calls=%async_computation.2 | async-start | bytes 4194304 | tf_op jit(solution)/shard_map/all_to_all | solution.py:114
  105.8 26.9 %all-gather.8.cloned.1.call-done = bf16[256,2048]{1,0:T(8,128)(2,1)} async-done(((bf16[32,2048]{1,0:T(8,128)(2,1)}), bf16[256,2048]{1,0:T(8,128)(2,1)}) %all-gather.8.cloned.1.call-update) | async-done | bytes 1048592 | tf_op jit(solution)/shard_map/all_gather | solution.py:22
  132.8 6.4 %collective-permute-start.1 = (bf16[8,32,2048]{2,1,0:T(8,128)(2,1)}, bf16[8,32,2048]{2,1,0:T(8,128)(2,1)S(1)}, u32[]{:S(2)}, u32[]{:S(2)}) collective-permute-start(bf16[8,32,2048]{2,1,0:T(8,128)(2,1)} %bitcast.95), channel_id=1, source_target_pairs={{0,32},{32,0},{64,96},{96,64},{128,160},{160,128},{192,224},{224,1... | collective-permute-start | bytes 3145736 | tf_op jit(solution)/shard_map/ppermute | solution.py:15
  139.2 2.5 collective-permute-done.1
  141.6 1.4 pad_maximum_fusion.2
  145.4 9.3 %all-to-all-done.2 = bf16[32,12,2048]{2,1,0:T(8,128)(2,1)S(1)} async-done(((bf16[32,12,2048]{2,1,0:T(8,128)(2,1)}), bf16[32,12,2048]{2,1,0:T(8,128)(2,1)S(1)}, u32[]{:S(2)}, u32[]{:S(2)}) %all-to-all-start.2) | async-done | bytes 1572896 | tf_op jit(solution)/shard_map/all_to_all | solution.py:114
  154.7 1.3 reshape.119
  156.0 5.8 %fusion = f32[384,1408]{1,0:T(8,128)S(1)} fusion(bf16[384,2048]{1,0:T(8,128)(2,1)} %reshape.119, bf16[2048,2112]{1,0:T(8,128)(2,1)} %all-gather.6.cloned.1.call-done), kind=kOutput, calls=%fused_computation | convolution fusion | flops 2214592512 | bytes 9502720 | tf_op jit(solution)/shard_map/dot_general | solution.py:117
  161.8 3.3 %fusion.3 = bf16[384,2048]{1,0:T(8,128)(2,1)S(1)} fusion(bf16[2048,2112]{1,0:T(8,128)(2,1)} %all-gather.6.cloned.1.call-done, f32[384,1408]{1,0:T(8,128)S(1)} %fusion), kind=kOutput, calls=%fused_computation.8 | convolution fusion | flops 1109704704 | bytes 7077888 | tf_op jit(solution)/shard_map/dot_general | solution.py:119
  165.2 1.5 reshape.122
  166.7 7.5 %all-to-all-start.3 = ((bf16[32,12,2048]{2,1,0:T(8,128)(2,1)}), bf16[32,12,2048]{2,1,0:T(8,128)(2,1)S(1)}, u32[]{:S(2)}, u32[]{:S(2)}) async-start(bf16[32,12,2048]{2,1,0:T(8,128)(2,1)} %reshape.122), calls=%async_computation.3 | async-start | bytes 4194304 | tf_op jit(solution)/shard_map/all_to_all | solution.py:121
  174.2 7.8 %all-gather.10.cloned.1.call-done = bf16[4096,176]{0,1:T(8,128)(2,1)} async-done(((bf16[512,176]{0,1:T(8,128)(2,1)}), bf16[4096,176]{0,1:T(8,128)(2,1)}) %all-gather.10.cloned.1.call-update) | async-done | bytes 1441808 | tf_op jit(solution)/shard_map/all_gather | solution.py:22
  182.0 1.6 copy.60
  183.6 7.3 %collective-permute-start.2 = (bf16[8,512,176]{1,2,0:T(8,128)(2,1)S(1)}, bf16[8,512,176]{1,2,0:T(8,128)(2,1)S(1)}, u32[]{:S(2)}, u32[]{:S(2)}) collective-permute-start(bf16[8,512,176]{1,2,0:T(8,128)(2,1)S(1)} %bitcast.92), channel_id=1, source_target_pairs={{0,32},{32,0},{64,96},{96,64},{128,160},{160,128},{192,224},{224,1... | collective-permute-start | bytes 4325384 | tf_op jit(solution)/shard_map/ppermute | solution.py:15
  195.0 1.6 convolution_convert_fusion.2
  196.6 26.5 %all-to-all-done.3 = bf16[32,12,2048]{2,1,0:T(8,128)(2,1)S(1)} async-done(((bf16[32,12,2048]{2,1,0:T(8,128)(2,1)}), bf16[32,12,2048]{2,1,0:T(8,128)(2,1)S(1)}, u32[]{:S(2)}, u32[]{:S(2)}) %all-to-all-start.3) | async-done | bytes 1572896 | tf_op jit(solution)/shard_map/all_to_all | solution.py:121
  223.1 6.7 %all-to-all-start.4 = ((bf16[16,32,128]{2,1,0:T(8,128)(2,1)}), bf16[16,32,128]{2,1,0:T(8,128)(2,1)}, u32[]{:S(2)}, u32[]{:S(2)}) async-start(bf16[16,32,128]{2,1,0:T(8,128)(2,1)} %bitcast.99), calls=%async_computation.4 | async-start | bytes 262144 | tf_op jit(solution)/shard_map/all_to_all | solution.py:138
  230.5 1.3 reshape.123
  231.8 7.2 %all-to-all-done.4 = bf16[16,32,128]{2,1,0:T(8,128)(2,1)} async-done(((bf16[16,32,128]{2,1,0:T(8,128)(2,1)}), bf16[16,32,128]{2,1,0:T(8,128)(2,1)}, u32[]{:S(2)}, u32[]{:S(2)}) %all-to-all-start.4) | async-done | bytes 131104 | tf_op jit(solution)/shard_map/all_to_all | solution.py:138
  239.0 2.4 multiply_reduce_fusion
  (75 shorter events, 13.7 us)
Async XLA Ops:
  6.5 137.1 %copy-start = (bf16[2048,2,176]{0,2,1:T(8,128)(2,1)S(1)}, bf16[2048,2,176]{0,2,1:T(8,128)(2,1)}, u32[]{:S(2)}) copy-start(bf16[2048,2,176]{0,2,1:T(8,128)(2,1)} %param.21) | copy-start | bytes 4325380
  6.5 3.0 %copy-start.6 = (bf16[32,2048]{1,0:T(8,128)(2,1)S(1)}, bf16[32,2048]{1,0:T(8,128)(2,1)}, u32[]{:S(2)}) copy-start(bf16[32,2048]{1,0:T(8,128)(2,1)} %param.13) | copy-start | bytes 393220
  6.5 86.9 %all-gather.6.cloned.1.call-start = ((), (), s32[]{:S(2)}) async-start(), calls=%async_computation.5 | async-start | bytes 9469952 | tf_op jit(solution)/shard_map/all_gather | solution.py:53
  53.9 7.8 %collective-permute-start = (bf16[8,32,2048]{2,1,0:T(8,128)(2,1)S(1)}, bf16[8,32,2048]{2,1,0:T(8,128)(2,1)S(1)}, u32[]{:S(2)}, u32[]{:S(2)}) collective-permute-start(bf16[8,32,2048]{2,1,0:T(8,128)(2,1)S(1)} %all_to_all.41), channel_id=1, source_target_pairs={{0,32},{32,0},{64,96},{96,64},{128,160},{160,128},{192,224},{224,1... | collective-permute-start | bytes 3145736 | tf_op jit(solution)/shard_map/ppermute | solution.py:15
  62.0 1.0 copy-start.5
  62.5 7.3 %copy-start.10 = (s32[32,6]{0,1:T(8,128)S(1)}, s32[32,6]{0,1:T(8,128)}, u32[]{:S(2)}) copy-start(s32[32,6]{0,1:T(8,128)} %param.17) | copy-start | bytes 2308
  62.6 7.3 %copy-start.13 = (s32[32]{0:T(128)S(1)}, s32[32]{0:T(128)}, u32[]{:S(2)}) copy-start(s32[32]{0:T(128)} %param.18) | copy-start | bytes 388
  62.6 17.9 %copy-start.7 = (bf16[32,2048]{1,0:T(8,128)(2,1)S(1)}, bf16[32,2048]{1,0:T(8,128)(2,1)}, u32[]{:S(2)}) copy-start(bf16[32,2048]{1,0:T(8,128)(2,1)} %param.12) | copy-start | bytes 393220
  62.6 18.1 %copy-start.8 = (f32[2048]{0:T(1024)S(1)}, f32[2048]{0:T(1024)}, u32[]{:S(2)}) copy-start(f32[2048]{0:T(1024)} %param.15) | copy-start | bytes 24580
  66.1 14.4 %all-to-all-start.1 = ((bf16[16,32,128]{2,1,0:T(8,128)(2,1)}), bf16[16,32,128]{2,1,0:T(8,128)(2,1)S(1)}, u32[]{:S(2)}, u32[]{:S(2)}) async-start(bf16[16,32,128]{2,1,0:T(8,128)(2,1)} %bitcast.4), calls=%async_computation.1 | async-start | bytes 262144 | tf_op jit(solution)/shard_map/all_to_all | solution.py:91
  69.8 63.0 %all-gather.8.cloned.1.call-start = ((), (), s32[]{:S(2)}) async-start(), calls=%async_computation.6 | async-start | bytes 1179648 | tf_op jit(solution)/shard_map/all_gather | solution.py:22
  80.6 14.7 %copy-start.2 = (bf16[32,2048]{1,0:T(8,128)(2,1)}, bf16[32,2048]{1,0:T(8,128)(2,1)S(1)}, u32[]{:S(2)}) copy-start(bf16[32,2048]{1,0:T(8,128)(2,1)S(1)} %get-tuple-element.6) | copy-start | bytes 393220
  80.6 14.6 %copy-start.11 = (f32[32]{0:T(128)}, f32[32]{0:T(128)S(1)}, u32[]{:S(2)}) copy-start(f32[32]{0:T(128)S(1)} %add_rsqrt_fusion.1) | copy-start | bytes 388
  96.1 58.6 %all-to-all-start.2 = ((bf16[32,12,2048]{2,1,0:T(8,128)(2,1)}), bf16[32,12,2048]{2,1,0:T(8,128)(2,1)S(1)}, u32[]{:S(2)}, u32[]{:S(2)}) async-start(bf16[32,12,2048]{2,1,0:T(8,128)(2,1)} %reshape.118), calls=%async_computation.2 | async-start | bytes 4194304 | tf_op jit(solution)/shard_map/all_to_all | solution.py:114
  105.8 76.3 %all-gather.10.cloned.1.call-start = ((), (), s32[]{:S(2)}) async-start(), calls=%async_computation.7 | async-start | bytes 1622016 | tf_op jit(solution)/shard_map/all_gather | solution.py:22
  132.8 8.9 %collective-permute-start.1 = (bf16[8,32,2048]{2,1,0:T(8,128)(2,1)}, bf16[8,32,2048]{2,1,0:T(8,128)(2,1)S(1)}, u32[]{:S(2)}, u32[]{:S(2)}) collective-permute-start(bf16[8,32,2048]{2,1,0:T(8,128)(2,1)} %bitcast.95), channel_id=1, source_target_pairs={{0,32},{32,0},{64,96},{96,64},{128,160},{160,128},{192,224},{224,1... | collective-permute-start | bytes 3145736 | tf_op jit(solution)/shard_map/ppermute | solution.py:15
  166.7 56.4 %all-to-all-start.3 = ((bf16[32,12,2048]{2,1,0:T(8,128)(2,1)}), bf16[32,12,2048]{2,1,0:T(8,128)(2,1)S(1)}, u32[]{:S(2)}, u32[]{:S(2)}) async-start(bf16[32,12,2048]{2,1,0:T(8,128)(2,1)} %reshape.122), calls=%async_computation.3 | async-start | bytes 4194304 | tf_op jit(solution)/shard_map/all_to_all | solution.py:121
  182.0 8.9 %copy-start.3 = (bf16[32,2048]{1,0:T(8,128)(2,1)S(1)}, bf16[32,2048]{1,0:T(8,128)(2,1)}, u32[]{:S(2)}) copy-start(bf16[32,2048]{1,0:T(8,128)(2,1)} %copy-done.2) | copy-start | bytes 393220
  182.0 8.9 %copy-start.12 = (f32[32]{0:T(128)S(1)}, f32[32]{0:T(128)}, u32[]{:S(2)}) copy-start(f32[32]{0:T(128)} %copy-done.11) | copy-start | bytes 388
  182.0 8.9 %copy-start.14 = (bf16[2048,32]{0,1:T(8,128)(2,1)S(1)}, bf16[2048,32]{0,1:T(8,128)(2,1)}, u32[]{:S(2)}) copy-start(bf16[2048,32]{0,1:T(8,128)(2,1)} %param.16) | copy-start | bytes 393220
  182.0 9.4 %copy-start.1 = (bf16[4096,176]{0,1:T(8,128)(2,1)S(1)}, bf16[4096,176]{0,1:T(8,128)(2,1)}, u32[]{:S(2)}) copy-start(bf16[4096,176]{0,1:T(8,128)(2,1)} %all-gather.10.cloned.1.call-done) | copy-start | bytes 4325380
  183.6 9.9 %collective-permute-start.2 = (bf16[8,512,176]{1,2,0:T(8,128)(2,1)S(1)}, bf16[8,512,176]{1,2,0:T(8,128)(2,1)S(1)}, u32[]{:S(2)}, u32[]{:S(2)}) collective-permute-start(bf16[8,512,176]{1,2,0:T(8,128)(2,1)S(1)} %bitcast.92), channel_id=1, source_target_pairs={{0,32},{32,0},{64,96},{96,64},{128,160},{160,128},{192,224},{224,1... | collective-permute-start | bytes 4325384 | tf_op jit(solution)/shard_map/ppermute | solution.py:15
  193.9 1.1 copy-start.4
  223.1 16.0 %all-to-all-start.4 = ((bf16[16,32,128]{2,1,0:T(8,128)(2,1)}), bf16[16,32,128]{2,1,0:T(8,128)(2,1)}, u32[]{:S(2)}, u32[]{:S(2)}) async-start(bf16[16,32,128]{2,1,0:T(8,128)(2,1)} %bitcast.99), calls=%async_computation.4 | async-start | bytes 262144 | tf_op jit(solution)/shard_map/all_to_all | solution.py:138
  230.5 10.9 %copy-start.9 = (f32[2048]{0:T(1024)S(1)}, f32[2048]{0:T(1024)}, u32[]{:S(2)}) copy-start(f32[2048]{0:T(1024)} %param.23) | copy-start | bytes 24580
Sparse Core Ops, SparseCore 0:
  9.7 83.6 all-gather.5
  96.2 36.5 all-gather.7
  145.5 36.4 all-gather.9

commit v12 on v11

--- a/solution.py
+++ b/solution.py
@@ -107,21 +107,24 @@
     select = jnp.any(placed.reshape(rows, choose, experts * capacity), axis=1).astype(jnp.bfloat16)
     outgoing = jnp.einsum("rs,rd->sd", select, normed, preferred_element_type=jnp.float32)
     outgoing = outgoing.astype(jnp.bfloat16).reshape(experts, capacity, width)
-    gate_up_all, down_all = turned_gather((expert_gate_up, expert_down), "dp", (1, 2))
-    gate_up_full = gate_up_all[0]
-    down_full = down_all[0]
-    hidden_units = gate_up_full.shape[1] // 2
+    hidden_units = expert_down.shape[1]
+    weights_part = jnp.concatenate([expert_gate_up[0], expert_down[0].T], axis=1)
+    weights_full = lax.all_gather(weights_part, "dp", axis=0, tiled=True)
+    gate_up_full = weights_full[:, : 2 * hidden_units]
+    down_turned_full = weights_full[:, 2 * hidden_units :]
     received = lax.all_to_all(outgoing, "expert", split_axis=0, concat_axis=0, tiled=True)
     sources, count, _ = received.shape
     flat = received.reshape(sources * count, width)
     both = jnp.dot(flat, gate_up_full, preferred_element_type=jnp.float32)
     active = (jax.nn.silu(both[:, :hidden_units]) * both[:, hidden_units:]).astype(jnp.bfloat16)
-    result = jnp.dot(active, down_full, preferred_element_type=jnp.float32).astype(jnp.bfloat16)
+    result = lax.dot_general(
+        active, down_turned_full, (((1,), (1,)), ((), ())), preferred_element_type=jnp.float32
+    ).astype(jnp.bfloat16)
     result = result.reshape(sources, count, width)
     returned = lax.all_to_all(result, "expert", split_axis=0, concat_axis=0, tiled=True)
     shared_units = shared_gate_up.shape[2]
     shared_pair = shared_gate_up.reshape(width, 2 * shared_units)
-    normed_shared = normed + (gate_up_full[0, 0] * 0 + outgoing[0, 0, 0] * 0).astype(normed.dtype)
+    normed_shared = normed + (weights_full[0, 0] * 0 + outgoing[0, 0, 0] * 0).astype(normed.dtype)
     both = jnp.dot(
         in_order(pair_gather(normed_shared, "dp"), 0),
         shared_pair,

time: 250 us -> 250 us (level)
  no operation moved by 1% of the time
where the time goes in v12:
time: 250 us; the launch traced here: 249 us
  waiting for transfers between devices  101 us (40%)
  starting transfers between devices  46.9 us (19%)
  blocking collectives  44.2 us (18%)
  matrix products  16.3 us (7%)
  between operations  15.4 us (6%)
  local copies, waits for them, and re-layouts  14.8 us (6%)
  other arithmetic  9.99 us (4%)
    all_to_all x1, blocking collectives, pair_collect(): lax.all_to_all(copies, axis, 0, 0, tiled=True, axis_index_groups=core_gro...  44.2 us
    all_gather x2, waiting for transfers between devices, pair_gather(): lax.all_gather(array, axis, axis=0, axis_index_groups=core_groups(axis))  34.7 us
    all_to_all x1, waiting for transfers between devices, per_device(): lax.all_to_all(result, 'expert', split_axis=0, concat_axis=0, tiled=True)  26.5 us
    ppermute x3, starting transfers between devices, with_sibling(): lax.ppermute(blocks, axis, [(i, i ^ 1) for i in range(lax.axis_size(axis))])  19.2 us
    all_to_all x1, starting transfers between devices, per_device(): lax.all_to_all(outgoing, 'expert', split_axis=0, concat_axis=0, tiled=True)  9.68 us
    all_to_all x1, waiting for transfers between devices, per_device(): lax.all_to_all(outgoing, 'expert', split_axis=0, concat_axis=0, tiled=True)  9.27 us
    all_to_all x1, waiting for transfers between devices, per_device(): lax.all_to_all(proj_cols, 'dp', split_axis=0, concat_axis=1, tiled=True)  8.85 us
    all_gather x1, waiting for transfers between devices, per_device(): weights_full = lax.all_gather(weights_part, 'dp', axis=0, tiled=True)  8.74 us
  transfers between devices with their start and end apart: 10, of which 10 were waited for; matrix products, arithmetic and copies ran while one was open for 13% of the time, Pallas kernels for 0%

profile of v12, /device:TPU:1, one launch (start us, length us, event | category | flops | bytes accessed | tf_op | source)
XLA Modules:
  0.0 248.7 jit_solution(5507769714941726172)
XLA Ops:
  6.5 1.2 copy.43
  7.7 1.8 pad_maximum_fusion.3
  9.7 44.2 %all_to_all.41 = bf16[8,32,2048]{2,1,0:T(8,128)(2,1)S(1)} all-to-all(bf16[8,32,2048]{2,1,0:T(8,128)(2,1)S(1)} %broadcast_in_dim.26), channel_id=1, replica_groups={{0,64,128,192,256,320,384,448},{32,96,160,224,288,352,416,480},{1,65,12..., dimensions={0} | all-to-all | bytes 2097152 | tf_op jit(solution)/shard_map/all_to_all | solution.py:28
  53.9 5.5 %collective-permute-start = (bf16[8,32,2048]{2,1,0:T(8,128)(2,1)S(1)}, bf16[8,32,2048]{2,1,0:T(8,128)(2,1)S(1)}, u32[]{:S(2)}, u32[]{:S(2)}) collective-permute-start(bf16[8,32,2048]{2,1,0:T(8,128)(2,1)S(1)} %all_to_all.41), channel_id=1, source_target_pairs={{0,32},{32,0},{64,96},{96,64},{128,160},{160,128},{192,224},{224,1... | collective-permute-start | bytes 3145736 | tf_op jit(solution)/shard_map/ppermute | solution.py:15
  59.5 2.3 collective-permute-done
  63.0 1.4 convolution_convert_fusion.1
  64.4 1.2 slice.48
  66.1 3.7 %all-to-all-start.1 = ((bf16[16,32,128]{2,1,0:T(8,128)(2,1)}), bf16[16,32,128]{2,1,0:T(8,128)(2,1)S(1)}, u32[]{:S(2)}, u32[]{:S(2)}) async-start(bf16[16,32,128]{2,1,0:T(8,128)(2,1)} %bitcast.4), calls=%async_computation.1 | async-start | bytes 262144 | tf_op jit(solution)/shard_map/all_to_all | solution.py:91
  71.6 8.8 %all-to-all-done.1 = bf16[16,32,128]{2,1,0:T(8,128)(2,1)S(1)} async-done(((bf16[16,32,128]{2,1,0:T(8,128)(2,1)}), bf16[16,32,128]{2,1,0:T(8,128)(2,1)S(1)}, u32[]{:S(2)}, u32[]{:S(2)}) %all-to-all-start.1) | async-done | bytes 131104 | tf_op jit(solution)/shard_map/all_to_all | solution.py:91
  81.3 1.6 reshape.112
  84.7 8.7 %all-gather.6.cloned.1.call-done = bf16[2048,2112]{1,0:T(8,128)(2,1)} async-done(((bf16[128,2112]{1,0:T(8,128)(2,1)}), bf16[2048,2112]{1,0:T(8,128)(2,1)}) %all-gather.6.cloned.1.call-update) | async-done | bytes 8650768 | tf_op jit(solution)/shard_map/all_gather | solution.py:112
  93.4 1.2 slice.55
  96.1 9.7 %all-to-all-start.2 = ((bf16[32,12,2048]{2,1,0:T(8,128)(2,1)}), bf16[32,12,2048]{2,1,0:T(8,128)(2,1)S(1)}, u32[]{:S(2)}, u32[]{:S(2)}) async-start(bf16[32,12,2048]{2,1,0:T(8,128)(2,1)} %reshape.112), calls=%async_computation.2 | async-start | bytes 4194304 | tf_op jit(solution)/shard_map/all_to_all | solution.py:115
  105.8 26.9 %all-gather.8.cloned.1.call-done = bf16[256,2048]{1,0:T(8,128)(2,1)} async-done(((bf16[32,2048]{1,0:T(8,128)(2,1)}), bf16[256,2048]{1,0:T(8,128)(2,1)}) %all-gather.8.cloned.1.call-update) | async-done | bytes 1048592 | tf_op jit(solution)/shard_map/all_gather | solution.py:22
  132.8 6.4 %collective-permute-start.1 = (bf16[8,32,2048]{2,1,0:T(8,128)(2,1)}, bf16[8,32,2048]{2,1,0:T(8,128)(2,1)S(1)}, u32[]{:S(2)}, u32[]{:S(2)}) collective-permute-start(bf16[8,32,2048]{2,1,0:T(8,128)(2,1)} %bitcast.86), channel_id=1, source_target_pairs={{0,32},{32,0},{64,96},{96,64},{128,160},{160,128},{192,224},{224,1... | collective-permute-start | bytes 3145736 | tf_op jit(solution)/shard_map/ppermute | solution.py:15
  139.2 2.5 collective-permute-done.1
  141.6 1.4 pad_maximum_fusion.2
  145.4 9.3 %all-to-all-done.2 = bf16[32,12,2048]{2,1,0:T(8,128)(2,1)S(1)} async-done(((bf16[32,12,2048]{2,1,0:T(8,128)(2,1)}), bf16[32,12,2048]{2,1,0:T(8,128)(2,1)S(1)}, u32[]{:S(2)}, u32[]{:S(2)}) %all-to-all-start.2) | async-done | bytes 1572896 | tf_op jit(solution)/shard_map/all_to_all | solution.py:115
  154.7 1.3 reshape.113
  156.0 5.8 %fusion = f32[384,1408]{1,0:T(8,128)S(1)} fusion(bf16[384,2048]{1,0:T(8,128)(2,1)} %reshape.113, bf16[2048,2112]{1,0:T(8,128)(2,1)} %all-gather.6.cloned.1.call-done), kind=kOutput, calls=%fused_computation | convolution fusion | flops 2214592512 | bytes 9502720 | tf_op jit(solution)/shard_map/dot_general | solution.py:118
  161.8 3.3 %fusion.4 = bf16[384,2048]{1,0:T(8,128)(2,1)S(1)} fusion(bf16[2048,2112]{1,0:T(8,128)(2,1)} %all-gather.6.cloned.1.call-done, f32[384,1408]{1,0:T(8,128)S(1)} %fusion), kind=kOutput, calls=%fused_computation.8 | convolution fusion | flops 1109704704 | bytes 7077888 | tf_op jit(solution)/shard_map/dot_general | solution.py:120
  165.2 1.5 reshape.114
  166.7 7.5 %all-to-all-start.3 = ((bf16[32,12,2048]{2,1,0:T(8,128)(2,1)}), bf16[32,12,2048]{2,1,0:T(8,128)(2,1)S(1)}, u32[]{:S(2)}, u32[]{:S(2)}) async-start(bf16[32,12,2048]{2,1,0:T(8,128)(2,1)} %reshape.114), calls=%async_computation.3 | async-start | bytes 4194304 | tf_op jit(solution)/shard_map/all_to_all | solution.py:124
  174.2 7.8 %all-gather.10.cloned.1.call-done = bf16[4096,176]{0,1:T(8,128)(2,1)} async-done(((bf16[512,176]{0,1:T(8,128)(2,1)}), bf16[4096,176]{0,1:T(8,128)(2,1)}) %all-gather.10.cloned.1.call-update) | async-done | bytes 1441808 | tf_op jit(solution)/shard_map/all_gather | solution.py:22
  182.0 1.6 copy.60
  183.6 7.3 %collective-permute-start.2 = (bf16[8,512,176]{1,2,0:T(8,128)(2,1)S(1)}, bf16[8,512,176]{1,2,0:T(8,128)(2,1)S(1)}, u32[]{:S(2)}, u32[]{:S(2)}) collective-permute-start(bf16[8,512,176]{1,2,0:T(8,128)(2,1)S(1)} %bitcast.83), channel_id=1, source_target_pairs={{0,32},{32,0},{64,96},{96,64},{128,160},{160,128},{192,224},{224,1... | collective-permute-start | bytes 4325384 | tf_op jit(solution)/shard_map/ppermute | solution.py:15
  195.0 1.6 convolution_convert_fusion.2
  196.6 26.5 %all-to-all-done.3 = bf16[32,12,2048]{2,1,0:T(8,128)(2,1)S(1)} async-done(((bf16[32,12,2048]{2,1,0:T(8,128)(2,1)}), bf16[32,12,2048]{2,1,0:T(8,128)(2,1)S(1)}, u32[]{:S(2)}, u32[]{:S(2)}) %all-to-all-start.3) | async-done | bytes 1572896 | tf_op jit(solution)/shard_map/all_to_all | solution.py:124
  223.1 6.7 %all-to-all-start.4 = ((bf16[16,32,128]{2,1,0:T(8,128)(2,1)}), bf16[16,32,128]{2,1,0:T(8,128)(2,1)}, u32[]{:S(2)}, u32[]{:S(2)}) async-start(bf16[16,32,128]{2,1,0:T(8,128)(2,1)} %bitcast.90), calls=%async_computation.4 | async-start | bytes 262144 | tf_op jit(solution)/shard_map/all_to_all | solution.py:141
  230.5 1.3 reshape.115
  231.8 7.2 %all-to-all-done.4 = bf16[16,32,128]{2,1,0:T(8,128)(2,1)} async-done(((bf16[16,32,128]{2,1,0:T(8,128)(2,1)}), bf16[16,32,128]{2,1,0:T(8,128)(2,1)}, u32[]{:S(2)}, u32[]{:S(2)}) %all-to-all-start.4) | async-done | bytes 131104 | tf_op jit(solution)/shard_map/all_to_all | solution.py:141
  239.0 2.4 multiply_reduce_fusion
  (75 shorter events, 13.7 us)
Async XLA Ops:
  6.5 137.1 %copy-start = (bf16[2048,2,176]{0,2,1:T(8,128)(2,1)S(1)}, bf16[2048,2,176]{0,2,1:T(8,128)(2,1)}, u32[]{:S(2)}) copy-start(bf16[2048,2,176]{0,2,1:T(8,128)(2,1)} %param.21) | copy-start | bytes 4325380
  6.5 3.0 %copy-start.6 = (bf16[32,2048]{1,0:T(8,128)(2,1)S(1)}, bf16[32,2048]{1,0:T(8,128)(2,1)}, u32[]{:S(2)}) copy-start(bf16[32,2048]{1,0:T(8,128)(2,1)} %param.13) | copy-start | bytes 393220
  6.5 86.9 %all-gather.6.cloned.1.call-start = ((), (), s32[]{:S(2)}) async-start(), calls=%async_computation.5 | async-start | bytes 9469952 | tf_op jit(solution)/shard_map/all_gather | solution.py:112
  53.9 7.8 %collective-permute-start = (bf16[8,32,2048]{2,1,0:T(8,128)(2,1)S(1)}, bf16[8,32,2048]{2,1,0:T(8,128)(2,1)S(1)}, u32[]{:S(2)}, u32[]{:S(2)}) collective-permute-start(bf16[8,32,2048]{2,1,0:T(8,128)(2,1)S(1)} %all_to_all.41), channel_id=1, source_target_pairs={{0,32},{32,0},{64,96},{96,64},{128,160},{160,128},{192,224},{224,1... | collective-permute-start | bytes 3145736 | tf_op jit(solution)/shard_map/ppermute | solution.py:15
  62.0 1.0 copy-start.5
  62.5 7.3 %copy-start.10 = (s32[32,6]{0,1:T(8,128)S(1)}, s32[32,6]{0,1:T(8,128)}, u32[]{:S(2)}) copy-start(s32[32,6]{0,1:T(8,128)} %param.17) | copy-start | bytes 2308
  62.6 7.3 %copy-start.13 = (s32[32]{0:T(128)S(1)}, s32[32]{0:T(128)}, u32[]{:S(2)}) copy-start(s32[32]{0:T(128)} %param.18) | copy-start | bytes 388
  62.6 17.9 %copy-start.7 = (bf16[32,2048]{1,0:T(8,128)(2,1)S(1)}, bf16[32,2048]{1,0:T(8,128)(2,1)}, u32[]{:S(2)}) copy-start(bf16[32,2048]{1,0:T(8,128)(2,1)} %param.12) | copy-start | bytes 393220
  62.6 18.1 %copy-start.8 = (f32[2048]{0:T(1024)S(1)}, f32[2048]{0:T(1024)}, u32[]{:S(2)}) copy-start(f32[2048]{0:T(1024)} %param.15) | copy-start | bytes 24580
  66.1 14.4 %all-to-all-start.1 = ((bf16[16,32,128]{2,1,0:T(8,128)(2,1)}), bf16[16,32,128]{2,1,0:T(8,128)(2,1)S(1)}, u32[]{:S(2)}, u32[]{:S(2)}) async-start(bf16[16,32,128]{2,1,0:T(8,128)(2,1)} %bitcast.4), calls=%async_computation.1 | async-start | bytes 262144 | tf_op jit(solution)/shard_map/all_to_all | solution.py:91
  69.8 63.0 %all-gather.8.cloned.1.call-start = ((), (), s32[]{:S(2)}) async-start(), calls=%async_computation.6 | async-start | bytes 1179648 | tf_op jit(solution)/shard_map/all_gather | solution.py:22
  80.6 14.7 %copy-start.2 = (bf16[32,2048]{1,0:T(8,128)(2,1)}, bf16[32,2048]{1,0:T(8,128)(2,1)S(1)}, u32[]{:S(2)}) copy-start(bf16[32,2048]{1,0:T(8,128)(2,1)S(1)} %get-tuple-element.6) | copy-start | bytes 393220
  80.6 14.6 %copy-start.11 = (f32[32]{0:T(128)}, f32[32]{0:T(128)S(1)}, u32[]{:S(2)}) copy-start(f32[32]{0:T(128)S(1)} %add_rsqrt_fusion.1) | copy-start | bytes 388
  96.1 58.6 %all-to-all-start.2 = ((bf16[32,12,2048]{2,1,0:T(8,128)(2,1)}), bf16[32,12,2048]{2,1,0:T(8,128)(2,1)S(1)}, u32[]{:S(2)}, u32[]{:S(2)}) async-start(bf16[32,12,2048]{2,1,0:T(8,128)(2,1)} %reshape.112), calls=%async_computation.2 | async-start | bytes 4194304 | tf_op jit(solution)/shard_map/all_to_all | solution.py:115
  105.8 76.3 %all-gather.10.cloned.1.call-start = ((), (), s32[]{:S(2)}) async-start(), calls=%async_computation.7 | async-start | bytes 1622016 | tf_op jit(solution)/shard_map/all_gather | solution.py:22
  132.8 8.9 %collective-permute-start.1 = (bf16[8,32,2048]{2,1,0:T(8,128)(2,1)}, bf16[8,32,2048]{2,1,0:T(8,128)(2,1)S(1)}, u32[]{:S(2)}, u32[]{:S(2)}) collective-permute-start(bf16[8,32,2048]{2,1,0:T(8,128)(2,1)} %bitcast.86), channel_id=1, source_target_pairs={{0,32},{32,0},{64,96},{96,64},{128,160},{160,128},{192,224},{224,1... | collective-permute-start | bytes 3145736 | tf_op jit(solution)/shard_map/ppermute | solution.py:15
  166.7 56.4 %all-to-all-start.3 = ((bf16[32,12,2048]{2,1,0:T(8,128)(2,1)}), bf16[32,12,2048]{2,1,0:T(8,128)(2,1)S(1)}, u32[]{:S(2)}, u32[]{:S(2)}) async-start(bf16[32,12,2048]{2,1,0:T(8,128)(2,1)} %reshape.114), calls=%async_computation.3 | async-start | bytes 4194304 | tf_op jit(solution)/shard_map/all_to_all | solution.py:124
  182.0 8.9 %copy-start.3 = (bf16[32,2048]{1,0:T(8,128)(2,1)S(1)}, bf16[32,2048]{1,0:T(8,128)(2,1)}, u32[]{:S(2)}) copy-start(bf16[32,2048]{1,0:T(8,128)(2,1)} %copy-done.2) | copy-start | bytes 393220
  182.0 8.9 %copy-start.12 = (f32[32]{0:T(128)S(1)}, f32[32]{0:T(128)}, u32[]{:S(2)}) copy-start(f32[32]{0:T(128)} %copy-done.11) | copy-start | bytes 388
  182.0 8.9 %copy-start.14 = (bf16[2048,32]{0,1:T(8,128)(2,1)S(1)}, bf16[2048,32]{0,1:T(8,128)(2,1)}, u32[]{:S(2)}) copy-start(bf16[2048,32]{0,1:T(8,128)(2,1)} %param.16) | copy-start | bytes 393220
  182.0 9.4 %copy-start.1 = (bf16[4096,176]{0,1:T(8,128)(2,1)S(1)}, bf16[4096,176]{0,1:T(8,128)(2,1)}, u32[]{:S(2)}) copy-start(bf16[4096,176]{0,1:T(8,128)(2,1)} %all-gather.10.cloned.1.call-done) | copy-start | bytes 4325380
  183.6 9.9 %collective-permute-start.2 = (bf16[8,512,176]{1,2,0:T(8,128)(2,1)S(1)}, bf16[8,512,176]{1,2,0:T(8,128)(2,1)S(1)}, u32[]{:S(2)}, u32[]{:S(2)}) collective-permute-start(bf16[8,512,176]{1,2,0:T(8,128)(2,1)S(1)} %bitcast.83), channel_id=1, source_target_pairs={{0,32},{32,0},{64,96},{96,64},{128,160},{160,128},{192,224},{224,1... | collective-permute-start | bytes 4325384 | tf_op jit(solution)/shard_map/ppermute | solution.py:15
  193.9 1.1 copy-start.4
  223.1 16.0 %all-to-all-start.4 = ((bf16[16,32,128]{2,1,0:T(8,128)(2,1)}), bf16[16,32,128]{2,1,0:T(8,128)(2,1)}, u32[]{:S(2)}, u32[]{:S(2)}) async-start(bf16[16,32,128]{2,1,0:T(8,128)(2,1)} %bitcast.90), calls=%async_computation.4 | async-start | bytes 262144 | tf_op jit(solution)/shard_map/all_to_all | solution.py:141
  230.5 10.9 %copy-start.9 = (f32[2048]{0:T(1024)S(1)}, f32[2048]{0:T(1024)}, u32[]{:S(2)}) copy-start(f32[2048]{0:T(1024)} %param.23) | copy-start | bytes 24580
Sparse Core Ops, SparseCore 0:
  9.7 83.6 all-gather.5
  96.2 36.5 all-gather.7
  145.5 36.4 all-gather.9

commit v13 on v11

--- a/solution.py
+++ b/solution.py
@@ -135,9 +135,17 @@
         shared_down,
         preferred_element_type=jnp.float32,
     )
-    shared_out = lax.all_to_all(
-        out_cols.astype(jnp.bfloat16), "dp", split_axis=0, concat_axis=1, tiled=True
-    ).astype(jnp.float32)
+    groups = lax.axis_size("dp")
+    core = lax.axis_index("dp") % 2
+    by_owner = out_cols.astype(jnp.bfloat16).reshape(groups // 2, 2, rows, -1)
+    mine = lax.dynamic_index_in_dim(by_owner, core, axis=1, keepdims=False)
+    theirs = lax.dynamic_index_in_dim(by_owner, 1 - core, axis=1, keepdims=False)
+    swapped = lax.ppermute(theirs, "dp", [(i, i ^ 1) for i in range(groups)])
+    blocks = jnp.where(
+        core == 0, jnp.stack([mine, swapped], axis=2), jnp.stack([swapped, mine], axis=2)
+    )
+    blocks = lax.all_to_all(blocks, "dp", 0, 0, tiled=True, axis_index_groups=core_groups("dp"))
+    shared_out = jnp.moveaxis(blocks, 0, 1).reshape(rows, -1).astype(jnp.float32)
     weighted = jnp.sum(
         placed.reshape(rows, choose, experts * capacity) * gates[:, :, None], axis=1
     )

time: 250 us -> 293 us (1.17)
  waiting for transfers between devices: 101 us -> 140 us
  starting transfers between devices: 46.9 us -> 42.1 us
  local copies, waits for them, and re-layouts: 14.8 us -> 18.3 us
    all_to_all x1, waiting for transfers between devices: 9.27 us -> 45 us  [per_device(): lax.all_to_all(outgoing, 'expert', split_axis=0, concat_axis=0, tiled=True)]
    all_to_all x1, waiting for transfers between devices: 26.5 us -> 31.9 us  [per_device(): lax.all_to_all(result, 'expert', split_axis=0, concat_axis=0, tiled=True)]
    ppermute x3, starting transfers between devices: 19.2 us -> 15.5 us  [with_sibling(): lax.ppermute(blocks, axis, [(i, i ^ 1) for i in range(lax.axis_size(axis))])]
    ppermute x3, waiting for transfers between devices: 5.84 us -> 2.26 us  [with_sibling(): lax.ppermute(blocks, axis, [(i, i ^ 1) for i in range(lax.axis_size(axis))])]
  transfers between devices with their start and end apart: 10 -> 11, of which waited for: 10 -> 8; matrix products, arithmetic and copies ran while one was open for 13% -> 13% of each run, Pallas kernels for 0% -> 0%
where the time goes in v13:
time: 293 us; the launch traced here: 289 us
  waiting for transfers between devices  140 us (48%)
  blocking collectives  44.2 us (15%)
  starting transfers between devices  42.1 us (14%)
  local copies, waits for them, and re-layouts  18.3 us (6%)
  matrix products  16.6 us (6%)
  between operations  15.5 us (5%)
  other arithmetic  12.6 us (4%)
    all_to_all x1, waiting for transfers between devices, per_device(): lax.all_to_all(outgoing, 'expert', split_axis=0, concat_axis=0, tiled=True)  45 us
    all_to_all x1, blocking collectives, pair_collect(): lax.all_to_all(copies, axis, 0, 0, tiled=True, axis_index_groups=core_gro...  44.2 us
    all_gather x2, waiting for transfers between devices, pair_gather(): lax.all_gather(array, axis, axis=0, axis_index_groups=core_groups(axis))  36.3 us
    all_to_all x1, waiting for transfers between devices, per_device(): lax.all_to_all(result, 'expert', split_axis=0, concat_axis=0, tiled=True)  31.9 us
    ppermute x3, starting transfers between devices, with_sibling(): lax.ppermute(blocks, axis, [(i, i ^ 1) for i in range(lax.axis_size(axis))])  15.5 us
    all_to_all x1, starting transfers between devices, per_device(): lax.all_to_all(outgoing, 'expert', split_axis=0, concat_axis=0, tiled=True)  9.27 us
    all_to_all x1, waiting for transfers between devices, per_device(): lax.all_to_all(proj_cols, 'dp', split_axis=0, concat_axis=1, tiled=True)  8.85 us
    all_gather x1, waiting for transfers between devices, turned_gather(): out = lax.all_gather(both, axis, axis=0, tiled=True)  8.58 us
  transfers between devices with their start and end apart: 11, of which 8 were waited for; matrix products, arithmetic and copies ran while one was open for 13% of the time, Pallas kernels for 0%

profile of v13, /device:TPU:1, one launch (start us, length us, event | category | flops | bytes accessed | tf_op | source)
XLA Modules:
  0.0 289.3 jit_solution(8988511042357055212)
XLA Ops:
  7.7 1.8 pad_maximum_fusion.3
  9.7 44.2 %all_to_all.33 = bf16[8,32,2048]{2,1,0:T(8,128)(2,1)S(1)} all-to-all(bf16[8,32,2048]{2,1,0:T(8,128)(2,1)S(1)} %broadcast_in_dim.26), channel_id=1, replica_groups={{0,64,128,192,256,320,384,448},{32,96,160,224,288,352,416,480},{1,65,12..., dimensions={0} | all-to-all | bytes 2097152 | tf_op jit(solution)/shard_map/all_to_all | solution.py:28
  54.0 5.5 %collective-permute-start = (bf16[8,32,2048]{2,1,0:T(8,128)(2,1)S(1)}, bf16[8,32,2048]{2,1,0:T(8,128)(2,1)S(1)}, u32[]{:S(2)}, u32[]{:S(2)}) collective-permute-start(bf16[8,32,2048]{2,1,0:T(8,128)(2,1)S(1)} %all_to_all.33), channel_id=1, source_target_pairs={{0,32},{32,0},{64,96},{96,64},{128,160},{160,128},{192,224},{224,1... | collective-permute-start | bytes 3145736 | tf_op jit(solution)/shard_map/ppermute | solution.py:15
  59.5 2.3 collective-permute-done
  63.0 1.4 convolution_convert_fusion.1
  64.4 1.2 slice.41
  66.3 3.7 %all-to-all-start.1 = ((bf16[16,32,128]{2,1,0:T(8,128)(2,1)}), bf16[16,32,128]{2,1,0:T(8,128)(2,1)S(1)}, u32[]{:S(2)}, u32[]{:S(2)}) async-start(bf16[16,32,128]{2,1,0:T(8,128)(2,1)} %bitcast.4), calls=%async_computation.1 | async-start | bytes 262144 | tf_op jit(solution)/shard_map/all_to_all | solution.py:91
  71.8 8.8 %all-to-all-done.1 = bf16[16,32,128]{2,1,0:T(8,128)(2,1)S(1)} async-done(((bf16[16,32,128]{2,1,0:T(8,128)(2,1)}), bf16[16,32,128]{2,1,0:T(8,128)(2,1)S(1)}, u32[]{:S(2)}, u32[]{:S(2)}) %all-to-all-start.1) | async-done | bytes 131104 | tf_op jit(solution)/shard_map/all_to_all | solution.py:91
  81.5 1.6 reshape.120
  84.9 8.6 %all-gather.6.cloned.1.call-done = bf16[2048,2112]{1,0:T(8,128)(2,1)} async-done(((bf16[128,2112]{1,0:T(8,128)(2,1)}), bf16[2048,2112]{1,0:T(8,128)(2,1)}) %all-gather.6.cloned.1.call-update) | async-done | bytes 8650768 | tf_op jit(solution)/shard_map/all_gather | solution.py:53
  96.1 36.2 %all-gather.8.cloned.1.call-done = bf16[256,2048]{1,0:T(8,128)(2,1)} async-done(((bf16[32,2048]{1,0:T(8,128)(2,1)}), bf16[256,2048]{1,0:T(8,128)(2,1)}) %all-gather.8.cloned.1.call-update) | async-done | bytes 1048592 | tf_op jit(solution)/shard_map/all_gather | solution.py:22
  132.3 7.1 %collective-permute-start.1 = (bf16[8,32,2048]{2,1,0:T(8,128)(2,1)}, bf16[8,32,2048]{2,1,0:T(8,128)(2,1)}, u32[]{:S(2)}, u32[]{:S(2)}) collective-permute-start(bf16[8,32,2048]{2,1,0:T(8,128)(2,1)} %bitcast.96), channel_id=1, source_target_pairs={{0,32},{32,0},{64,96},{96,64},{128,160},{160,128},{192,224},{224,1... | collective-permute-start | bytes 3145736 | tf_op jit(solution)/shard_map/ppermute | solution.py:15
  139.5 9.3 %all-to-all-start.2 = ((bf16[32,12,2048]{2,1,0:T(8,128)(2,1)}), bf16[32,12,2048]{2,1,0:T(8,128)(2,1)S(1)}, u32[]{:S(2)}, u32[]{:S(2)}) async-start(bf16[32,12,2048]{2,1,0:T(8,128)(2,1)} %reshape.120), calls=%async_computation.2 | async-start | bytes 4194304 | tf_op jit(solution)/shard_map/all_to_all | solution.py:114
  148.8 1.7 pad_maximum_fusion.2
  152.9 45.0 %all-to-all-done.2 = bf16[32,12,2048]{2,1,0:T(8,128)(2,1)S(1)} async-done(((bf16[32,12,2048]{2,1,0:T(8,128)(2,1)}), bf16[32,12,2048]{2,1,0:T(8,128)(2,1)S(1)}, u32[]{:S(2)}, u32[]{:S(2)}) %all-to-all-start.2) | async-done | bytes 1572896 | tf_op jit(solution)/shard_map/all_to_all | solution.py:114
  197.9 1.3 reshape.121
  199.3 5.7 %fusion = f32[384,1408]{1,0:T(8,128)S(1)} fusion(bf16[384,2048]{1,0:T(8,128)(2,1)} %reshape.121, bf16[2048,2112]{1,0:T(8,128)(2,1)} %all-gather.6.cloned.1.call-done), kind=kOutput, calls=%fused_computation | convolution fusion | flops 2214592512 | bytes 9502720 | tf_op jit(solution)/shard_map/dot_general | solution.py:117
  205.0 3.3 %fusion.3 = bf16[384,2048]{1,0:T(8,128)(2,1)S(1)} fusion(bf16[2048,2112]{1,0:T(8,128)(2,1)} %all-gather.6.cloned.1.call-done, f32[384,1408]{1,0:T(8,128)S(1)} %fusion), kind=kOutput, calls=%fused_computation.8 | convolution fusion | flops 1109704704 | bytes 7077888 | tf_op jit(solution)/shard_map/dot_general | solution.py:119
  208.4 1.5 reshape.124
  209.9 7.6 %all-to-all-start.3 = ((bf16[32,12,2048]{2,1,0:T(8,128)(2,1)}), bf16[32,12,2048]{2,1,0:T(8,128)(2,1)S(1)}, u32[]{:S(2)}, u32[]{:S(2)}) async-start(bf16[32,12,2048]{2,1,0:T(8,128)(2,1)} %reshape.124), calls=%async_computation.3 | async-start | bytes 4194304 | tf_op jit(solution)/shard_map/all_to_all | solution.py:121
  217.6 2.6 copy.65
  220.2 2.8 collective-permute-start.2
  223.0 1.2 fusion.18
  224.4 2.0 copy.59
  226.8 1.6 pad_maximum_fusion
  230.5 1.9 collective-permute-start.3
  232.5 1.2 collective-permute-done.3
  234.4 31.9 %all-to-all-done.3 = bf16[32,12,2048]{2,1,0:T(8,128)(2,1)S(1)} async-done(((bf16[32,12,2048]{2,1,0:T(8,128)(2,1)}), bf16[32,12,2048]{2,1,0:T(8,128)(2,1)S(1)}, u32[]{:S(2)}, u32[]{:S(2)}) %all-to-all-start.3) | async-done | bytes 1572896 | tf_op jit(solution)/shard_map/all_to_all | solution.py:121
  266.3 4.0 %all-to-all-start.4 = ((bf16[8,32,2,128]{3,1,2,0:T(8,128)(2,1)}), bf16[8,32,2,128]{3,1,2,0:T(8,128)(2,1)}, u32[]{:S(2)}, u32[]{:S(2)}) async-start(bf16[8,32,2,128]{3,1,2,0:T(8,128)(2,1)} %copy.52), calls=%async_computation.4 | async-start | bytes 262144 | tf_op jit(solution)/shard_map/all_to_all | solution.py:147
  271.0 1.3 reshape.125
  272.4 5.9 %all-to-all-done.4 = bf16[8,32,2,128]{3,1,2,0:T(8,128)(2,1)} async-done(((bf16[8,32,2,128]{3,1,2,0:T(8,128)(2,1)}), bf16[8,32,2,128]{3,1,2,0:T(8,128)(2,1)}, u32[]{:S(2)}, u32[]{:S(2)}) %all-to-all-start.4) | async-done | bytes 131104 | tf_op jit(solution)/shard_map/all_to_all | solution.py:147
  279.7 2.4 multiply_reduce_fusion
  (75 shorter events, 16.8 us)
Async XLA Ops:
  6.5 144.6 %copy-start = (bf16[2048,2,176]{0,2,1:T(8,128)(2,1)S(1)}, bf16[2048,2,176]{0,2,1:T(8,128)(2,1)}, u32[]{:S(2)}) copy-start(bf16[2048,2,176]{0,2,1:T(8,128)(2,1)} %param.21) | copy-start | bytes 4325380
  6.5 3.1 %copy-start.4 = (bf16[32,2048]{1,0:T(8,128)(2,1)S(1)}, bf16[32,2048]{1,0:T(8,128)(2,1)}, u32[]{:S(2)}) copy-start(bf16[32,2048]{1,0:T(8,128)(2,1)} %param.13) | copy-start | bytes 393220
  6.5 86.9 %all-gather.6.cloned.1.call-start = ((), (), s32[]{:S(2)}) async-start(), calls=%async_computation.5 | async-start | bytes 9469952 | tf_op jit(solution)/shard_map/all_gather | solution.py:53
  54.0 7.8 %collective-permute-start = (bf16[8,32,2048]{2,1,0:T(8,128)(2,1)S(1)}, bf16[8,32,2048]{2,1,0:T(8,128)(2,1)S(1)}, u32[]{:S(2)}, u32[]{:S(2)}) collective-permute-start(bf16[8,32,2048]{2,1,0:T(8,128)(2,1)S(1)} %all_to_all.33), channel_id=1, source_target_pairs={{0,32},{32,0},{64,96},{96,64},{128,160},{160,128},{192,224},{224,1... | collective-permute-start | bytes 3145736 | tf_op jit(solution)/shard_map/ppermute | solution.py:15
  62.0 1.0 copy-start.3
  62.6 7.4 %copy-start.8 = (s32[32,6]{0,1:T(8,128)S(1)}, s32[32,6]{0,1:T(8,128)}, u32[]{:S(2)}) copy-start(s32[32,6]{0,1:T(8,128)} %param.17) | copy-start | bytes 2308
  62.6 7.4 %copy-start.10 = (s32[32]{0:T(128)S(1)}, s32[32]{0:T(128)}, u32[]{:S(2)}) copy-start(s32[32]{0:T(128)} %param.18) | copy-start | bytes 388
  62.6 18.0 %copy-start.5 = (bf16[32,2048]{1,0:T(8,128)(2,1)S(1)}, bf16[32,2048]{1,0:T(8,128)(2,1)}, u32[]{:S(2)}) copy-start(bf16[32,2048]{1,0:T(8,128)(2,1)} %param.12) | copy-start | bytes 393220
  62.6 18.2 %copy-start.6 = (f32[2048]{0:T(1024)S(1)}, f32[2048]{0:T(1024)}, u32[]{:S(2)}) copy-start(f32[2048]{0:T(1024)} %param.15) | copy-start | bytes 24580
  66.3 14.4 %all-to-all-start.1 = ((bf16[16,32,128]{2,1,0:T(8,128)(2,1)}), bf16[16,32,128]{2,1,0:T(8,128)(2,1)S(1)}, u32[]{:S(2)}, u32[]{:S(2)}) async-start(bf16[16,32,128]{2,1,0:T(8,128)(2,1)} %bitcast.4), calls=%async_computation.1 | async-start | bytes 262144 | tf_op jit(solution)/shard_map/all_to_all | solution.py:91
  69.9 62.4 %all-gather.8.cloned.1.call-start = ((), (), s32[]{:S(2)}) async-start(), calls=%async_computation.6 | async-start | bytes 1179648 | tf_op jit(solution)/shard_map/all_gather | solution.py:22
  80.8 14.5 %copy-start.1 = (bf16[32,2048]{1,0:T(8,128)(2,1)}, bf16[32,2048]{1,0:T(8,128)(2,1)S(1)}, u32[]{:S(2)}) copy-start(bf16[32,2048]{1,0:T(8,128)(2,1)S(1)} %get-tuple-element.6) | copy-start | bytes 393220
  80.8 14.5 %copy-start.9 = (f32[32]{0:T(128)}, f32[32]{0:T(128)S(1)}, u32[]{:S(2)}) copy-start(f32[32]{0:T(128)S(1)} %add_rsqrt_fusion.1) | copy-start | bytes 388
  132.3 16.5 %collective-permute-start.1 = (bf16[8,32,2048]{2,1,0:T(8,128)(2,1)}, bf16[8,32,2048]{2,1,0:T(8,128)(2,1)}, u32[]{:S(2)}, u32[]{:S(2)}) collective-permute-start(bf16[8,32,2048]{2,1,0:T(8,128)(2,1)} %bitcast.96), channel_id=1, source_target_pairs={{0,32},{32,0},{64,96},{96,64},{128,160},{160,128},{192,224},{224,1... | collective-permute-start | bytes 3145736 | tf_op jit(solution)/shard_map/ppermute | solution.py:15
  139.5 58.4 %all-to-all-start.2 = ((bf16[32,12,2048]{2,1,0:T(8,128)(2,1)}), bf16[32,12,2048]{2,1,0:T(8,128)(2,1)S(1)}, u32[]{:S(2)}, u32[]{:S(2)}) async-start(bf16[32,12,2048]{2,1,0:T(8,128)(2,1)} %reshape.120), calls=%async_computation.2 | async-start | bytes 4194304 | tf_op jit(solution)/shard_map/all_to_all | solution.py:114
  148.8 68.8 %all-gather.10.cloned.1.call-start = ((), (), s32[]{:S(2)}) async-start(), calls=%async_computation.7 | async-start | bytes 1622016 | tf_op jit(solution)/shard_map/all_gather | solution.py:22
  209.9 56.4 %all-to-all-start.3 = ((bf16[32,12,2048]{2,1,0:T(8,128)(2,1)}), bf16[32,12,2048]{2,1,0:T(8,128)(2,1)S(1)}, u32[]{:S(2)}, u32[]{:S(2)}) async-start(bf16[32,12,2048]{2,1,0:T(8,128)(2,1)} %reshape.124), calls=%async_computation.3 | async-start | bytes 4194304 | tf_op jit(solution)/shard_map/all_to_all | solution.py:121
  220.2 6.6 %collective-permute-start.2 = (bf16[8,512,176]{1,2,0:T(8,128)(2,1)}, bf16[8,512,176]{1,2,0:T(8,128)(2,1)}, u32[]{:S(2)}, u32[]{:S(2)}) collective-permute-start(bf16[8,512,176]{1,2,0:T(8,128)(2,1)} %bitcast.86), channel_id=1, source_target_pairs={{0,32},{32,0},{64,96},{96,64},{128,160},{160,128},{192,224},{224,1... | collective-permute-start | bytes 4325384 | tf_op jit(solution)/shard_map/ppermute | solution.py:15
  228.4 1.1 copy-start.2
  230.5 3.1 %collective-permute-start.3 = (bf16[8,32,128]{2,1,0:T(8,128)(2,1)S(1)}, bf16[8,32,128]{2,1,0:T(8,128)(2,1)S(1)}, u32[]{:S(2)}, u32[]{:S(2)}) collective-permute-start(bf16[8,32,128]{2,1,0:T(8,128)(2,1)S(1)} %get-tuple-element.8), channel_id=1, source_target_pairs={{0,32},{32,0},{64,96},{96,64},{128,160},{160,128},{192,224},{224,1... | collective-permute-start | bytes 196616 | tf_op jit(solution)/shard_map/ppermute | solution.py:143
  266.3 12.0 %all-to-all-start.4 = ((bf16[8,32,2,128]{3,1,2,0:T(8,128)(2,1)}), bf16[8,32,2,128]{3,1,2,0:T(8,128)(2,1)}, u32[]{:S(2)}, u32[]{:S(2)}) async-start(bf16[8,32,2,128]{3,1,2,0:T(8,128)(2,1)} %copy.52), calls=%async_computation.4 | async-start | bytes 262144 | tf_op jit(solution)/shard_map/all_to_all | solution.py:147
  272.4 9.7 %copy-start.7 = (f32[2048]{0:T(1024)S(1)}, f32[2048]{0:T(1024)}, u32[]{:S(2)}) copy-start(f32[2048]{0:T(1024)} %param.23) | copy-start | bytes 24580
Sparse Core Ops, SparseCore 0:
  9.7 83.6 all-gather.5
  96.2 36.0 all-gather.7
  153.0 37.2 all-gather.9
